TPU v7x, 32 devices: a whole 2x2x4 slice. The times are simulated.
32 devices in a mesh: dp: 8 (over z, x), expert: 4 (over y, core).
Axes of the slice: x: 2, y: 2, z: 4, core: 2. Of those that a mesh axis runs over, the one named last changes fastest.
Arguments:
- hidden: bfloat16 [2048, 2304], P(('dp', 'expert')), may hold values from -6 to 6
- tree_qkv: bfloat16 [2048, 6912], P(('dp', 'expert')), may hold values from -7 to 7
- prompt_kv: bfloat16 [8, 512, 4608], P('dp', 'expert'), may hold values from -6 to 6
- prompt_len: int32 [8], P('dp'), may hold values from 128 to 512, as said below
- private_kv: bfloat16 [32, 512, 4608], P(('dp', 'expert')), may hold values from -6 to 6
- priv_len: int32 [32], P(('dp', 'expert')), may hold values from 1 to 512, as said below
- parents: int32 [32, 64], P(('dp', 'expert')), may hold values from -1 to 62, as said below
- leaf: int32 [32], P(('dp', 'expert')), may hold values from 0 to 63
- w_out: bfloat16 [2304, 2304], replicated, may hold values from -3 to 3
- norm_gain: float32 [2304], replicated, may hold values from 0.1 to 1.9
- w_router: bfloat16 [2304, 4], replicated, as said below
- routes: int32 [2048, 2], P(('dp', 'expert')), may hold values from 0 to 3, all different within a row; in each aligned block of 64 rows (0 to 63, 64 to 127, ...) at most 48 rows name the same one
- w_gate_up: bfloat16 [4, 2, 2304, 5760], P('expert', None, None, 'dp'), may hold values from -0.125 to 0.125
- w_down: bfloat16 [4, 5760, 2304], P('expert', 'dp'), may hold values from -0.15625 to 0.15625
Outputs:
- layer_out: bfloat16 [2048, 2304], P(('dp', 'expert'))
- accepted_kv: bfloat16 [32, 64, 4608], P(('dp', 'expert'))
Inputs may be any that keep to these rules, and one draw needn't show every extreme that they name: `routes`: the rows of one device (aligned blocks of 64 rows) name each expert at most 48 times; the two experts of a row differ. `prompt_len`: some group's length is exactly 512. `priv_len`: some request's length is exactly 512. parents[r, 0] = -1; for t >= 1, max(0, t - 8) <= parents[r, t] <= t - 1. `w_router`: entries lie within 3 / sqrt(27648) of zero.
All inputs are finite; a program needn't handle non-finite values.
Results may differ from a plain program's by a relative error of at most 0.014.
Values may be sent and summed in bfloat16 or wider, within the bound.
No kernel may reach another device: no remote copies, remote signals or barrier semaphores. Data moves between devices by JAX's collectives and lax.ppermute only.
A program may use at most 128 MiB of HBM per device.

v0:
```python
import functools
import math

import jax
import jax.numpy as jnp
from jax import lax
from jax.experimental import pallas as pl
from jax.sharding import PartitionSpec as P

H = 36
HD = 64
TREE = 64
REQ_DEV = 1


NEG = -1e30
EPS = 1e-05
HIGH = lax.Precision.HIGHEST


def closure(parents):
    count = parents.shape[-1]
    columns = jnp.arange(count, dtype=jnp.int32)
    reached = (parents[:, :, None] == columns[None, None, :]).astype(jnp.float32) + jnp.eye(
        count, dtype=jnp.float32
    )[None]
    for sweeps in range((count - 1).bit_length()):
        reached = jnp.minimum(jnp.einsum("rij,rjk->rik", reached, reached, precision=HIGH), 1.0)
    return reached


def compact(reach_one, leaf_one, kv_one):
    count = reach_one.shape[0]
    marked = jnp.sum(
        jnp.where(jnp.arange(count, dtype=jnp.int32)[:, None] == leaf_one, reach_one, 0.0), axis=0
    )
    earlier = (
        jnp.arange(count, dtype=jnp.int32)[None, :] < jnp.arange(count, dtype=jnp.int32)[:, None]
    ).astype(jnp.float32)
    ordinal = jnp.dot(earlier, marked, precision=HIGH)
    slot_ids = jnp.arange(count, dtype=jnp.int32).astype(jnp.float32)
    chosen = jnp.where(slot_ids[:, None] == ordinal[None, :], marked[None, :], 0.0)
    return jnp.dot(chosen.astype(jnp.bfloat16), kv_one, preferred_element_type=jnp.float32).astype(
        jnp.bfloat16
    )


def partial_attention(query_matrix_rows, cache_rows, allowed):
    features = cache_rows.shape[1] // 2
    slots = cache_rows.shape[0]
    key_matrix_rows = cache_rows[:, :features].reshape(slots, H, HD)
    value_matrix_rows = cache_rows[:, features:].reshape(slots, H, HD)
    attention_score_scale = 1.0 / math.sqrt(HD)
    attention_scores = (
        jnp.einsum(
            "was,zas->waz", query_matrix_rows, key_matrix_rows, preferred_element_type=jnp.float32
        )
        * attention_score_scale
    )
    widened = allowed[:, None, :]
    attention_scores = jnp.where(widened, attention_scores, NEG)
    maxima = jnp.max(attention_scores, axis=-1)
    attention_weights = jnp.where(widened, jnp.exp(attention_scores - maxima[..., None]), 0.0)
    totals = jnp.sum(attention_weights, axis=-1)
    weighted_sum = jnp.einsum(
        "ubj,jbx->ubx",
        attention_weights.astype(jnp.bfloat16),
        value_matrix_rows,
        preferred_element_type=jnp.float32,
    )
    return (maxima, totals, weighted_sum)


def join_parts(first_part, second_part):
    highest = jnp.maximum(first_part[0], second_part[0])
    scale_first = jnp.exp(first_part[0] - highest)
    scale_second = jnp.exp(second_part[0] - highest)
    totals = first_part[1] * scale_first + second_part[1] * scale_second
    weighted_sum = first_part[2] * scale_first[..., None] + second_part[2] * scale_second[..., None]
    return (highest, totals, weighted_sum)


def as_rows(part_state, row_count):
    return (
        part_state[0].reshape(row_count, H),
        part_state[1].reshape(row_count, H),
        part_state[2].reshape(row_count, H, HD),
    )


def attend_kernel(*refs, count, scale):
    q_ref = refs[0]
    sources = refs[1:1 + 3 * count]
    acc_ref, top_ref, total_ref = refs[1 + 3 * count:]
    width = q_ref.shape[1] // 2
    for head in range(2):
        cols = slice(head * width, (head + 1) * width)
        query = q_ref[:, cols]
        scores = []
        for index in range(count):
            keys = sources[3 * index][:, cols]
            raw = lax.dot_general(
                query, keys, (((1,), (1,)), ((), ())), preferred_element_type=jnp.float32
            ) * scale
            scores.append(jnp.where(sources[3 * index + 2][...] > 0.5, raw, NEG))
        top = scores[0].max(axis=1, keepdims=True)
        for more in scores[1:]:
            top = jnp.maximum(top, more.max(axis=1, keepdims=True))
        total = jnp.zeros_like(top)
        acc = jnp.zeros((query.shape[0], width), jnp.float32)
        for index in range(count):
            weights = jnp.where(sources[3 * index + 2][...] > 0.5, jnp.exp(scores[index] - top), 0.0)
            total = total + weights.sum(axis=1, keepdims=True)
            acc = acc + jnp.dot(
                weights.astype(jnp.bfloat16),
                sources[3 * index + 1][:, cols],
                preferred_element_type=jnp.float32,
            )
        acc_ref[:, cols] = acc
        top_ref[:, cols] = jnp.broadcast_to(top, acc.shape)
        total_ref[:, cols] = jnp.broadcast_to(total, acc.shape)


def attend(query_rows, sources):
    rows, features = query_rows.shape
    pairs = features // (2 * HD)
    block = 2 * HD
    operands = [query_rows]
    specs = [pl.BlockSpec((rows, block), lambda h: (0, h))]
    for table, key_offset, value_offset, allowed in sources:
        slots = table.shape[0]
        operands += [table, table, allowed.astype(jnp.float32)]
        specs += [
            pl.BlockSpec((slots, block), lambda h, o=key_offset: (0, o + h)),
            pl.BlockSpec((slots, block), lambda h, o=value_offset: (0, o + h)),
            pl.BlockSpec((rows, slots), lambda h: (0, 0)),
        ]
    shape = jax.ShapeDtypeStruct((rows, features), jnp.float32)
    out_spec = pl.BlockSpec((rows, block), lambda h: (0, h))
    return pl.pallas_call(
        functools.partial(attend_kernel, count=len(sources), scale=1.0 / math.sqrt(HD)),
        grid=(pairs,),
        in_specs=specs,
        out_specs=(out_spec, out_spec, out_spec),
        out_shape=(shape, shape, shape),
    )(*operands)


def dp_ring(mesh):
    count = mesh.shape["dp"]
    try:
        axis = list(mesh.axis_names).index("dp")
        places = [tuple(mesh.devices.take(i, axis=axis).reshape(-1)[0].coords) for i in range(count)]
        varying = [a for a in range(len(places[0])) if len({c[a] for c in places}) > 1]
        changes = {a: sum(places[i][a] != places[i + 1][a] for i in range(count - 1)) for a in varying}
        slow, fast = sorted(varying, key=lambda a: changes[a])
        rows = sorted({c[slow] for c in places})
        cols = sorted({c[fast] for c in places})
        where = {(c[slow], c[fast]): i for i, c in enumerate(places)}
        if len(varying) != 2 or len(rows) * len(cols) != count or len(rows) % 2 or len(cols) < 2:
            raise ValueError
        cycle = [where[(rows[0], cols[0])]]
        for r, row in enumerate(rows):
            ordered = cols[1:] if r % 2 == 0 else cols[1:][::-1]
            cycle += [where[(row, col)] for col in ordered]
        cycle += [where[(row, cols[0])] for row in rows[1:][::-1]]
        if sorted(cycle) != list(range(count)):
            raise ValueError
        return cycle
    except Exception:
        return list(range(count))


def ring_gather(piece, ring, step):
    count = len(ring)
    pairs = [(ring[p], ring[(p + step) % count]) for p in range(count)]
    arrived = [piece]
    for unused in range(count - 1):
        piece = lax.ppermute(piece, "dp", pairs)
        arrived.append(piece)
    return arrived


def ring_reduce(blocks, ring, step):
    count = len(ring)
    pairs = [(ring[p], ring[(p + step) % count]) for p in range(count)]
    moving = blocks[1]
    for index in range(2, count):
        received = lax.ppermute(moving, "dp", pairs).astype(jnp.float32)
        moving = (received + blocks[index].astype(jnp.float32)).astype(jnp.bfloat16)
    received = lax.ppermute(moving, "dp", pairs).astype(jnp.float32)
    return received + blocks[0].astype(jnp.float32)


def local(
    ring,
    hidden,
    tree_qkv,
    prompt_kv,
    prompt_len,
    private_kv,
    priv_len,
    parents,
    leaf,
    w_out,
    norm_gain,
    w_router,
    routes,
    w_gate_up,
    w_down,
):
    row_count = hidden.shape[0]
    features = hidden.shape[1]
    new_kv = tree_qkv[:, features:]
    reached = closure(parents)
    grouped_kv = new_kv.reshape(REQ_DEV, TREE, 2 * features)
    blocks = features // (2 * HD)
    private_slots = jnp.arange(private_kv.shape[1], dtype=jnp.int32)
    private_ok = jnp.broadcast_to(private_slots[None, :] < priv_len[0], (row_count, private_kv.shape[1]))
    local_acc, local_top, local_total = attend(
        tree_qkv[:, :features],
        [
            (private_kv[0], 0, blocks, private_ok),
            (tree_qkv, blocks, 2 * blocks, reached[0] > 0.5),
        ],
    )
    shard_rows = lax.all_gather(prompt_kv, "expert", axis=1, tiled=True)
    piece_len = shard_rows.shape[1]
    places = jnp.arange(piece_len, dtype=jnp.int32)
    prompt_ok = jnp.broadcast_to((places < prompt_len[0])[None, :], (row_count, piece_len))
    prompt_acc, prompt_top, prompt_total = attend(
        tree_qkv[:, :features], [(shard_rows[0], 0, blocks, prompt_ok)]
    )
    highest = jnp.maximum(local_top, prompt_top)
    scale_local = jnp.exp(local_top - highest)
    scale_prompt = jnp.exp(prompt_top - highest)
    totals = local_total * scale_local + prompt_total * scale_prompt
    weighted = local_acc * scale_local + prompt_acc * scale_prompt
    context = (weighted / totals).astype(jnp.bfloat16)
    attended = jnp.dot(context, w_out, preferred_element_type=jnp.float32)
    middle = (hidden.astype(jnp.float32) + attended).astype(jnp.bfloat16)
    middle32 = middle.astype(jnp.float32)
    normed = (
        middle32 * lax.rsqrt(jnp.mean(middle32 * middle32, axis=1, keepdims=True) + EPS) * norm_gain
    ).astype(jnp.bfloat16)
    logits = jnp.dot(normed, w_router, preferred_element_type=jnp.float32)
    experts = w_router.shape[1]
    choose = routes[:, :, None] == jnp.arange(experts, dtype=jnp.int32)[None, None, :]
    picked = jnp.sum(jnp.where(choose, logits[:, None, :], 0.0), axis=2)
    gate_first = jax.nn.sigmoid(picked[:, 0] - picked[:, 1])
    gate_second = jax.nn.sigmoid(picked[:, 1] - picked[:, 0])
    capacity = 3 * row_count // experts
    onehot = choose.reshape(2 * row_count, experts).astype(jnp.float32)
    assign_ids = jnp.arange(2 * row_count, dtype=jnp.int32)
    earlier = (assign_ids[None, :] < assign_ids[:, None]).astype(jnp.float32)
    before = jnp.dot(earlier, onehot, precision=HIGH)
    slot_rank = jnp.sum(before * onehot, axis=1).astype(jnp.int32)
    target = routes.reshape(2 * row_count) * capacity + slot_rank
    select = (jnp.arange(experts * capacity, dtype=jnp.int32)[:, None] == target[None, :]).astype(
        jnp.bfloat16
    )
    doubled = jnp.repeat(normed, 2, axis=0)
    outgoing = (
        jnp.dot(select, doubled, preferred_element_type=jnp.float32)
        .astype(jnp.bfloat16)
        .reshape(experts, capacity, features)
    )
    gate_cols = w_gate_up[0, 0]
    up_cols = w_gate_up[0, 1]
    down_rows = w_down[0]
    arrived = lax.all_to_all(outgoing, "expert", split_axis=0, concat_axis=0, tiled=True)
    arrived = arrived.reshape(experts * capacity, features)
    half = experts * capacity // 2
    forward = ring_gather(arrived[:half], ring, 1)
    backward = ring_gather(arrived[half:], ring, -1)
    forward_out = []
    backward_out = []
    for index in range(len(ring)):
        pooled = jnp.concatenate([forward[index], backward[index]], axis=0)
        gate_act = jnp.dot(pooled, gate_cols, preferred_element_type=jnp.float32)
        upper = jnp.dot(pooled, up_cols, preferred_element_type=jnp.float32)
        hidden_units = (jax.nn.silu(gate_act) * upper).astype(jnp.bfloat16)
        partial = jnp.dot(hidden_units, down_rows, preferred_element_type=jnp.float32).astype(jnp.bfloat16)
        forward_out.append(partial[:half])
        backward_out.append(partial[half:])
    summed_rows = jnp.concatenate(
        [ring_reduce(forward_out, ring, 1), ring_reduce(backward_out, ring, -1)], axis=0
    )
    returned = lax.all_to_all(
        summed_rows.reshape(experts, capacity, features).astype(jnp.bfloat16),
        "expert",
        split_axis=0,
        concat_axis=0,
        tiled=True,
    ).astype(jnp.float32)
    flat_back = returned.reshape(experts * capacity, features)
    fetched = jnp.take(flat_back, target, axis=0).reshape(row_count, 2, features)
    layer_out = (
        middle32 + gate_first[:, None] * fetched[:, 0] + gate_second[:, None] * fetched[:, 1]
    ).astype(jnp.bfloat16)
    accepted_kv = jax.vmap(compact)(reached, leaf, grouped_kv)
    return (layer_out, accepted_kv)


def solution(mesh):
    placed = (
        P(("dp", "expert"), None),
        P(("dp", "expert"), None),
        P("dp", "expert", None),
        P("dp"),
        P(("dp", "expert"), None, None),
        P(("dp", "expert")),
        P(("dp", "expert"), None),
        P(("dp", "expert")),
        P(),
        P(),
        P(),
        P(("dp", "expert"), None),
        P("expert", None, None, "dp"),
        P("expert", "dp", None),
    )
    ring = dp_ring(mesh)
    return jax.shard_map(
        functools.partial(local, ring),
        mesh=mesh,
        in_specs=placed,
        out_specs=(P(("dp", "expert"), None), P(("dp", "expert"), None, None)),
        check_vma=False,
    )
```

profile of v0, /device:TPU:0, one launch (start us, length us, event | category | flops | bytes accessed | tf_op | source)
XLA Modules:
  0.0 304.4 jit_solution(13105342184615041351)
XLA Ops:
  7.9 1.9 slice.87.refs_0_
  17.2 18.7 %shard_map.152 = (f32[64,2304]{1,0:T(8,128)}, f32[64,2304]{1,0:T(8,128)}, f32[64,2304]{1,0:T(8,128)}) custom-call(bf16[64,2304]{1,0:T(8,128)(2,1)} %slice.87.refs_0_, bf16[512,4608]{1,0:T(8,128)(2,1)} %bitcast.165, bf16[512,4608]{1,0:T(8,128)(2,1)} %bitcast.166, f32[64,512]{1,0:T(8,128)} %broadcast_in_dim.42.refs_3_, bf16[64,6912]{1,0:T(8,128)(2,1)} %refs_5_.1, ...), custom_call_target="tpu_custom_call" | custom-call | tf_op jit(solution)/shard_map/pallas_call | solution.py:140
  36.0 13.8 %all-gather.2.cloned.1.call-done = bf16[1,512,4608]{2,1,0:T(8,128)(2,1)} async-done(((bf16[1,128,4608]{2,1,0:T(8,128)(2,1)}), bf16[1,512,4608]{2,1,0:T(8,128)(2,1)}) %all-gather.2.cloned.1.call-update) | async-done | bytes 4718608 | tf_op jit(solution)/shard_map/all_gather | solution.py:227
  50.4 17.4 %shard_map.153 = (f32[64,2304]{1,0:T(8,128)}, f32[64,2304]{1,0:T(8,128)}, f32[64,2304]{1,0:T(8,128)}) custom-call(bf16[64,2304]{1,0:T(8,128)(2,1)} %slice.87.refs_0_, bf16[512,4608]{1,0:T(8,128)(2,1)} %bitcast.167, bf16[512,4608]{1,0:T(8,128)(2,1)} %bitcast.168, f32[64,512]{1,0:T(8,128)} %broadcast_in_dim.47.refs_3_), custom_call_target="tpu_custom_call" | custom-call | tf_op jit(solution)/shard_map/pallas_call | solution.py:140
  67.8 7.3 %multiply_reduce_fusion = (f32[64]{0:T(128)S(1)}, f32[64,2304]{1,0:T(8,128)S(1)}) fusion(bf16[2304,2304]{1,0:T(8,128)(2,1)} %param.22, f32[64,2304]{1,0:T(8,128)} %get-tuple-element.13, f32[64,2304]{1,0:T(8,128)} %get-tuple-element.12, f32[64,2304]{1,0:T(8,128)} %get-tuple-element.11, f32[64,2304]{1,0:T(8,128)} %get-tuple-element.10, ...), kind=kOutput, calls=%fused_computation.109 | convolution fusion | flops 681983936 | bytes 15040768 | tf_op jit(solution)/shard_map/dot_general | solution.py:240
  76.8 1.1 broadcast_in_dim.51
  77.9 2.7 reshape.316
  80.6 2.4 convolution_convert_fusion.1
  83.0 4.2 %all-to-all-start = ((bf16[4,48,2304]{2,1,0:T(8,128)(2,1)}), bf16[4,48,2304]{2,1,0:T(8,128)(2,1)}, u32[]{:S(2)}, u32[]{:S(2)}) async-start(bf16[4,48,2304]{2,1,0:T(8,128)(2,1)} %bitcast.170), calls=%async_computation | async-start | bytes 1769472 | tf_op jit(solution)/shard_map/all_to_all | solution.py:271
  87.5 12.5 %all-to-all-done = bf16[4,48,2304]{2,1,0:T(8,128)(2,1)} async-done(((bf16[4,48,2304]{2,1,0:T(8,128)(2,1)}), bf16[4,48,2304]{2,1,0:T(8,128)(2,1)}, u32[]{:S(2)}, u32[]{:S(2)}) %all-to-all-start) | async-done | bytes 884768 | tf_op jit(solution)/shard_map/all_to_all | solution.py:271
  100.0 1.2 fusion.142
  101.2 1.5 collective-permute-start
  102.7 2.2 fusion
  105.5 3.9 %fusion.27 = f32[192,720]{1,0:T(8,128)} fusion(bf16[96,2304]{1,0:T(8,128)(2,1)S(1)} %bitcast.172, bf16[96,2304]{1,0:T(8,128)(2,1)S(1)} %bitcast.175, bf16[1,2,2304,720]{2,3,1,0:T(8,128)(2,1)} %param.26), kind=kOutput, calls=%fused_computation.39 | convolution fusion | flops 638779392 | bytes 4755456 | tf_op jit(solution)/shard_map/dot_general | solution.py:280
  109.5 3.4 %collective-permute-done = bf16[96,2304]{1,0:T(8,128)(2,1)S(1)} collective-permute-done((bf16[96,2304]{1,0:T(8,128)(2,1)S(1)}, bf16[96,2304]{1,0:T(8,128)(2,1)S(1)}, u32[]{:S(2)}, u32[]{:S(2)}) %collective-permute-start) | collective-permute-done | bytes 442400 | tf_op jit(solution)/shard_map/ppermute | solution.py:179
  112.9 3.4 %collective-permute-done.1 = bf16[96,2304]{1,0:T(8,128)(2,1)S(1)} collective-permute-done((bf16[96,2304]{1,0:T(8,128)(2,1)S(1)}, bf16[96,2304]{1,0:T(8,128)(2,1)S(1)}, u32[]{:S(2)}, u32[]{:S(2)}) %collective-permute-start.1) | collective-permute-done | bytes 442400 | tf_op jit(solution)/shard_map/ppermute | solution.py:179
  118.0 3.9 %fusion.41 = f32[192,720]{1,0:T(8,128)} fusion(bf16[192,2304]{1,0:T(8,128)(2,1)S(1)} %constant_dynamic-update-slice_fusion, bf16[1,2,2304,720]{2,3,1,0:T(8,128)(2,1)} %param.26), kind=kOutput, calls=%fused_computation.53 | convolution fusion | flops 637009920 | bytes 4755456 | tf_op jit(solution)/shard_map/dot_general | solution.py:280
  121.9 5.6 %convolution_convert_fusion.9 = bf16[192,2304]{1,0:T(8,128)(2,1)} fusion(bf16[1,720,2304]{2,1,0:T(8,128)(2,1)S(1)} %copy-done, f32[192,720]{1,0:T(8,128)} %fusion.41, bf16[192,2304]{1,0:T(8,128)(2,1)} %copy-done.13, bf16[1,2,2304,720]{2,3,1,0:T(8,128)(2,1)} %param.26), kind=kOutput, calls=%fused_computation.11 | convolution fusion | flops 1275291648 | bytes 8994816 | tf_op jit(solution)/shard_map/dot_general | solution.py:283
  127.5 1.5 collective-permute-start.3
  129.5 2.1 fusion.141
  131.6 1.5 collective-permute-start.2
  133.7 7.2 %collective-permute-done.3 = bf16[96,2304]{1,0:T(8,128)(2,1)} collective-permute-done((bf16[96,2304]{1,0:T(8,128)(2,1)}, bf16[96,2304]{1,0:T(8,128)(2,1)}, u32[]{:S(2)}, u32[]{:S(2)}) %collective-permute-start.3) | collective-permute-done | bytes 442400 | tf_op jit(solution)/shard_map/ppermute | solution.py:179
  144.3 3.9 %fusion.39 = f32[192,720]{1,0:T(8,128)} fusion(bf16[192,2304]{1,0:T(8,128)(2,1)S(1)} %constant_dynamic-update-slice_fusion.2, bf16[1,2,2304,720]{2,3,1,0:T(8,128)(2,1)} %param.26), kind=kOutput, calls=%fused_computation.51 | convolution fusion | flops 637009920 | bytes 4755456 | tf_op jit(solution)/shard_map/dot_general | solution.py:280
  148.2 1.5 collective-permute-start.6
  150.2 5.6 %convolution_convert_fusion.8 = bf16[192,2304]{1,0:T(8,128)(2,1)} fusion(bf16[1,720,2304]{2,1,0:T(8,128)(2,1)S(1)} %copy-done, f32[192,720]{1,0:T(8,128)} %fusion.39, bf16[192,2304]{1,0:T(8,128)(2,1)} %copy-done.8, bf16[1,2,2304,720]{2,3,1,0:T(8,128)(2,1)} %param.26), kind=kOutput, calls=%fused_computation.10 | convolution fusion | flops 1275291648 | bytes 8994816 | tf_op jit(solution)/shard_map/dot_general | solution.py:283
  155.8 2.5 add_convert_fusion.13
  158.4 1.5 collective-permute-start.5
  161.4 1.0 constant_dynamic-update-slice_fusion.4
  163.4 3.9 %fusion.37 = f32[192,720]{1,0:T(8,128)} fusion(bf16[192,2304]{1,0:T(8,128)(2,1)S(1)} %constant_dynamic-update-slice_fusion.4, bf16[1,2,2304,720]{2,3,1,0:T(8,128)(2,1)} %param.26), kind=kOutput, calls=%fused_computation.49 | convolution fusion | flops 637009920 | bytes 4755456 | tf_op jit(solution)/shard_map/dot_general | solution.py:280
  167.3 1.5 collective-permute-start.9
  169.3 5.6 %convolution_convert_fusion.7 = bf16[192,2304]{1,0:T(8,128)(2,1)} fusion(bf16[1,720,2304]{2,1,0:T(8,128)(2,1)S(1)} %copy-done, f32[192,720]{1,0:T(8,128)} %fusion.37, bf16[192,2304]{1,0:T(8,128)(2,1)} %copy-done.9, bf16[1,2,2304,720]{2,3,1,0:T(8,128)(2,1)} %param.26), kind=kOutput, calls=%fused_computation.9 | convolution fusion | flops 1275291648 | bytes 8994816 | tf_op jit(solution)/shard_map/dot_general | solution.py:283
  174.9 2.5 add_convert_fusion.12
  177.5 1.5 collective-permute-start.8
  183.3 3.9 %fusion.35 = f32[192,720]{1,0:T(8,128)} fusion(bf16[192,2304]{1,0:T(8,128)(2,1)S(1)} %constant_dynamic-update-slice_fusion.6, bf16[1,2,2304,720]{2,3,1,0:T(8,128)(2,1)} %param.26), kind=kOutput, calls=%fused_computation.47 | convolution fusion | flops 637009920 | bytes 4755456 | tf_op jit(solution)/shard_map/dot_general | solution.py:280
  187.2 1.5 collective-permute-start.12
  189.3 5.6 %convolution_convert_fusion.6 = bf16[192,2304]{1,0:T(8,128)(2,1)} fusion(bf16[1,720,2304]{2,1,0:T(8,128)(2,1)S(1)} %copy-done, f32[192,720]{1,0:T(8,128)} %fusion.35, bf16[192,2304]{1,0:T(8,128)(2,1)} %copy-done.10, bf16[1,2,2304,720]{2,3,1,0:T(8,128)(2,1)} %param.26), kind=kOutput, calls=%fused_computation.8 | convolution fusion | flops 1275291648 | bytes 8994816 | tf_op jit(solution)/shard_map/dot_general | solution.py:283
  194.9 2.5 add_convert_fusion.11
  197.4 1.5 collective-permute-start.11
  203.2 3.9 %fusion.33 = f32[192,720]{1,0:T(8,128)} fusion(bf16[192,2304]{1,0:T(8,128)(2,1)S(1)} %constant_dynamic-update-slice_fusion.8, bf16[1,2,2304,720]{2,3,1,0:T(8,128)(2,1)} %param.26), kind=kOutput, calls=%fused_computation.45 | convolution fusion | flops 637009920 | bytes 4755456 | tf_op jit(solution)/shard_map/dot_general | solution.py:280
  207.1 1.4 collective-permute-start.15
  209.2 5.6 %convolution_convert_fusion.5 = bf16[192,2304]{1,0:T(8,128)(2,1)} fusion(bf16[1,720,2304]{2,1,0:T(8,128)(2,1)S(1)} %copy-done, f32[192,720]{1,0:T(8,128)} %fusion.33, bf16[192,2304]{1,0:T(8,128)(2,1)} %copy-done.11, bf16[1,2,2304,720]{2,3,1,0:T(8,128)(2,1)} %param.26), kind=kOutput, calls=%fused_computation.7 | convolution fusion | flops 1275291648 | bytes 8994816 | tf_op jit(solution)/shard_map/dot_general | solution.py:283
  214.8 2.5 add_convert_fusion.10
  217.3 1.4 collective-permute-start.14
  219.3 1.2 collective-permute-done.15
  223.7 3.9 %fusion.31 = f32[192,720]{1,0:T(8,128)} fusion(bf16[192,2304]{1,0:T(8,128)(2,1)S(1)} %constant_dynamic-update-slice_fusion.10, bf16[1,2,2304,720]{2,3,1,0:T(8,128)(2,1)} %param.26), kind=kOutput, calls=%fused_computation.43 | convolution fusion | flops 637009920 | bytes 4755456 | tf_op jit(solution)/shard_map/dot_general | solution.py:280
  228.4 1.3 collective-permute-start.19
  229.7 5.6 %convolution_convert_fusion.4 = bf16[192,2304]{1,0:T(8,128)(2,1)} fusion(bf16[1,720,2304]{2,1,0:T(8,128)(2,1)S(1)} %copy-done, f32[192,720]{1,0:T(8,128)} %fusion.31, bf16[192,2304]{1,0:T(8,128)(2,1)} %copy-done.12, bf16[1,2,2304,720]{2,3,1,0:T(8,128)(2,1)} %param.26), kind=kOutput, calls=%fused_computation.6 | convolution fusion | flops 1275291648 | bytes 8994816 | tf_op jit(solution)/shard_map/dot_general | solution.py:283
  235.3 2.6 add_convert_fusion.9
  238.6 1.3 collective-permute-start.26
  243.3 3.9 %fusion.29 = f32[192,720]{1,0:T(8,128)} fusion(bf16[192,2304]{1,0:T(8,128)(2,1)S(1)} %constant_dynamic-update-slice_fusion.12, bf16[1,2,2304,720]{2,3,1,0:T(8,128)(2,1)} %param.26), kind=kOutput, calls=%fused_computation.41 | convolution fusion | flops 637009920 | bytes 4755456 | tf_op jit(solution)/shard_map/dot_general | solution.py:280
  247.2 5.6 %convolution_convert_fusion.3 = bf16[192,2304]{1,0:T(8,128)(2,1)} fusion(bf16[1,720,2304]{2,1,0:T(8,128)(2,1)S(1)} %copy-done, f32[192,720]{1,0:T(8,128)} %fusion.29, bf16[192,2304]{1,0:T(8,128)(2,1)} %copy-done.7, bf16[1,2,2304,720]{2,3,1,0:T(8,128)(2,1)} %param.26), kind=kOutput, calls=%fused_computation.5 | convolution fusion | flops 1275291648 | bytes 8994816 | tf_op jit(solution)/shard_map/dot_general | solution.py:283
  252.8 2.5 add_convert_fusion.8
  255.3 1.1 collective-permute-start.20
  257.3 5.6 %convolution_convert_fusion.2 = bf16[192,2304]{1,0:T(8,128)(2,1)} fusion(bf16[1,720,2304]{2,1,0:T(8,128)(2,1)S(1)} %copy-done, f32[192,720]{1,0:T(8,128)} %fusion.27, bf16[96,2304]{1,0:T(8,128)(2,1)} %bitcast.173, bf16[96,2304]{1,0:T(8,128)(2,1)} %bitcast.176, bf16[1,2,2304,720]{2,3,1,0:T(8,128)(2,1)} %param.26), kind=kOutput, calls=%fused_computation.4 | convolution fusion | flops 1277061120 | bytes 8994816 | tf_op jit(solution)/shard_map/dot_general | solution.py:283
  263.9 1.1 collective-permute-done.27
  265.0 1.6 add_convert_fusion.7
  267.6 4.2 %all-to-all-start.1 = ((bf16[4,48,2304]{2,1,0:T(8,128)(2,1)}), bf16[4,48,2304]{2,1,0:T(8,128)(2,1)}, u32[]{:S(2)}, u32[]{:S(2)}) async-start(bf16[4,48,2304]{2,1,0:T(8,128)(2,1)} %bitcast.169), calls=%async_computation.1 | async-start | bytes 1769472 | tf_op jit(solution)/shard_map/all_to_all | solution.py:289
  271.8 1.1 fusion.143
  273.1 11.5 %all-to-all-done.1 = bf16[4,48,2304]{2,1,0:T(8,128)(2,1)} async-done(((bf16[4,48,2304]{2,1,0:T(8,128)(2,1)}), bf16[4,48,2304]{2,1,0:T(8,128)(2,1)}, u32[]{:S(2)}, u32[]{:S(2)}) %all-to-all-start.1) | async-done | bytes 884768 | tf_op jit(solution)/shard_map/all_to_all | solution.py:289
  284.6 2.5 bitcast_convert_fusion
  287.1 4.0 %gather_fusion = f32[128,2304]{1,0:T(8,128)} fusion(f32[192,2304]{1,0:T(8,128)} %bitcast_convert_fusion, s32[1024]{0:T(1024)S(1)} %pad_clamp_fusion), kind=kCustom, calls=%fused_computation | custom fusion | bytes 2359808 | tf_op jit(solution)/shard_map/jit(_take)/gather | solution.py:297
  291.1 3.0 gather.7
  294.1 1.4 copy_select_fusion
  295.6 2.0 fusion.56
  (119 shorter events, 40.8 us)
Async XLA Ops:
  7.2 114.7 %copy-start = (bf16[1,720,2304]{2,1,0:T(8,128)(2,1)S(1)}, bf16[1,720,2304]{2,1,0:T(8,128)(2,1)}, u32[]{:S(2)}) copy-start(bf16[1,720,2304]{2,1,0:T(8,128)(2,1)} %param.27) | copy-start | bytes 9953284
  7.2 42.6 %all-gather.2.cloned.1.call-start = ((), (), s32[]{:S(2)}) async-start(), calls=%async_computation.2 | async-start | bytes 5898240 | tf_op jit(solution)/shard_map/all_gather | solution.py:227
  67.8 8.1 %copy-start.16 = (f32[2304]{0:T(1024)S(1)}, f32[2304]{0:T(1024)}, u32[]{:S(2)}) copy-start(f32[2304]{0:T(1024)} %param.23) | copy-start | bytes 27652
  75.1 0.8 copy-start.1
  75.1 12.3 %copy-start.15 = (s32[64,2]{0,1:T(2,128)S(1)}, s32[64,2]{0,1:T(2,128)}, u32[]{:S(2)}) copy-start(s32[64,2]{0,1:T(2,128)} %param.25) | copy-start | bytes 1540
  76.1 0.7 copy-start.2
  83.0 17.0 %all-to-all-start = ((bf16[4,48,2304]{2,1,0:T(8,128)(2,1)}), bf16[4,48,2304]{2,1,0:T(8,128)(2,1)}, u32[]{:S(2)}, u32[]{:S(2)}) async-start(bf16[4,48,2304]{2,1,0:T(8,128)(2,1)} %bitcast.170), calls=%async_computation | async-start | bytes 1769472 | tf_op jit(solution)/shard_map/all_to_all | solution.py:271
  101.2 8.2 %copy-start.3 = (bf16[2,48,2304]{2,1,0:T(8,128)(2,1)}, bf16[2,48,2304]{2,1,0:T(8,128)(2,1)S(1)}, u32[]{:S(2)}) copy-start(bf16[2,48,2304]{2,1,0:T(8,128)(2,1)S(1)} %get-tuple-element.30) | copy-start | bytes 1327108
  101.2 8.2 %copy-start.4 = (bf16[2,48,2304]{2,1,0:T(8,128)(2,1)}, bf16[2,48,2304]{2,1,0:T(8,128)(2,1)S(1)}, u32[]{:S(2)}) copy-start(bf16[2,48,2304]{2,1,0:T(8,128)(2,1)S(1)} %get-tuple-element.31) | copy-start | bytes 1327108
  101.2 11.7 %collective-permute-start = (bf16[96,2304]{1,0:T(8,128)(2,1)S(1)}, bf16[96,2304]{1,0:T(8,128)(2,1)S(1)}, u32[]{:S(2)}, u32[]{:S(2)}) collective-permute-start(bf16[96,2304]{1,0:T(8,128)(2,1)S(1)} %bitcast.174), channel_id=1, source_target_pairs={{0,4},{4,12},{12,20},{20,28},{28,24},{24,16},{16,8},{8,0},{1,5},{5... | collective-permute-start | bytes 1327112 | tf_op jit(solution)/shard_map/ppermute | solution.py:179
  105.0 11.3 %collective-permute-start.1 = (bf16[96,2304]{1,0:T(8,128)(2,1)S(1)}, bf16[96,2304]{1,0:T(8,128)(2,1)S(1)}, u32[]{:S(2)}, u32[]{:S(2)}) collective-permute-start(bf16[96,2304]{1,0:T(8,128)(2,1)S(1)} %bitcast.171), channel_id=1, source_target_pairs={{0,8},{4,0},{12,4},{20,12},{28,20},{24,28},{16,24},{8,16},{1,9},{5... | collective-permute-start | bytes 1327112 | tf_op jit(solution)/shard_map/ppermute | solution.py:179
  112.9 3.4 %copy-start.5 = (bf16[96,2304]{1,0:T(8,128)(2,1)}, bf16[96,2304]{1,0:T(8,128)(2,1)S(1)}, u32[]{:S(2)}) copy-start(bf16[96,2304]{1,0:T(8,128)(2,1)S(1)} %collective-permute-done) | copy-start | bytes 1327108
  116.3 0.8 copy-start.6
  117.1 0.9 copy-start.13
  127.5 13.4 %collective-permute-start.3 = (bf16[96,2304]{1,0:T(8,128)(2,1)}, bf16[96,2304]{1,0:T(8,128)(2,1)}, u32[]{:S(2)}, u32[]{:S(2)}) collective-permute-start(bf16[96,2304]{1,0:T(8,128)(2,1)} %copy-done.5), channel_id=1, source_target_pairs={{0,4},{4,12},{12,20},{20,28},{28,24},{24,16},{16,8},{8,0},{1,5},{5... | collective-permute-start | bytes 1327112 | tf_op jit(solution)/shard_map/ppermute | solution.py:179
  129.0 13.4 %collective-permute-start.4 = (bf16[96,2304]{1,0:T(8,128)(2,1)}, bf16[96,2304]{1,0:T(8,128)(2,1)}, u32[]{:S(2)}, u32[]{:S(2)}) collective-permute-start(bf16[96,2304]{1,0:T(8,128)(2,1)} %copy-done.6), channel_id=1, source_target_pairs={{0,8},{4,0},{12,4},{20,12},{28,20},{24,28},{16,24},{8,16},{1,9},{5... | collective-permute-start | bytes 1327112 | tf_op jit(solution)/shard_map/ppermute | solution.py:179
  131.6 24.2 %collective-permute-start.2 = (bf16[96,2304]{1,0:T(8,128)(2,1)}, bf16[96,2304]{1,0:T(8,128)(2,1)}, u32[]{:S(2)}, u32[]{:S(2)}) collective-permute-start(bf16[96,2304]{1,0:T(8,128)(2,1)} %get-tuple-element.28), channel_id=1, source_target_pairs={{0,4},{4,12},{12,20},{20,28},{28,24},{24,16},{16,8},{8,0},{1,5},{5... | collective-permute-start | bytes 1327112 | tf_op jit(solution)/shard_map/ppermute | solution.py:189
  133.1 22.7 %collective-permute-start.21 = (bf16[96,2304]{1,0:T(8,128)(2,1)}, bf16[96,2304]{1,0:T(8,128)(2,1)}, u32[]{:S(2)}, u32[]{:S(2)}) collective-permute-start(bf16[96,2304]{1,0:T(8,128)(2,1)} %get-tuple-element.29), channel_id=1, source_target_pairs={{0,8},{4,0},{12,4},{20,12},{28,20},{24,28},{16,24},{8,16},{1,9},{5... | collective-permute-start | bytes 1327112 | tf_op jit(solution)/shard_map/ppermute | solution.py:189
  143.4 0.9 copy-start.8
  148.2 12.2 %collective-permute-start.6 = (bf16[96,2304]{1,0:T(8,128)(2,1)}, bf16[96,2304]{1,0:T(8,128)(2,1)}, u32[]{:S(2)}, u32[]{:S(2)}) collective-permute-start(bf16[96,2304]{1,0:T(8,128)(2,1)} %collective-permute-done.3), channel_id=1, source_target_pairs={{0,4},{4,12},{12,20},{20,28},{28,24},{24,16},{16,8},{8,0},{1,5},{5... | collective-permute-start | bytes 1327112 | tf_op jit(solution)/shard_map/ppermute | solution.py:179
  149.7 11.8 %collective-permute-start.7 = (bf16[96,2304]{1,0:T(8,128)(2,1)}, bf16[96,2304]{1,0:T(8,128)(2,1)}, u32[]{:S(2)}, u32[]{:S(2)}) collective-permute-start(bf16[96,2304]{1,0:T(8,128)(2,1)} %collective-permute-done.4), channel_id=1, source_target_pairs={{0,8},{4,0},{12,4},{20,12},{28,20},{24,28},{16,24},{8,16},{1,9},{5... | collective-permute-start | bytes 1327112 | tf_op jit(solution)/shard_map/ppermute | solution.py:179
  158.4 16.6 %collective-permute-start.5 = (bf16[96,2304]{1,0:T(8,128)(2,1)}, bf16[96,2304]{1,0:T(8,128)(2,1)}, u32[]{:S(2)}, u32[]{:S(2)}) collective-permute-start(bf16[96,2304]{1,0:T(8,128)(2,1)} %get-tuple-element.26), channel_id=1, source_target_pairs={{0,4},{4,12},{12,20},{20,28},{28,24},{24,16},{16,8},{8,0},{1,5},{5... | collective-permute-start | bytes 1327112 | tf_op jit(solution)/shard_map/ppermute | solution.py:189
  159.8 15.1 %collective-permute-start.22 = (bf16[96,2304]{1,0:T(8,128)(2,1)}, bf16[96,2304]{1,0:T(8,128)(2,1)}, u32[]{:S(2)}, u32[]{:S(2)}) collective-permute-start(bf16[96,2304]{1,0:T(8,128)(2,1)} %get-tuple-element.27), channel_id=1, source_target_pairs={{0,8},{4,0},{12,4},{20,12},{28,20},{24,28},{16,24},{8,16},{1,9},{5... | collective-permute-start | bytes 1327112 | tf_op jit(solution)/shard_map/ppermute | solution.py:189
  162.5 0.9 copy-start.9
  167.3 12.4 %collective-permute-start.9 = (bf16[96,2304]{1,0:T(8,128)(2,1)}, bf16[96,2304]{1,0:T(8,128)(2,1)}, u32[]{:S(2)}, u32[]{:S(2)}) collective-permute-start(bf16[96,2304]{1,0:T(8,128)(2,1)} %collective-permute-done.6), channel_id=1, source_target_pairs={{0,4},{4,12},{12,20},{20,28},{28,24},{24,16},{16,8},{8,0},{1,5},{5... | collective-permute-start | bytes 1327112 | tf_op jit(solution)/shard_map/ppermute | solution.py:179
  168.8 12.6 %collective-permute-start.10 = (bf16[96,2304]{1,0:T(8,128)(2,1)}, bf16[96,2304]{1,0:T(8,128)(2,1)}, u32[]{:S(2)}, u32[]{:S(2)}) collective-permute-start(bf16[96,2304]{1,0:T(8,128)(2,1)} %collective-permute-done.7), channel_id=1, source_target_pairs={{0,8},{4,0},{12,4},{20,12},{28,20},{24,28},{16,24},{8,16},{1,9},{5... | collective-permute-start | bytes 1327112 | tf_op jit(solution)/shard_map/ppermute | solution.py:179
  177.5 17.4 %collective-permute-start.8 = (bf16[96,2304]{1,0:T(8,128)(2,1)}, bf16[96,2304]{1,0:T(8,128)(2,1)}, u32[]{:S(2)}, u32[]{:S(2)}) collective-permute-start(bf16[96,2304]{1,0:T(8,128)(2,1)} %get-tuple-element.24), channel_id=1, source_target_pairs={{0,4},{4,12},{12,20},{20,28},{28,24},{24,16},{16,8},{8,0},{1,5},{5... | collective-permute-start | bytes 1327112 | tf_op jit(solution)/shard_map/ppermute | solution.py:189
  179.0 15.9 %collective-permute-start.23 = (bf16[96,2304]{1,0:T(8,128)(2,1)}, bf16[96,2304]{1,0:T(8,128)(2,1)}, u32[]{:S(2)}, u32[]{:S(2)}) collective-permute-start(bf16[96,2304]{1,0:T(8,128)(2,1)} %get-tuple-element.25), channel_id=1, source_target_pairs={{0,8},{4,0},{12,4},{20,12},{28,20},{24,28},{16,24},{8,16},{1,9},{5... | collective-permute-start | bytes 1327112 | tf_op jit(solution)/shard_map/ppermute | solution.py:189
  182.4 0.9 copy-start.10
  187.2 12.3 %collective-permute-start.12 = (bf16[96,2304]{1,0:T(8,128)(2,1)}, bf16[96,2304]{1,0:T(8,128)(2,1)}, u32[]{:S(2)}, u32[]{:S(2)}) collective-permute-start(bf16[96,2304]{1,0:T(8,128)(2,1)} %collective-permute-done.9), channel_id=1, source_target_pairs={{0,4},{4,12},{12,20},{20,28},{28,24},{24,16},{16,8},{8,0},{1,5},{5... | collective-permute-start | bytes 1327112 | tf_op jit(solution)/shard_map/ppermute | solution.py:179
  188.7 12.5 %collective-permute-start.13 = (bf16[96,2304]{1,0:T(8,128)(2,1)}, bf16[96,2304]{1,0:T(8,128)(2,1)}, u32[]{:S(2)}, u32[]{:S(2)}) collective-permute-start(bf16[96,2304]{1,0:T(8,128)(2,1)} %collective-permute-done.10), channel_id=1, source_target_pairs={{0,8},{4,0},{12,4},{20,12},{28,20},{24,28},{16,24},{8,16},{1,9},{5... | collective-permute-start | bytes 1327112 | tf_op jit(solution)/shard_map/ppermute | solution.py:179
  197.4 17.3 %collective-permute-start.11 = (bf16[96,2304]{1,0:T(8,128)(2,1)}, bf16[96,2304]{1,0:T(8,128)(2,1)}, u32[]{:S(2)}, u32[]{:S(2)}) collective-permute-start(bf16[96,2304]{1,0:T(8,128)(2,1)} %get-tuple-element.22), channel_id=1, source_target_pairs={{0,4},{4,12},{12,20},{20,28},{28,24},{24,16},{16,8},{8,0},{1,5},{5... | collective-permute-start | bytes 1327112 | tf_op jit(solution)/shard_map/ppermute | solution.py:189
  198.9 15.8 %collective-permute-start.24 = (bf16[96,2304]{1,0:T(8,128)(2,1)}, bf16[96,2304]{1,0:T(8,128)(2,1)}, u32[]{:S(2)}, u32[]{:S(2)}) collective-permute-start(bf16[96,2304]{1,0:T(8,128)(2,1)} %get-tuple-element.23), channel_id=1, source_target_pairs={{0,8},{4,0},{12,4},{20,12},{28,20},{24,28},{16,24},{8,16},{1,9},{5... | collective-permute-start | bytes 1327112 | tf_op jit(solution)/shard_map/ppermute | solution.py:189
  202.3 0.9 copy-start.11
  207.1 13.3 %collective-permute-start.15 = (bf16[96,2304]{1,0:T(8,128)(2,1)}, bf16[96,2304]{1,0:T(8,128)(2,1)}, u32[]{:S(2)}, u32[]{:S(2)}) collective-permute-start(bf16[96,2304]{1,0:T(8,128)(2,1)} %collective-permute-done.12), channel_id=1, source_target_pairs={{0,4},{4,12},{12,20},{20,28},{28,24},{24,16},{16,8},{8,0},{1,5},{5... | collective-permute-start | bytes 1327112 | tf_op jit(solution)/shard_map/ppermute | solution.py:179
  208.5 13.3 %collective-permute-start.16 = (bf16[96,2304]{1,0:T(8,128)(2,1)}, bf16[96,2304]{1,0:T(8,128)(2,1)}, u32[]{:S(2)}, u32[]{:S(2)}) collective-permute-start(bf16[96,2304]{1,0:T(8,128)(2,1)} %collective-permute-done.13), channel_id=1, source_target_pairs={{0,8},{4,0},{12,4},{20,12},{28,20},{24,28},{16,24},{8,16},{1,9},{5... | collective-permute-start | bytes 1327112 | tf_op jit(solution)/shard_map/ppermute | solution.py:179
  217.3 18.0 %collective-permute-start.14 = (bf16[96,2304]{1,0:T(8,128)(2,1)}, bf16[96,2304]{1,0:T(8,128)(2,1)}, u32[]{:S(2)}, u32[]{:S(2)}) collective-permute-start(bf16[96,2304]{1,0:T(8,128)(2,1)} %get-tuple-element.20), channel_id=1, source_target_pairs={{0,4},{4,12},{12,20},{20,28},{28,24},{24,16},{16,8},{8,0},{1,5},{5... | collective-permute-start | bytes 1327112 | tf_op jit(solution)/shard_map/ppermute | solution.py:189
  218.7 16.6 %collective-permute-start.25 = (bf16[96,2304]{1,0:T(8,128)(2,1)}, bf16[96,2304]{1,0:T(8,128)(2,1)}, u32[]{:S(2)}, u32[]{:S(2)}) collective-permute-start(bf16[96,2304]{1,0:T(8,128)(2,1)} %get-tuple-element.21), channel_id=1, source_target_pairs={{0,8},{4,0},{12,4},{20,12},{28,20},{24,28},{16,24},{8,16},{1,9},{5... | collective-permute-start | bytes 1327112 | tf_op jit(solution)/shard_map/ppermute | solution.py:189
  222.8 0.9 copy-start.12
  227.7 12.6 %collective-permute-start.18 = (bf16[96,2304]{1,0:T(8,128)(2,1)}, bf16[96,2304]{1,0:T(8,128)(2,1)}, u32[]{:S(2)}, u32[]{:S(2)}) collective-permute-start(bf16[96,2304]{1,0:T(8,128)(2,1)} %collective-permute-done.15), channel_id=1, source_target_pairs={{0,4},{4,12},{12,20},{20,28},{28,24},{24,16},{16,8},{8,0},{1,5},{5... | collective-permute-start | bytes 1327112 | tf_op jit(solution)/shard_map/ppermute | solution.py:179
  228.4 12.9 %collective-permute-start.19 = (bf16[96,2304]{1,0:T(8,128)(2,1)}, bf16[96,2304]{1,0:T(8,128)(2,1)}, u32[]{:S(2)}, u32[]{:S(2)}) collective-permute-start(bf16[96,2304]{1,0:T(8,128)(2,1)} %collective-permute-done.16), channel_id=1, source_target_pairs={{0,8},{4,0},{12,4},{20,12},{28,20},{24,28},{16,24},{8,16},{1,9},{5... | collective-permute-start | bytes 1327112 | tf_op jit(solution)/shard_map/ppermute | solution.py:179
  237.8 14.9 %collective-permute-start.17 = (bf16[96,2304]{1,0:T(8,128)(2,1)}, bf16[96,2304]{1,0:T(8,128)(2,1)}, u32[]{:S(2)}, u32[]{:S(2)}) collective-permute-start(bf16[96,2304]{1,0:T(8,128)(2,1)} %get-tuple-element.18), channel_id=1, source_target_pairs={{0,4},{4,12},{12,20},{20,28},{28,24},{24,16},{16,8},{8,0},{1,5},{5... | collective-permute-start | bytes 1327112 | tf_op jit(solution)/shard_map/ppermute | solution.py:189
  238.6 14.2 %collective-permute-start.26 = (bf16[96,2304]{1,0:T(8,128)(2,1)}, bf16[96,2304]{1,0:T(8,128)(2,1)}, u32[]{:S(2)}, u32[]{:S(2)}) collective-permute-start(bf16[96,2304]{1,0:T(8,128)(2,1)} %get-tuple-element.19), channel_id=1, source_target_pairs={{0,8},{4,0},{12,4},{20,12},{28,20},{24,28},{16,24},{8,16},{1,9},{5... | collective-permute-start | bytes 1327112 | tf_op jit(solution)/shard_map/ppermute | solution.py:189
  242.4 0.9 copy-start.7
  255.3 8.6 %collective-permute-start.20 = (bf16[96,2304]{1,0:T(8,128)(2,1)}, bf16[96,2304]{1,0:T(8,128)(2,1)}, u32[]{:S(2)}, u32[]{:S(2)}) collective-permute-start(bf16[96,2304]{1,0:T(8,128)(2,1)} %get-tuple-element.16), channel_id=1, source_target_pairs={{0,4},{4,12},{12,20},{20,28},{28,24},{24,16},{16,8},{8,0},{1,5},{5... | collective-permute-start | bytes 1327112 | tf_op jit(solution)/shard_map/ppermute | solution.py:191
  256.4 8.6 %collective-permute-start.27 = (bf16[96,2304]{1,0:T(8,128)(2,1)}, bf16[96,2304]{1,0:T(8,128)(2,1)}, u32[]{:S(2)}, u32[]{:S(2)}) collective-permute-start(bf16[96,2304]{1,0:T(8,128)(2,1)} %get-tuple-element.17), channel_id=1, source_target_pairs={{0,8},{4,0},{12,4},{20,12},{28,20},{24,28},{16,24},{8,16},{1,9},{5... | collective-permute-start | bytes 1327112 | tf_op jit(solution)/shard_map/ppermute | solution.py:191
  262.9 8.9 %copy-start.14 = (bf16[2304,4]{0,1:T(4,128)(2,1)S(1)}, bf16[2304,4]{0,1:T(4,128)(2,1)}, u32[]{:S(2)}) copy-start(bf16[2304,4]{0,1:T(4,128)(2,1)} %param.24) | copy-start | bytes 55300
  267.6 17.0 %all-to-all-start.1 = ((bf16[4,48,2304]{2,1,0:T(8,128)(2,1)}), bf16[4,48,2304]{2,1,0:T(8,128)(2,1)}, u32[]{:S(2)}, u32[]{:S(2)}) async-start(bf16[4,48,2304]{2,1,0:T(8,128)(2,1)} %bitcast.169), calls=%async_computation.1 | async-start | bytes 1769472 | tf_op jit(solution)/shard_map/all_to_all | solution.py:289
Sparse Core Ops, SparseCore 0:
  9.5 40.1 all-gather.1
where the time goes:
time: 307 us; the launch traced here: 304 us
  matrix products  90.9 us (30%)
  waiting for transfers between devices  58.4 us (19%)
  local copies, waits for them, and re-layouts  40.1 us (13%)
  starting transfers between devices  36.9 us (12%)
  Pallas kernels  36.1 us (12%)
  other arithmetic  25.6 us (8%)
  between operations  16.4 us (5%)
    dot_general x8, matrix products, local(): jnp.dot(hidden_units, down_rows, preferred_element_type=jnp.float32)  44.8 us
    pallas_call x2, Pallas kernels, attend(): pl.pallas_call(functools.partial(attend_kernel, count=len(sources), scale...  36.1 us
    dot_general x8, matrix products, local(): gate_act = jnp.dot(pooled, gate_cols, preferred_element_type=jnp.float32)  31.2 us
    ppermute x14, waiting for transfers between devices, ring_gather(): piece = lax.ppermute(piece, 'dp', pairs)  17.9 us
    unnamed x42, local copies, waits for them, and re-layouts  15.7 us
    convert_element_type x6, other arithmetic, ring_reduce(): moving = (received + blocks[index].astype(jnp.float32)).astype(jnp.bfloat16)  15.2 us
    ppermute x14, starting transfers between devices, ring_gather(): piece = lax.ppermute(piece, 'dp', pairs)  14.2 us
    ppermute x14, starting transfers between devices, ring_reduce(): received = lax.ppermute(moving, 'dp', pairs).astype(jnp.float32)  14.2 us
  transfers between devices with their start and end apart: 31, of which 16 were waited for; matrix products, arithmetic and copies ran while one was open for 34% of the time, Pallas kernels for 6%

commit v1 on v0

--- a/solution.py
+++ b/solution.py
@@ -275,14 +275,19 @@
     backward = ring_gather(arrived[half:], ring, -1)
     forward_out = []
     backward_out = []
-    for index in range(len(ring)):
-        pooled = jnp.concatenate([forward[index], backward[index]], axis=0)
+    together = 2 if len(ring) % 2 == 0 else 1
+    for first in range(0, len(ring), together):
+        chosen = range(first, first + together)
+        pooled = jnp.concatenate(
+            [forward[index] for index in chosen] + [backward[index] for index in chosen], axis=0
+        )
         gate_act = jnp.dot(pooled, gate_cols, preferred_element_type=jnp.float32)
         upper = jnp.dot(pooled, up_cols, preferred_element_type=jnp.float32)
         hidden_units = (jax.nn.silu(gate_act) * upper).astype(jnp.bfloat16)
         partial = jnp.dot(hidden_units, down_rows, preferred_element_type=jnp.float32).astype(jnp.bfloat16)
-        forward_out.append(partial[:half])
-        backward_out.append(partial[half:])
+        for offset in range(together):
+            forward_out.append(partial[offset * half:(offset + 1) * half])
+            backward_out.append(partial[(together + offset) * half:(together + offset + 1) * half])
     summed_rows = jnp.concatenate(
         [ring_reduce(forward_out, ring, 1), ring_reduce(backward_out, ring, -1)], axis=0
     )

time: 307 us -> 333 us (1.085)
  waiting for transfers between devices: 58.4 us -> 122 us
  matrix products: 90.9 us -> 64.4 us
  blocking collectives: 0 us -> 15.1 us
  local copies, waits for them, and re-layouts: 40.1 us -> 27.7 us
  other arithmetic: 25.6 us -> 16.6 us
  starting transfers between devices: 36.9 us -> 32.8 us
    ppermute x14, waiting for transfers between devices: 17.9 us -> 57.9 us  [ring_gather(): piece = lax.ppermute(piece, 'dp', pairs)]
    ppermute x14, waiting for transfers between devices: 2.08 us -> 35.2 us  [ring_reduce(): received = lax.ppermute(moving, 'dp', pairs).astype(jnp.float32)]
    all_to_all x0 -> x1, blocking collectives: none -> 15.1 us  [local(): lax.all_to_all(outgoing, 'expert', split_axis=0, concat_axis=0, tiled=True)]
    dot_general x8 -> x4, matrix products: 44.8 us -> 30.5 us  [local(): jnp.dot(hidden_units, down_rows, preferred_element_type=jnp.float32)]
    all_to_all x1 -> x0, waiting for transfers between devices: 12.5 us -> none  [local(): lax.all_to_all(outgoing, 'expert', split_axis=0, concat_axis=0, tiled=True)]
    dot_general x8 -> x4, matrix products: 31.2 us -> 21 us  [local(): upper = jnp.dot(pooled, up_cols, preferred_element_type=jnp.float32)]
    concatenate x7 -> x3, local copies, waits for them, and re-layouts: 6.29 us -> 0.09 us  [local(): jnp.concatenate([forward[index] for index in chosen] + [backward[index] f...]
    convert_element_type x6, other arithmetic: 15.2 us -> 9.96 us  [ring_reduce(): moving = (received + blocks[index].astype(jnp.float32)).astype(jnp.bfloat16)]
  transfers between devices with their start and end apart: 31 -> 30, of which waited for: 16 -> 17; matrix products, arithmetic and copies ran while one was open for 34% -> 23% of each run, Pallas kernels for 6% -> 6%
where the time goes in v1:
time: 333 us; the launch traced here: 331 us
  waiting for transfers between devices  122 us (37%)
  matrix products  64.4 us (19%)
  Pallas kernels  36.1 us (11%)
  starting transfers between devices  32.8 us (10%)
  local copies, waits for them, and re-layouts  27.7 us (8%)
  other arithmetic  16.6 us (5%)
  between operations  16.4 us (5%)
  blocking collectives  15.1 us (5%)
    ppermute x14, waiting for transfers between devices, ring_gather(): piece = lax.ppermute(piece, 'dp', pairs)  57.9 us
    pallas_call x2, Pallas kernels, attend(): pl.pallas_call(functools.partial(attend_kernel, count=len(sources), scale...  36.1 us
    ppermute x14, waiting for transfers between devices, ring_reduce(): received = lax.ppermute(moving, 'dp', pairs).astype(jnp.float32)  35.2 us
    dot_general x4, matrix products, local(): jnp.dot(hidden_units, down_rows, preferred_element_type=jnp.float32)  30.5 us
    dot_general x4, matrix products, local(): upper = jnp.dot(pooled, up_cols, preferred_element_type=jnp.float32)  21 us
    all_gather x1, waiting for transfers between devices, local(): shard_rows = lax.all_gather(prompt_kv, 'expert', axis=1, tiled=True)  17.1 us
    all_to_all x1, blocking collectives, local(): lax.all_to_all(outgoing, 'expert', split_axis=0, concat_axis=0, tiled=True)  15.1 us
    ppermute x14, starting transfers between devices, ring_reduce(): received = lax.ppermute(moving, 'dp', pairs).astype(jnp.float32)  14.3 us
  transfers between devices with their start and end apart: 30, of which 17 were waited for; matrix products, arithmetic and copies ran while one was open for 23% of the time, Pallas kernels for 6%

profile of v1, /device:TPU:0, one launch (start us, length us, event | category | flops | bytes accessed | tf_op | source)
XLA Modules:
  0.0 331.5 jit_solution(1695206429889322464)
XLA Ops:
  7.9 1.8 slice.87.refs_0_
  13.8 18.7 %shard_map.152 = (f32[64,2304]{1,0:T(8,128)}, f32[64,2304]{1,0:T(8,128)}, f32[64,2304]{1,0:T(8,128)}) custom-call(bf16[64,2304]{1,0:T(8,128)(2,1)} %slice.87.refs_0_, bf16[512,4608]{1,0:T(8,128)(2,1)} %bitcast.115, bf16[512,4608]{1,0:T(8,128)(2,1)} %bitcast.116, f32[64,512]{1,0:T(8,128)} %broadcast_in_dim.42.refs_3_, bf16[64,6912]{1,0:T(8,128)(2,1)} %refs_5_.1, ...), custom_call_target="tpu_custom_call" | custom-call | tf_op jit(solution)/shard_map/pallas_call | solution.py:140
  32.6 17.1 %all-gather.2.cloned.1.call-done = bf16[1,512,4608]{2,1,0:T(8,128)(2,1)} async-done(((bf16[1,128,4608]{2,1,0:T(8,128)(2,1)}), bf16[1,512,4608]{2,1,0:T(8,128)(2,1)}) %all-gather.2.cloned.1.call-update) | async-done | bytes 4718608 | tf_op jit(solution)/shard_map/all_gather | solution.py:227
  50.4 17.4 %shard_map.153 = (f32[64,2304]{1,0:T(8,128)}, f32[64,2304]{1,0:T(8,128)}, f32[64,2304]{1,0:T(8,128)}) custom-call(bf16[64,2304]{1,0:T(8,128)(2,1)} %slice.87.refs_0_, bf16[512,4608]{1,0:T(8,128)(2,1)} %bitcast.117, bf16[512,4608]{1,0:T(8,128)(2,1)} %bitcast.118, f32[64,512]{1,0:T(8,128)} %broadcast_in_dim.47.refs_3_), custom_call_target="tpu_custom_call" | custom-call | tf_op jit(solution)/shard_map/pallas_call | solution.py:140
  67.8 7.3 %multiply_reduce_fusion = (f32[64]{0:T(128)S(1)}, f32[64,2304]{1,0:T(8,128)S(1)}) fusion(bf16[2304,2304]{1,0:T(8,128)(2,1)} %param.22, f32[64,2304]{1,0:T(8,128)} %get-tuple-element.13, f32[64,2304]{1,0:T(8,128)} %get-tuple-element.12, f32[64,2304]{1,0:T(8,128)} %get-tuple-element.11, f32[64,2304]{1,0:T(8,128)} %get-tuple-element.10, ...), kind=kOutput, calls=%fused_computation.83 | convolution fusion | flops 681983936 | bytes 15040768 | tf_op jit(solution)/shard_map/dot_general | solution.py:240
  76.8 1.1 broadcast_in_dim.51
  77.9 2.7 reshape.316
  80.6 1.4 convolution_convert_fusion.5
  82.1 15.1 %all_to_all.10 = bf16[4,48,2304]{2,1,0:T(8,128)(2,1)S(1)} all-to-all(bf16[4,48,2304]{2,1,0:T(8,128)(2,1)S(1)} %bitcast.120), channel_id=1, replica_groups=mesh['dp'=8,'expert'=4] {'expert'}, dimensions={0} | all-to-all | bytes 1769472 | tf_op jit(solution)/shard_map/all_to_all | solution.py:271
  97.2 1.5 collective-permute-start
  99.3 9.7 %collective-permute-done = bf16[96,2304]{1,0:T(8,128)(2,1)} collective-permute-done((bf16[96,2304]{1,0:T(8,128)(2,1)S(1)}, bf16[96,2304]{1,0:T(8,128)(2,1)}, u32[]{:S(2)}, u32[]{:S(2)}) %collective-permute-start) | collective-permute-done | bytes 442400 | tf_op jit(solution)/shard_map/ppermute | solution.py:179
  109.1 1.5 collective-permute-start.3
  111.1 5.1 %fusion.13 = f32[384,720]{0,1:T(8,128)} fusion(bf16[1,2,2304,720]{2,3,1,0:T(8,128)(2,1)} %param.26, bf16[96,2304]{1,0:T(8,128)(2,1)} %collective-permute-done.1, bf16[96,2304]{1,0:T(8,128)(2,1)S(1)} %bitcast.125, bf16[96,2304]{1,0:T(8,128)(2,1)} %collective-permute-done, bf16[96,2304]{1,0:T(8,128)(2,1)S(1)} %bitcast.122), kind=kOutput, calls=%fused_computation.21 | convolution fusion | flops 1281097728 | bytes 6193152 | tf_op jit(solution)/shard_map/dot_general | solution.py:285
  116.2 7.7 %convolution_convert_fusion.4 = bf16[384,2304]{1,0:T(8,128)(2,1)} fusion(bf16[1,720,2304]{2,1,0:T(8,128)(2,1)S(1)} %copy-done, f32[384,720]{0,1:T(8,128)} %fusion.13, bf16[1,2,2304,720]{2,3,1,0:T(8,128)(2,1)} %param.26, bf16[96,2304]{1,0:T(8,128)(2,1)} %collective-permute-done.1, bf16[96,2304]{1,0:T(8,128)(2,1)} %bitcast.126, ...), kind=kOutput, calls=%fused_computation.6 | convolution fusion | flops 2557661184 | bytes 11280384 | tf_op jit(solution)/shard_map/dot_general | solution.py:287
  123.9 1.5 collective-permute-start.4
  125.3 2.2 fusion.79
  127.5 1.5 collective-permute-start.2
  130.1 1.0 constant_dynamic-update-slice_fusion.3
  131.1 6.1 %collective-permute-done.4 = bf16[96,2304]{1,0:T(8,128)(2,1)} collective-permute-done((bf16[96,2304]{1,0:T(8,128)(2,1)}, bf16[96,2304]{1,0:T(8,128)(2,1)}, u32[]{:S(2)}, u32[]{:S(2)}) %collective-permute-start.4) | collective-permute-done | bytes 442400 | tf_op jit(solution)/shard_map/ppermute | solution.py:179
  137.2 1.0 constant_dynamic-update-slice_fusion.2
  138.3 1.0 constant_dynamic-update-slice_fusion.1
  139.3 9.0 %collective-permute-done.6 = bf16[96,2304]{1,0:T(8,128)(2,1)S(1)} collective-permute-done((bf16[96,2304]{1,0:T(8,128)(2,1)}, bf16[96,2304]{1,0:T(8,128)(2,1)S(1)}, u32[]{:S(2)}, u32[]{:S(2)}) %collective-permute-start.6) | collective-permute-done | bytes 442400 | tf_op jit(solution)/shard_map/ppermute | solution.py:179
  149.2 5.5 %fusion.11 = f32[384,720]{0,1:T(8,128)} fusion(bf16[384,2304]{1,0:T(8,128)(2,1)S(1)} %constant_dynamic-update-slice_fusion, bf16[1,2,2304,720]{2,3,1,0:T(8,128)(2,1)} %param.26), kind=kOutput, calls=%fused_computation.19 | convolution fusion | flops 1274019840 | bytes 6193152 | tf_op jit(solution)/shard_map/dot_general | solution.py:285
  154.7 1.5 collective-permute-start.9
  156.2 7.6 %convolution_convert_fusion.3 = bf16[384,2304]{1,0:T(8,128)(2,1)} fusion(bf16[1,720,2304]{2,1,0:T(8,128)(2,1)S(1)} %copy-done, f32[384,720]{0,1:T(8,128)} %fusion.11, bf16[384,2304]{1,0:T(8,128)(2,1)} %copy-done.14, bf16[1,2,2304,720]{2,3,1,0:T(8,128)(2,1)} %param.26), kind=kOutput, calls=%fused_computation.5 | convolution fusion | flops 2550583296 | bytes 11280384 | tf_op jit(solution)/shard_map/dot_general | solution.py:287
  163.8 1.8 add_convert_fusion.13
  165.6 1.6 collective-permute-start.7
  168.2 1.5 collective-permute-start.10
  169.7 9.0 %collective-permute-done.7 = bf16[96,2304]{1,0:T(8,128)(2,1)S(1)} collective-permute-done((bf16[96,2304]{1,0:T(8,128)(2,1)S(1)}, bf16[96,2304]{1,0:T(8,128)(2,1)S(1)}, u32[]{:S(2)}, u32[]{:S(2)}) %collective-permute-start.7) | collective-permute-done | bytes 442400 | tf_op jit(solution)/shard_map/ppermute | solution.py:189
  178.7 1.5 collective-permute-done.22
  180.2 1.1 add_convert_fusion.12
  181.8 1.5 collective-permute-start.23
  183.3 6.3 %collective-permute-done.11 = bf16[96,2304]{1,0:T(8,128)(2,1)S(1)} collective-permute-done((bf16[96,2304]{1,0:T(8,128)(2,1)S(1)}, bf16[96,2304]{1,0:T(8,128)(2,1)S(1)}, u32[]{:S(2)}, u32[]{:S(2)}) %collective-permute-start.11) | collective-permute-done | bytes 442400 | tf_op jit(solution)/shard_map/ppermute | solution.py:179
  190.2 1.0 constant_dynamic-update-slice_fusion.7
  191.2 1.0 constant_dynamic-update-slice_fusion.6
  192.3 11.5 %collective-permute-done.12 = bf16[96,2304]{1,0:T(8,128)(2,1)S(1)} collective-permute-done((bf16[96,2304]{1,0:T(8,128)(2,1)S(1)}, bf16[96,2304]{1,0:T(8,128)(2,1)S(1)}, u32[]{:S(2)}, u32[]{:S(2)}) %collective-permute-start.12) | collective-permute-done | bytes 442400 | tf_op jit(solution)/shard_map/ppermute | solution.py:179
  204.7 5.5 %fusion.9 = f32[384,720]{0,1:T(8,128)} fusion(bf16[384,2304]{1,0:T(8,128)(2,1)S(1)} %constant_dynamic-update-slice_fusion.4, bf16[1,2,2304,720]{2,3,1,0:T(8,128)(2,1)} %param.26), kind=kOutput, calls=%fused_computation.17 | convolution fusion | flops 1274019840 | bytes 6193152 | tf_op jit(solution)/shard_map/dot_general | solution.py:285
  210.7 7.6 %convolution_convert_fusion.2 = bf16[384,2304]{1,0:T(8,128)(2,1)} fusion(bf16[1,720,2304]{2,1,0:T(8,128)(2,1)S(1)} %copy-done, f32[384,720]{0,1:T(8,128)} %fusion.9, bf16[384,2304]{1,0:T(8,128)(2,1)} %copy-done.15, bf16[1,2,2304,720]{2,3,1,0:T(8,128)(2,1)} %param.26), kind=kOutput, calls=%fused_computation.4 | convolution fusion | flops 2550583296 | bytes 11280384 | tf_op jit(solution)/shard_map/dot_general | solution.py:287
  218.4 2.5 add_convert_fusion.11
  221.5 1.4 collective-permute-start.24
  224.1 1.5 collective-permute-start.17
  226.1 8.1 %collective-permute-done.13 = bf16[96,2304]{1,0:T(8,128)(2,1)} collective-permute-done((bf16[96,2304]{1,0:T(8,128)(2,1)}, bf16[96,2304]{1,0:T(8,128)(2,1)}, u32[]{:S(2)}, u32[]{:S(2)}) %collective-permute-start.13) | collective-permute-done | bytes 442400 | tf_op jit(solution)/shard_map/ppermute | solution.py:189
  234.9 2.6 add_convert_fusion.10
  238.0 1.5 collective-permute-start.25
  239.5 4.8 %collective-permute-done.17 = bf16[96,2304]{1,0:T(8,128)(2,1)S(1)} collective-permute-done((bf16[96,2304]{1,0:T(8,128)(2,1)}, bf16[96,2304]{1,0:T(8,128)(2,1)S(1)}, u32[]{:S(2)}, u32[]{:S(2)}) %collective-permute-start.17) | collective-permute-done | bytes 442400 | tf_op jit(solution)/shard_map/ppermute | solution.py:179
  244.3 1.4 collective-permute-start.18
  245.6 1.0 constant_dynamic-update-slice_fusion.11
  246.8 10.4 %collective-permute-done.18 = bf16[96,2304]{1,0:T(8,128)(2,1)S(1)} collective-permute-done((bf16[96,2304]{1,0:T(8,128)(2,1)S(1)}, bf16[96,2304]{1,0:T(8,128)(2,1)S(1)}, u32[]{:S(2)}, u32[]{:S(2)}) %collective-permute-start.18) | collective-permute-done | bytes 442400 | tf_op jit(solution)/shard_map/ppermute | solution.py:179
  257.2 1.2 copy-done.13
  258.4 4.9 %fusion.7 = f32[384,720]{0,1:T(8,128)} fusion(bf16[384,2304]{1,0:T(8,128)(2,1)S(1)} %constant_dynamic-update-slice_fusion.8, bf16[1,2,2304,720]{2,3,1,0:T(8,128)(2,1)} %param.26), kind=kOutput, calls=%fused_computation.15 | convolution fusion | flops 1274019840 | bytes 6193152 | tf_op jit(solution)/shard_map/dot_general | solution.py:285
  263.3 7.6 %convolution_convert_fusion.1 = bf16[384,2304]{1,0:T(8,128)(2,1)} fusion(bf16[1,720,2304]{2,1,0:T(8,128)(2,1)S(1)} %copy-done, f32[384,720]{0,1:T(8,128)} %fusion.7, bf16[384,2304]{1,0:T(8,128)(2,1)} %copy-done.13, bf16[1,2,2304,720]{2,3,1,0:T(8,128)(2,1)} %param.26), kind=kOutput, calls=%fused_computation.3 | convolution fusion | flops 2550583296 | bytes 11280384 | tf_op jit(solution)/shard_map/dot_general | solution.py:287
  270.9 1.8 add_convert_fusion.9
  273.3 1.5 collective-permute-start.26
  275.0 1.2 fusion
  276.2 8.7 %collective-permute-done.19 = bf16[96,2304]{1,0:T(8,128)(2,1)S(1)} collective-permute-done((bf16[96,2304]{1,0:T(8,128)(2,1)S(1)}, bf16[96,2304]{1,0:T(8,128)(2,1)S(1)}, u32[]{:S(2)}, u32[]{:S(2)}) %collective-permute-start.19) | collective-permute-done | bytes 442400 | tf_op jit(solution)/shard_map/ppermute | solution.py:189
  286.1 2.0 collective-permute-start.27
  288.1 6.3 %collective-permute-done.20 = bf16[96,2304]{1,0:T(8,128)(2,1)S(1)} collective-permute-done((bf16[96,2304]{1,0:T(8,128)(2,1)S(1)}, bf16[96,2304]{1,0:T(8,128)(2,1)S(1)}, u32[]{:S(2)}, u32[]{:S(2)}) %collective-permute-start.20) | collective-permute-done | bytes 442400 | tf_op jit(solution)/shard_map/ppermute | solution.py:191
  295.7 4.2 %all-to-all-start.1 = ((bf16[4,48,2304]{2,1,0:T(8,128)(2,1)}), bf16[4,48,2304]{2,1,0:T(8,128)(2,1)}, u32[]{:S(2)}, u32[]{:S(2)}) async-start(bf16[4,48,2304]{2,1,0:T(8,128)(2,1)} %bitcast.119), calls=%async_computation.1 | async-start | bytes 1769472 | tf_op jit(solution)/shard_map/all_to_all | solution.py:294
  299.9 1.1 fusion.81
  301.1 11.5 %all-to-all-done.1 = bf16[4,48,2304]{2,1,0:T(8,128)(2,1)} async-done(((bf16[4,48,2304]{2,1,0:T(8,128)(2,1)}), bf16[4,48,2304]{2,1,0:T(8,128)(2,1)}, u32[]{:S(2)}, u32[]{:S(2)}) %all-to-all-start.1) | async-done | bytes 884768 | tf_op jit(solution)/shard_map/all_to_all | solution.py:294
  312.7 2.5 bitcast_convert_fusion
  315.2 4.0 %gather_fusion = f32[128,2304]{1,0:T(8,128)} fusion(f32[192,2304]{1,0:T(8,128)} %bitcast_convert_fusion, s32[1024]{0:T(1024)S(1)} %pad_clamp_fusion), kind=kCustom, calls=%fused_computation | custom fusion | bytes 2359808 | tf_op jit(solution)/shard_map/jit(_take)/gather | solution.py:302
  319.2 3.0 gather.7
  322.2 1.5 copy_select_fusion
  (114 shorter events, 19.6 us)
Async XLA Ops:
  7.2 109.0 %copy-start = (bf16[1,720,2304]{2,1,0:T(8,128)(2,1)S(1)}, bf16[1,720,2304]{2,1,0:T(8,128)(2,1)}, u32[]{:S(2)}) copy-start(bf16[1,720,2304]{2,1,0:T(8,128)(2,1)} %param.27) | copy-start | bytes 9953284
  7.2 3.9 %copy-start.17 = (s32[64,2]{0,1:T(2,128)S(1)}, s32[64,2]{0,1:T(2,128)}, u32[]{:S(2)}) copy-start(s32[64,2]{0,1:T(2,128)} %param.25) | copy-start | bytes 1540
  7.2 4.1 %copy-start.19 = (s32[1,64]{1,0:T(1,128)S(1)}, s32[1,64]{1,0:T(1,128)}, u32[]{:S(2)}) copy-start(s32[1,64]{1,0:T(1,128)} %param.20) | copy-start | bytes 772
  7.2 42.6 %all-gather.2.cloned.1.call-start = ((), (), s32[]{:S(2)}) async-start(), calls=%async_computation.2 | async-start | bytes 5898240 | tf_op jit(solution)/shard_map/all_gather | solution.py:227
  67.8 8.1 %copy-start.18 = (f32[2304]{0:T(1024)S(1)}, f32[2304]{0:T(1024)}, u32[]{:S(2)}) copy-start(f32[2304]{0:T(1024)} %param.23) | copy-start | bytes 27652
  75.1 0.8 copy-start.2
  76.1 0.7 copy-start.4
  97.2 13.9 %copy-start.8 = (bf16[2,48,2304]{2,1,0:T(8,128)(2,1)}, bf16[2,48,2304]{2,1,0:T(8,128)(2,1)S(1)}, u32[]{:S(2)}) copy-start(bf16[2,48,2304]{2,1,0:T(8,128)(2,1)S(1)} %get-tuple-element.30) | copy-start | bytes 1327108
  97.2 13.9 %copy-start.9 = (bf16[2,48,2304]{2,1,0:T(8,128)(2,1)}, bf16[2,48,2304]{2,1,0:T(8,128)(2,1)S(1)}, u32[]{:S(2)}) copy-start(bf16[2,48,2304]{2,1,0:T(8,128)(2,1)S(1)} %get-tuple-element.31) | copy-start | bytes 1327108
  97.2 11.8 %collective-permute-start = (bf16[96,2304]{1,0:T(8,128)(2,1)S(1)}, bf16[96,2304]{1,0:T(8,128)(2,1)}, u32[]{:S(2)}, u32[]{:S(2)}) collective-permute-start(bf16[96,2304]{1,0:T(8,128)(2,1)S(1)} %bitcast.121), channel_id=1, source_target_pairs={{0,4},{4,12},{12,20},{20,28},{28,24},{24,16},{16,8},{8,0},{1,5},{5... | collective-permute-start | bytes 1327112 | tf_op jit(solution)/shard_map/ppermute | solution.py:179
  98.8 11.8 %collective-permute-start.1 = (bf16[96,2304]{1,0:T(8,128)(2,1)S(1)}, bf16[96,2304]{1,0:T(8,128)(2,1)}, u32[]{:S(2)}, u32[]{:S(2)}) collective-permute-start(bf16[96,2304]{1,0:T(8,128)(2,1)S(1)} %bitcast.124), channel_id=1, source_target_pairs={{0,8},{4,0},{12,4},{20,12},{28,20},{24,28},{16,24},{8,16},{1,9},{5... | collective-permute-start | bytes 1327112 | tf_op jit(solution)/shard_map/ppermute | solution.py:179
  109.1 14.8 %collective-permute-start.3 = (bf16[96,2304]{1,0:T(8,128)(2,1)}, bf16[96,2304]{1,0:T(8,128)(2,1)}, u32[]{:S(2)}, u32[]{:S(2)}) collective-permute-start(bf16[96,2304]{1,0:T(8,128)(2,1)} %collective-permute-done), channel_id=1, source_target_pairs={{0,4},{4,12},{12,20},{20,28},{28,24},{24,16},{16,8},{8,0},{1,5},{5... | collective-permute-start | bytes 1327112 | tf_op jit(solution)/shard_map/ppermute | solution.py:179
  110.5 19.0 %collective-permute-start.5 = (bf16[96,2304]{1,0:T(8,128)(2,1)}, bf16[96,2304]{1,0:T(8,128)(2,1)}, u32[]{:S(2)}, u32[]{:S(2)}) collective-permute-start(bf16[96,2304]{1,0:T(8,128)(2,1)} %collective-permute-done.1), channel_id=1, source_target_pairs={{0,8},{4,0},{12,4},{20,12},{28,20},{24,28},{16,24},{8,16},{1,9},{5... | collective-permute-start | bytes 1327112 | tf_op jit(solution)/shard_map/ppermute | solution.py:179
  123.9 13.4 %collective-permute-start.4 = (bf16[96,2304]{1,0:T(8,128)(2,1)}, bf16[96,2304]{1,0:T(8,128)(2,1)}, u32[]{:S(2)}, u32[]{:S(2)}) collective-permute-start(bf16[96,2304]{1,0:T(8,128)(2,1)} %collective-permute-done.3), channel_id=1, source_target_pairs={{0,4},{4,12},{12,20},{20,28},{28,24},{24,16},{16,8},{8,0},{1,5},{5... | collective-permute-start | bytes 1327112 | tf_op jit(solution)/shard_map/ppermute | solution.py:179
  127.5 36.3 %collective-permute-start.2 = (bf16[96,2304]{1,0:T(8,128)(2,1)}, bf16[96,2304]{1,0:T(8,128)(2,1)}, u32[]{:S(2)}, u32[]{:S(2)}) collective-permute-start(bf16[96,2304]{1,0:T(8,128)(2,1)} %get-tuple-element.28), channel_id=1, source_target_pairs={{0,4},{4,12},{12,20},{20,28},{28,24},{24,16},{16,8},{8,0},{1,5},{5... | collective-permute-start | bytes 1327112 | tf_op jit(solution)/shard_map/ppermute | solution.py:189
  129.0 34.8 %collective-permute-start.21 = (bf16[96,2304]{1,0:T(8,128)(2,1)}, bf16[96,2304]{1,0:T(8,128)(2,1)}, u32[]{:S(2)}, u32[]{:S(2)}) collective-permute-start(bf16[96,2304]{1,0:T(8,128)(2,1)} %get-tuple-element.29), channel_id=1, source_target_pairs={{0,8},{4,0},{12,4},{20,12},{28,20},{24,28},{16,24},{8,16},{1,9},{5... | collective-permute-start | bytes 1327112 | tf_op jit(solution)/shard_map/ppermute | solution.py:189
  129.5 18.8 %collective-permute-start.6 = (bf16[96,2304]{1,0:T(8,128)(2,1)}, bf16[96,2304]{1,0:T(8,128)(2,1)S(1)}, u32[]{:S(2)}, u32[]{:S(2)}) collective-permute-start(bf16[96,2304]{1,0:T(8,128)(2,1)} %collective-permute-done.5), channel_id=1, source_target_pairs={{0,8},{4,0},{12,4},{20,12},{28,20},{24,28},{16,24},{8,16},{1,9},{5... | collective-permute-start | bytes 1327112 | tf_op jit(solution)/shard_map/ppermute | solution.py:179
  148.4 0.8 copy-start.11
  149.2 5.5 %copy-start.14 = (bf16[384,2304]{1,0:T(8,128)(2,1)}, bf16[384,2304]{1,0:T(8,128)(2,1)S(1)}, u32[]{:S(2)}) copy-start(bf16[384,2304]{1,0:T(8,128)(2,1)S(1)} %constant_dynamic-update-slice_fusion) | copy-start | bytes 5308420
  154.7 13.5 %collective-permute-start.9 = (bf16[96,2304]{1,0:T(8,128)(2,1)}, bf16[96,2304]{1,0:T(8,128)(2,1)}, u32[]{:S(2)}, u32[]{:S(2)}) collective-permute-start(bf16[96,2304]{1,0:T(8,128)(2,1)} %collective-permute-done.4), channel_id=1, source_target_pairs={{0,4},{4,12},{12,20},{20,28},{28,24},{24,16},{16,8},{8,0},{1,5},{5... | collective-permute-start | bytes 1327112 | tf_op jit(solution)/shard_map/ppermute | solution.py:179
  163.8 3.9 %copy-start.12 = (bf16[96,2304]{1,0:T(8,128)(2,1)S(1)}, bf16[96,2304]{1,0:T(8,128)(2,1)}, u32[]{:S(2)}) copy-start(bf16[96,2304]{1,0:T(8,128)(2,1)} %copy-done.11) | copy-start | bytes 1327108
  163.8 16.4 %copy-start.6 = (bf16[384,2304]{1,0:T(8,128)(2,1)S(1)}, bf16[384,2304]{1,0:T(8,128)(2,1)}, u32[]{:S(2)}) copy-start(bf16[384,2304]{1,0:T(8,128)(2,1)} %convolution_convert_fusion.3) | copy-start | bytes 5308420
  165.6 13.1 %collective-permute-start.7 = (bf16[96,2304]{1,0:T(8,128)(2,1)S(1)}, bf16[96,2304]{1,0:T(8,128)(2,1)S(1)}, u32[]{:S(2)}, u32[]{:S(2)}) collective-permute-start(bf16[96,2304]{1,0:T(8,128)(2,1)S(1)} %get-tuple-element.26), channel_id=1, source_target_pairs={{0,4},{4,12},{12,20},{20,28},{28,24},{24,16},{16,8},{8,0},{1,5},{5... | collective-permute-start | bytes 1327112 | tf_op jit(solution)/shard_map/ppermute | solution.py:189
  167.1 13.0 %collective-permute-start.22 = (bf16[96,2304]{1,0:T(8,128)(2,1)S(1)}, bf16[96,2304]{1,0:T(8,128)(2,1)S(1)}, u32[]{:S(2)}, u32[]{:S(2)}) collective-permute-start(bf16[96,2304]{1,0:T(8,128)(2,1)S(1)} %get-tuple-element.27), channel_id=1, source_target_pairs={{0,8},{4,0},{12,4},{20,12},{28,20},{24,28},{16,24},{8,16},{1,9},{5... | collective-permute-start | bytes 1327112 | tf_op jit(solution)/shard_map/ppermute | solution.py:189
  167.7 22.0 %collective-permute-start.11 = (bf16[96,2304]{1,0:T(8,128)(2,1)S(1)}, bf16[96,2304]{1,0:T(8,128)(2,1)S(1)}, u32[]{:S(2)}, u32[]{:S(2)}) collective-permute-start(bf16[96,2304]{1,0:T(8,128)(2,1)S(1)} %copy-done.12), channel_id=1, source_target_pairs={{0,8},{4,0},{12,4},{20,12},{28,20},{24,28},{16,24},{8,16},{1,9},{5... | collective-permute-start | bytes 1327112 | tf_op jit(solution)/shard_map/ppermute | solution.py:179
  168.2 23.0 %collective-permute-start.10 = (bf16[96,2304]{1,0:T(8,128)(2,1)}, bf16[96,2304]{1,0:T(8,128)(2,1)}, u32[]{:S(2)}, u32[]{:S(2)}) collective-permute-start(bf16[96,2304]{1,0:T(8,128)(2,1)} %collective-permute-done.9), channel_id=1, source_target_pairs={{0,4},{4,12},{12,20},{20,28},{28,24},{24,16},{16,8},{8,0},{1,5},{5... | collective-permute-start | bytes 1327112 | tf_op jit(solution)/shard_map/ppermute | solution.py:179
  181.3 37.1 %collective-permute-start.8 = (bf16[96,2304]{1,0:T(8,128)(2,1)}, bf16[96,2304]{1,0:T(8,128)(2,1)}, u32[]{:S(2)}, u32[]{:S(2)}) collective-permute-start(bf16[96,2304]{1,0:T(8,128)(2,1)} %get-tuple-element.24), channel_id=1, source_target_pairs={{0,4},{4,12},{12,20},{20,28},{28,24},{24,16},{16,8},{8,0},{1,5},{5... | collective-permute-start | bytes 1327112 | tf_op jit(solution)/shard_map/ppermute | solution.py:189
  181.8 36.5 %collective-permute-start.23 = (bf16[96,2304]{1,0:T(8,128)(2,1)}, bf16[96,2304]{1,0:T(8,128)(2,1)}, u32[]{:S(2)}, u32[]{:S(2)}) collective-permute-start(bf16[96,2304]{1,0:T(8,128)(2,1)} %get-tuple-element.25), channel_id=1, source_target_pairs={{0,8},{4,0},{12,4},{20,12},{28,20},{24,28},{16,24},{8,16},{1,9},{5... | collective-permute-start | bytes 1327112 | tf_op jit(solution)/shard_map/ppermute | solution.py:189
  189.7 14.2 %collective-permute-start.12 = (bf16[96,2304]{1,0:T(8,128)(2,1)S(1)}, bf16[96,2304]{1,0:T(8,128)(2,1)S(1)}, u32[]{:S(2)}, u32[]{:S(2)}) collective-permute-start(bf16[96,2304]{1,0:T(8,128)(2,1)S(1)} %collective-permute-done.11), channel_id=1, source_target_pairs={{0,8},{4,0},{12,4},{20,12},{28,20},{24,28},{16,24},{8,16},{1,9},{5... | collective-permute-start | bytes 1327112 | tf_op jit(solution)/shard_map/ppermute | solution.py:179
  203.8 0.8 copy-start.10
  204.7 5.5 %copy-start.15 = (bf16[384,2304]{1,0:T(8,128)(2,1)}, bf16[384,2304]{1,0:T(8,128)(2,1)S(1)}, u32[]{:S(2)}) copy-start(bf16[384,2304]{1,0:T(8,128)(2,1)S(1)} %constant_dynamic-update-slice_fusion.4) | copy-start | bytes 5308420
  210.2 15.4 %collective-permute-start.15 = (bf16[96,2304]{1,0:T(8,128)(2,1)}, bf16[96,2304]{1,0:T(8,128)(2,1)}, u32[]{:S(2)}, u32[]{:S(2)}) collective-permute-start(bf16[96,2304]{1,0:T(8,128)(2,1)} %collective-permute-done.10), channel_id=1, source_target_pairs={{0,4},{4,12},{12,20},{20,28},{28,24},{24,16},{16,8},{8,0},{1,5},{5... | collective-permute-start | bytes 1327112 | tf_op jit(solution)/shard_map/ppermute | solution.py:179
  220.9 13.4 %collective-permute-start.13 = (bf16[96,2304]{1,0:T(8,128)(2,1)}, bf16[96,2304]{1,0:T(8,128)(2,1)}, u32[]{:S(2)}, u32[]{:S(2)}) collective-permute-start(bf16[96,2304]{1,0:T(8,128)(2,1)} %get-tuple-element.22), channel_id=1, source_target_pairs={{0,4},{4,12},{12,20},{20,28},{28,24},{24,16},{16,8},{8,0},{1,5},{5... | collective-permute-start | bytes 1327112 | tf_op jit(solution)/shard_map/ppermute | solution.py:189
  221.5 13.4 %collective-permute-start.24 = (bf16[96,2304]{1,0:T(8,128)(2,1)}, bf16[96,2304]{1,0:T(8,128)(2,1)}, u32[]{:S(2)}, u32[]{:S(2)}) collective-permute-start(bf16[96,2304]{1,0:T(8,128)(2,1)} %get-tuple-element.23), channel_id=1, source_target_pairs={{0,8},{4,0},{12,4},{20,12},{28,20},{24,28},{16,24},{8,16},{1,9},{5... | collective-permute-start | bytes 1327112 | tf_op jit(solution)/shard_map/ppermute | solution.py:189
  224.1 20.2 %collective-permute-start.17 = (bf16[96,2304]{1,0:T(8,128)(2,1)}, bf16[96,2304]{1,0:T(8,128)(2,1)S(1)}, u32[]{:S(2)}, u32[]{:S(2)}) collective-permute-start(bf16[96,2304]{1,0:T(8,128)(2,1)} %copy-done.10), channel_id=1, source_target_pairs={{0,8},{4,0},{12,4},{20,12},{28,20},{24,28},{16,24},{8,16},{1,9},{5... | collective-permute-start | bytes 1327112 | tf_op jit(solution)/shard_map/ppermute | solution.py:179
  225.6 21.1 %collective-permute-start.16 = (bf16[96,2304]{1,0:T(8,128)(2,1)}, bf16[96,2304]{1,0:T(8,128)(2,1)S(1)}, u32[]{:S(2)}, u32[]{:S(2)}) collective-permute-start(bf16[96,2304]{1,0:T(8,128)(2,1)} %collective-permute-done.15), channel_id=1, source_target_pairs={{0,4},{4,12},{12,20},{20,28},{28,24},{24,16},{16,8},{8,0},{1,5},{5... | collective-permute-start | bytes 1327112 | tf_op jit(solution)/shard_map/ppermute | solution.py:179
  237.5 33.4 %collective-permute-start.14 = (bf16[96,2304]{1,0:T(8,128)(2,1)}, bf16[96,2304]{1,0:T(8,128)(2,1)}, u32[]{:S(2)}, u32[]{:S(2)}) collective-permute-start(bf16[96,2304]{1,0:T(8,128)(2,1)} %get-tuple-element.20), channel_id=1, source_target_pairs={{0,4},{4,12},{12,20},{20,28},{28,24},{24,16},{16,8},{8,0},{1,5},{5... | collective-permute-start | bytes 1327112 | tf_op jit(solution)/shard_map/ppermute | solution.py:189
  238.0 32.9 %collective-permute-start.25 = (bf16[96,2304]{1,0:T(8,128)(2,1)}, bf16[96,2304]{1,0:T(8,128)(2,1)}, u32[]{:S(2)}, u32[]{:S(2)}) collective-permute-start(bf16[96,2304]{1,0:T(8,128)(2,1)} %get-tuple-element.21), channel_id=1, source_target_pairs={{0,8},{4,0},{12,4},{20,12},{28,20},{24,28},{16,24},{8,16},{1,9},{5... | collective-permute-start | bytes 1327112 | tf_op jit(solution)/shard_map/ppermute | solution.py:189
  244.3 12.9 %collective-permute-start.18 = (bf16[96,2304]{1,0:T(8,128)(2,1)S(1)}, bf16[96,2304]{1,0:T(8,128)(2,1)S(1)}, u32[]{:S(2)}, u32[]{:S(2)}) collective-permute-start(bf16[96,2304]{1,0:T(8,128)(2,1)S(1)} %collective-permute-done.17), channel_id=1, source_target_pairs={{0,8},{4,0},{12,4},{20,12},{28,20},{24,28},{16,24},{8,16},{1,9},{5... | collective-permute-start | bytes 1327112 | tf_op jit(solution)/shard_map/ppermute | solution.py:179
  257.2 1.2 copy-start.13
  270.9 4.1 %copy-start.1 = (bf16[64,6912]{1,0:T(8,128)(2,1)S(1)}, bf16[64,6912]{1,0:T(8,128)(2,1)}, u32[]{:S(2)}) copy-start(bf16[64,6912]{1,0:T(8,128)(2,1)} %refs_5_.1) | copy-start | bytes 2654212
  270.9 14.9 %copy-start.7 = (bf16[384,2304]{1,0:T(8,128)(2,1)S(1)}, bf16[384,2304]{1,0:T(8,128)(2,1)}, u32[]{:S(2)}) copy-start(bf16[384,2304]{1,0:T(8,128)(2,1)} %convolution_convert_fusion.1) | copy-start | bytes 5308420
  272.7 12.3 %collective-permute-start.19 = (bf16[96,2304]{1,0:T(8,128)(2,1)S(1)}, bf16[96,2304]{1,0:T(8,128)(2,1)S(1)}, u32[]{:S(2)}, u32[]{:S(2)}) collective-permute-start(bf16[96,2304]{1,0:T(8,128)(2,1)S(1)} %get-tuple-element.18), channel_id=1, source_target_pairs={{0,4},{4,12},{12,20},{20,28},{28,24},{24,16},{16,8},{8,0},{1,5},{5... | collective-permute-start | bytes 1327112 | tf_op jit(solution)/shard_map/ppermute | solution.py:189
  273.3 12.5 %collective-permute-start.26 = (bf16[96,2304]{1,0:T(8,128)(2,1)S(1)}, bf16[96,2304]{1,0:T(8,128)(2,1)S(1)}, u32[]{:S(2)}, u32[]{:S(2)}) collective-permute-start(bf16[96,2304]{1,0:T(8,128)(2,1)S(1)} %get-tuple-element.19), channel_id=1, source_target_pairs={{0,8},{4,0},{12,4},{20,12},{28,20},{24,28},{16,24},{8,16},{1,9},{5... | collective-permute-start | bytes 1327112 | tf_op jit(solution)/shard_map/ppermute | solution.py:189
  275.0 19.5 %copy-start.5 = (bf16[384,2304]{1,0:T(8,128)(2,1)S(1)}, bf16[384,2304]{1,0:T(8,128)(2,1)}, u32[]{:S(2)}) copy-start(bf16[384,2304]{1,0:T(8,128)(2,1)} %convolution_convert_fusion.4) | copy-start | bytes 5308420
  286.0 8.4 %collective-permute-start.20 = (bf16[96,2304]{1,0:T(8,128)(2,1)S(1)}, bf16[96,2304]{1,0:T(8,128)(2,1)S(1)}, u32[]{:S(2)}, u32[]{:S(2)}) collective-permute-start(bf16[96,2304]{1,0:T(8,128)(2,1)S(1)} %get-tuple-element.16), channel_id=1, source_target_pairs={{0,4},{4,12},{12,20},{20,28},{28,24},{24,16},{16,8},{8,0},{1,5},{5... | collective-permute-start | bytes 1327112 | tf_op jit(solution)/shard_map/ppermute | solution.py:191
  286.1 8.4 %collective-permute-start.27 = (bf16[96,2304]{1,0:T(8,128)(2,1)S(1)}, bf16[96,2304]{1,0:T(8,128)(2,1)S(1)}, u32[]{:S(2)}, u32[]{:S(2)}) collective-permute-start(bf16[96,2304]{1,0:T(8,128)(2,1)S(1)} %get-tuple-element.17), channel_id=1, source_target_pairs={{0,8},{4,0},{12,4},{20,12},{28,20},{24,28},{16,24},{8,16},{1,9},{5... | collective-permute-start | bytes 1327112 | tf_op jit(solution)/shard_map/ppermute | solution.py:191
  294.7 5.3 %copy-start.16 = (bf16[2304,4]{0,1:T(4,128)(2,1)S(1)}, bf16[2304,4]{0,1:T(4,128)(2,1)}, u32[]{:S(2)}) copy-start(bf16[2304,4]{0,1:T(4,128)(2,1)} %param.24) | copy-start | bytes 55300
  295.7 17.0 %all-to-all-start.1 = ((bf16[4,48,2304]{2,1,0:T(8,128)(2,1)}), bf16[4,48,2304]{2,1,0:T(8,128)(2,1)}, u32[]{:S(2)}, u32[]{:S(2)}) async-start(bf16[4,48,2304]{2,1,0:T(8,128)(2,1)} %bitcast.119), calls=%async_computation.1 | async-start | bytes 1769472 | tf_op jit(solution)/shard_map/all_to_all | solution.py:294
  322.2 1.5 copy-start.3
Sparse Core Ops, SparseCore 0:
  9.6 40.1 all-gather.1

commit v2 on v0

--- a/solution.py
+++ b/solution.py
@@ -92,8 +92,8 @@
     q_ref = refs[0]
     sources = refs[1:1 + 3 * count]
     acc_ref, top_ref, total_ref = refs[1 + 3 * count:]
-    width = q_ref.shape[1] // 2
-    for head in range(2):
+    width = HD
+    for head in range(q_ref.shape[1] // HD):
         cols = slice(head * width, (head + 1) * width)
         query = q_ref[:, cols]
         scores = []
@@ -123,8 +123,9 @@
 
 def attend(query_rows, sources):
     rows, features = query_rows.shape
-    pairs = features // (2 * HD)
-    block = 2 * HD
+    group = 4 if (features // HD) % 4 == 0 else 2
+    pairs = features // (group * HD)
+    block = group * HD
     operands = [query_rows]
     specs = [pl.BlockSpec((rows, block), lambda h: (0, h))]
     for table, key_offset, value_offset, allowed in sources:
@@ -214,7 +215,7 @@
     new_kv = tree_qkv[:, features:]
     reached = closure(parents)
     grouped_kv = new_kv.reshape(REQ_DEV, TREE, 2 * features)
-    blocks = features // (2 * HD)
+    blocks = features // ((4 if (features // HD) % 4 == 0 else 2) * HD)
     private_slots = jnp.arange(private_kv.shape[1], dtype=jnp.int32)
     private_ok = jnp.broadcast_to(private_slots[None, :] < priv_len[0], (row_count, private_kv.shape[1]))
     local_acc, local_top, local_total = attend(

time: 307 us -> 302 us (0.984)
  Pallas kernels: 36.1 us -> 28.6 us
  waiting for transfers between devices: 58.4 us -> 61.9 us
    pallas_call x2, Pallas kernels: 36.1 us -> 28.6 us  [attend(): pl.pallas_call(functools.partial(attend_kernel, count=len(sources), scale...]
    all_gather x1, waiting for transfers between devices: 13.8 us -> 17.2 us  [local(): shard_rows = lax.all_gather(prompt_kv, 'expert', axis=1, tiled=True)]
  transfers between devices with their start and end apart: 31 -> 31, of which waited for: 16 -> 16; matrix products, arithmetic and copies ran while one was open for 34% -> 35% of each run, Pallas kernels for 6% -> 5%
where the time goes in v2:
time: 302 us; the launch traced here: 300 us
  matrix products  90.9 us (30%)
  waiting for transfers between devices  61.9 us (20%)
  local copies, waits for them, and re-layouts  40.1 us (13%)
  starting transfers between devices  36.9 us (12%)
  Pallas kernels  28.6 us (9%)
  other arithmetic  25.6 us (8%)
  between operations  16.4 us (5%)
    dot_general x8, matrix products, local(): jnp.dot(hidden_units, down_rows, preferred_element_type=jnp.float32)  44.8 us
    dot_general x8, matrix products, local(): gate_act = jnp.dot(pooled, gate_cols, preferred_element_type=jnp.float32)  31.2 us
    pallas_call x2, Pallas kernels, attend(): pl.pallas_call(functools.partial(attend_kernel, count=len(sources), scale...  28.6 us
    ppermute x14, waiting for transfers between devices, ring_gather(): piece = lax.ppermute(piece, 'dp', pairs)  17.8 us
    all_gather x1, waiting for transfers between devices, local(): shard_rows = lax.all_gather(prompt_kv, 'expert', axis=1, tiled=True)  17.2 us
    unnamed x42, local copies, waits for them, and re-layouts  15.7 us
    convert_element_type x6, other arithmetic, ring_reduce(): moving = (received + blocks[index].astype(jnp.float32)).astype(jnp.bfloat16)  15.2 us
    ppermute x14, starting transfers between devices, ring_gather(): piece = lax.ppermute(piece, 'dp', pairs)  14.2 us
  transfers between devices with their start and end apart: 31, of which 16 were waited for; matrix products, arithmetic and copies ran while one was open for 35% of the time, Pallas kernels for 5%

profile of v2, /device:TPU:0, one launch (start us, length us, event | category | flops | bytes accessed | tf_op | source)
XLA Modules:
  0.0 300.3 jit_solution(7139063973556592877)
XLA Ops:
  7.9 1.9 slice.87.refs_0_
  17.2 15.3 %shard_map.152 = (f32[64,2304]{1,0:T(8,128)}, f32[64,2304]{1,0:T(8,128)}, f32[64,2304]{1,0:T(8,128)}) custom-call(bf16[64,2304]{1,0:T(8,128)(2,1)} %slice.87.refs_0_, bf16[512,4608]{1,0:T(8,128)(2,1)} %bitcast.165, bf16[512,4608]{1,0:T(8,128)(2,1)} %bitcast.166, f32[64,512]{1,0:T(8,128)} %broadcast_in_dim.42.refs_3_, bf16[64,6912]{1,0:T(8,128)(2,1)} %refs_5_.1, ...), custom_call_target="tpu_custom_call" | custom-call | tf_op jit(solution)/shard_map/pallas_call | solution.py:141
  32.6 17.2 %all-gather.2.cloned.1.call-done = bf16[1,512,4608]{2,1,0:T(8,128)(2,1)} async-done(((bf16[1,128,4608]{2,1,0:T(8,128)(2,1)}), bf16[1,512,4608]{2,1,0:T(8,128)(2,1)}) %all-gather.2.cloned.1.call-update) | async-done | bytes 4718608 | tf_op jit(solution)/shard_map/all_gather | solution.py:228
  50.4 13.3 %shard_map.153 = (f32[64,2304]{1,0:T(8,128)}, f32[64,2304]{1,0:T(8,128)}, f32[64,2304]{1,0:T(8,128)}) custom-call(bf16[64,2304]{1,0:T(8,128)(2,1)} %slice.87.refs_0_, bf16[512,4608]{1,0:T(8,128)(2,1)} %bitcast.167, bf16[512,4608]{1,0:T(8,128)(2,1)} %bitcast.168, f32[64,512]{1,0:T(8,128)} %broadcast_in_dim.47.refs_3_), custom_call_target="tpu_custom_call" | custom-call | tf_op jit(solution)/shard_map/pallas_call | solution.py:141
  63.7 7.3 %multiply_reduce_fusion = (f32[64]{0:T(128)S(1)}, f32[64,2304]{1,0:T(8,128)S(1)}) fusion(bf16[2304,2304]{1,0:T(8,128)(2,1)} %param.22, f32[64,2304]{1,0:T(8,128)} %get-tuple-element.13, f32[64,2304]{1,0:T(8,128)} %get-tuple-element.12, f32[64,2304]{1,0:T(8,128)} %get-tuple-element.11, f32[64,2304]{1,0:T(8,128)} %get-tuple-element.10, ...), kind=kOutput, calls=%fused_computation.109 | convolution fusion | flops 681983936 | bytes 15040768 | tf_op jit(solution)/shard_map/dot_general | solution.py:241
  72.7 1.1 broadcast_in_dim.51
  73.8 2.7 reshape.316
  76.5 2.4 convolution_convert_fusion.1
  78.9 4.2 %all-to-all-start = ((bf16[4,48,2304]{2,1,0:T(8,128)(2,1)}), bf16[4,48,2304]{2,1,0:T(8,128)(2,1)}, u32[]{:S(2)}, u32[]{:S(2)}) async-start(bf16[4,48,2304]{2,1,0:T(8,128)(2,1)} %bitcast.170), calls=%async_computation | async-start | bytes 1769472 | tf_op jit(solution)/shard_map/all_to_all | solution.py:272
  83.3 12.5 %all-to-all-done = bf16[4,48,2304]{2,1,0:T(8,128)(2,1)} async-done(((bf16[4,48,2304]{2,1,0:T(8,128)(2,1)}), bf16[4,48,2304]{2,1,0:T(8,128)(2,1)}, u32[]{:S(2)}, u32[]{:S(2)}) %all-to-all-start) | async-done | bytes 884768 | tf_op jit(solution)/shard_map/all_to_all | solution.py:272
  95.9 1.2 fusion.142
  97.1 1.5 collective-permute-start
  98.6 2.2 fusion
  101.4 3.9 %fusion.27 = f32[192,720]{1,0:T(8,128)} fusion(bf16[96,2304]{1,0:T(8,128)(2,1)S(1)} %bitcast.172, bf16[96,2304]{1,0:T(8,128)(2,1)S(1)} %bitcast.175, bf16[1,2,2304,720]{2,3,1,0:T(8,128)(2,1)} %param.26), kind=kOutput, calls=%fused_computation.39 | convolution fusion | flops 638779392 | bytes 4755456 | tf_op jit(solution)/shard_map/dot_general | solution.py:281
  105.3 3.4 %collective-permute-done = bf16[96,2304]{1,0:T(8,128)(2,1)S(1)} collective-permute-done((bf16[96,2304]{1,0:T(8,128)(2,1)S(1)}, bf16[96,2304]{1,0:T(8,128)(2,1)S(1)}, u32[]{:S(2)}, u32[]{:S(2)}) %collective-permute-start) | collective-permute-done | bytes 442400 | tf_op jit(solution)/shard_map/ppermute | solution.py:180
  108.8 3.4 %collective-permute-done.1 = bf16[96,2304]{1,0:T(8,128)(2,1)S(1)} collective-permute-done((bf16[96,2304]{1,0:T(8,128)(2,1)S(1)}, bf16[96,2304]{1,0:T(8,128)(2,1)S(1)}, u32[]{:S(2)}, u32[]{:S(2)}) %collective-permute-start.1) | collective-permute-done | bytes 442400 | tf_op jit(solution)/shard_map/ppermute | solution.py:180
  113.9 3.9 %fusion.41 = f32[192,720]{1,0:T(8,128)} fusion(bf16[192,2304]{1,0:T(8,128)(2,1)S(1)} %constant_dynamic-update-slice_fusion, bf16[1,2,2304,720]{2,3,1,0:T(8,128)(2,1)} %param.26), kind=kOutput, calls=%fused_computation.53 | convolution fusion | flops 637009920 | bytes 4755456 | tf_op jit(solution)/shard_map/dot_general | solution.py:281
  117.8 5.6 %convolution_convert_fusion.9 = bf16[192,2304]{1,0:T(8,128)(2,1)} fusion(bf16[1,720,2304]{2,1,0:T(8,128)(2,1)S(1)} %copy-done, f32[192,720]{1,0:T(8,128)} %fusion.41, bf16[192,2304]{1,0:T(8,128)(2,1)} %copy-done.13, bf16[1,2,2304,720]{2,3,1,0:T(8,128)(2,1)} %param.26), kind=kOutput, calls=%fused_computation.11 | convolution fusion | flops 1275291648 | bytes 8994816 | tf_op jit(solution)/shard_map/dot_general | solution.py:284
  123.4 1.5 collective-permute-start.3
  125.4 2.1 fusion.141
  127.5 1.5 collective-permute-start.2
  129.5 7.2 %collective-permute-done.3 = bf16[96,2304]{1,0:T(8,128)(2,1)} collective-permute-done((bf16[96,2304]{1,0:T(8,128)(2,1)}, bf16[96,2304]{1,0:T(8,128)(2,1)}, u32[]{:S(2)}, u32[]{:S(2)}) %collective-permute-start.3) | collective-permute-done | bytes 442400 | tf_op jit(solution)/shard_map/ppermute | solution.py:180
  140.2 3.9 %fusion.39 = f32[192,720]{1,0:T(8,128)} fusion(bf16[192,2304]{1,0:T(8,128)(2,1)S(1)} %constant_dynamic-update-slice_fusion.2, bf16[1,2,2304,720]{2,3,1,0:T(8,128)(2,1)} %param.26), kind=kOutput, calls=%fused_computation.51 | convolution fusion | flops 637009920 | bytes 4755456 | tf_op jit(solution)/shard_map/dot_general | solution.py:281
  144.1 1.5 collective-permute-start.6
  146.1 5.6 %convolution_convert_fusion.8 = bf16[192,2304]{1,0:T(8,128)(2,1)} fusion(bf16[1,720,2304]{2,1,0:T(8,128)(2,1)S(1)} %copy-done, f32[192,720]{1,0:T(8,128)} %fusion.39, bf16[192,2304]{1,0:T(8,128)(2,1)} %copy-done.8, bf16[1,2,2304,720]{2,3,1,0:T(8,128)(2,1)} %param.26), kind=kOutput, calls=%fused_computation.10 | convolution fusion | flops 1275291648 | bytes 8994816 | tf_op jit(solution)/shard_map/dot_general | solution.py:284
  151.7 2.5 add_convert_fusion.13
  154.2 1.5 collective-permute-start.5
  157.3 1.0 constant_dynamic-update-slice_fusion.4
  159.3 3.9 %fusion.37 = f32[192,720]{1,0:T(8,128)} fusion(bf16[192,2304]{1,0:T(8,128)(2,1)S(1)} %constant_dynamic-update-slice_fusion.4, bf16[1,2,2304,720]{2,3,1,0:T(8,128)(2,1)} %param.26), kind=kOutput, calls=%fused_computation.49 | convolution fusion | flops 637009920 | bytes 4755456 | tf_op jit(solution)/shard_map/dot_general | solution.py:281
  163.2 1.5 collective-permute-start.9
  165.2 5.6 %convolution_convert_fusion.7 = bf16[192,2304]{1,0:T(8,128)(2,1)} fusion(bf16[1,720,2304]{2,1,0:T(8,128)(2,1)S(1)} %copy-done, f32[192,720]{1,0:T(8,128)} %fusion.37, bf16[192,2304]{1,0:T(8,128)(2,1)} %copy-done.9, bf16[1,2,2304,720]{2,3,1,0:T(8,128)(2,1)} %param.26), kind=kOutput, calls=%fused_computation.9 | convolution fusion | flops 1275291648 | bytes 8994816 | tf_op jit(solution)/shard_map/dot_general | solution.py:284
  170.8 2.5 add_convert_fusion.12
  173.4 1.5 collective-permute-start.8
  179.3 3.9 %fusion.35 = f32[192,720]{1,0:T(8,128)} fusion(bf16[192,2304]{1,0:T(8,128)(2,1)S(1)} %constant_dynamic-update-slice_fusion.6, bf16[1,2,2304,720]{2,3,1,0:T(8,128)(2,1)} %param.26), kind=kOutput, calls=%fused_computation.47 | convolution fusion | flops 637009920 | bytes 4755456 | tf_op jit(solution)/shard_map/dot_general | solution.py:281
  183.2 1.5 collective-permute-start.12
  185.2 5.6 %convolution_convert_fusion.6 = bf16[192,2304]{1,0:T(8,128)(2,1)} fusion(bf16[1,720,2304]{2,1,0:T(8,128)(2,1)S(1)} %copy-done, f32[192,720]{1,0:T(8,128)} %fusion.35, bf16[192,2304]{1,0:T(8,128)(2,1)} %copy-done.10, bf16[1,2,2304,720]{2,3,1,0:T(8,128)(2,1)} %param.26), kind=kOutput, calls=%fused_computation.8 | convolution fusion | flops 1275291648 | bytes 8994816 | tf_op jit(solution)/shard_map/dot_general | solution.py:284
  190.8 2.5 add_convert_fusion.11
  193.4 1.5 collective-permute-start.11
  199.2 3.9 %fusion.33 = f32[192,720]{1,0:T(8,128)} fusion(bf16[192,2304]{1,0:T(8,128)(2,1)S(1)} %constant_dynamic-update-slice_fusion.8, bf16[1,2,2304,720]{2,3,1,0:T(8,128)(2,1)} %param.26), kind=kOutput, calls=%fused_computation.45 | convolution fusion | flops 637009920 | bytes 4755456 | tf_op jit(solution)/shard_map/dot_general | solution.py:281
  203.1 1.2 collective-permute-start.15
  205.1 5.6 %convolution_convert_fusion.5 = bf16[192,2304]{1,0:T(8,128)(2,1)} fusion(bf16[1,720,2304]{2,1,0:T(8,128)(2,1)S(1)} %copy-done, f32[192,720]{1,0:T(8,128)} %fusion.33, bf16[192,2304]{1,0:T(8,128)(2,1)} %copy-done.11, bf16[1,2,2304,720]{2,3,1,0:T(8,128)(2,1)} %param.26), kind=kOutput, calls=%fused_computation.7 | convolution fusion | flops 1275291648 | bytes 8994816 | tf_op jit(solution)/shard_map/dot_general | solution.py:284
  210.8 2.5 add_convert_fusion.10
  213.3 1.2 collective-permute-start.14
  219.7 3.9 %fusion.31 = f32[192,720]{1,0:T(8,128)} fusion(bf16[192,2304]{1,0:T(8,128)(2,1)S(1)} %constant_dynamic-update-slice_fusion.10, bf16[1,2,2304,720]{2,3,1,0:T(8,128)(2,1)} %param.26), kind=kOutput, calls=%fused_computation.43 | convolution fusion | flops 637009920 | bytes 4755456 | tf_op jit(solution)/shard_map/dot_general | solution.py:281
  224.4 1.2 collective-permute-start.19
  225.6 5.6 %convolution_convert_fusion.4 = bf16[192,2304]{1,0:T(8,128)(2,1)} fusion(bf16[1,720,2304]{2,1,0:T(8,128)(2,1)S(1)} %copy-done, f32[192,720]{1,0:T(8,128)} %fusion.31, bf16[192,2304]{1,0:T(8,128)(2,1)} %copy-done.12, bf16[1,2,2304,720]{2,3,1,0:T(8,128)(2,1)} %param.26), kind=kOutput, calls=%fused_computation.6 | convolution fusion | flops 1275291648 | bytes 8994816 | tf_op jit(solution)/shard_map/dot_general | solution.py:284
  231.2 2.6 add_convert_fusion.9
  234.5 1.2 collective-permute-start.26
  237.1 1.0 constant_dynamic-update-slice_fusion.12
  239.1 3.9 %fusion.29 = f32[192,720]{1,0:T(8,128)} fusion(bf16[192,2304]{1,0:T(8,128)(2,1)S(1)} %constant_dynamic-update-slice_fusion.12, bf16[1,2,2304,720]{2,3,1,0:T(8,128)(2,1)} %param.26), kind=kOutput, calls=%fused_computation.41 | convolution fusion | flops 637009920 | bytes 4755456 | tf_op jit(solution)/shard_map/dot_general | solution.py:281
  243.0 5.6 %convolution_convert_fusion.3 = bf16[192,2304]{1,0:T(8,128)(2,1)} fusion(bf16[1,720,2304]{2,1,0:T(8,128)(2,1)S(1)} %copy-done, f32[192,720]{1,0:T(8,128)} %fusion.29, bf16[192,2304]{1,0:T(8,128)(2,1)} %copy-done.7, bf16[1,2,2304,720]{2,3,1,0:T(8,128)(2,1)} %param.26), kind=kOutput, calls=%fused_computation.5 | convolution fusion | flops 1275291648 | bytes 8994816 | tf_op jit(solution)/shard_map/dot_general | solution.py:284
  248.6 2.5 add_convert_fusion.8
  251.1 1.2 collective-permute-start.20
  253.1 5.6 %convolution_convert_fusion.2 = bf16[192,2304]{1,0:T(8,128)(2,1)} fusion(bf16[1,720,2304]{2,1,0:T(8,128)(2,1)S(1)} %copy-done, f32[192,720]{1,0:T(8,128)} %fusion.27, bf16[96,2304]{1,0:T(8,128)(2,1)} %bitcast.173, bf16[96,2304]{1,0:T(8,128)(2,1)} %bitcast.176, bf16[1,2,2304,720]{2,3,1,0:T(8,128)(2,1)} %param.26), kind=kOutput, calls=%fused_computation.4 | convolution fusion | flops 1277061120 | bytes 8994816 | tf_op jit(solution)/shard_map/dot_general | solution.py:284
  259.7 1.2 collective-permute-done.27
  260.9 1.6 add_convert_fusion.7
  263.5 4.2 %all-to-all-start.1 = ((bf16[4,48,2304]{2,1,0:T(8,128)(2,1)}), bf16[4,48,2304]{2,1,0:T(8,128)(2,1)}, u32[]{:S(2)}, u32[]{:S(2)}) async-start(bf16[4,48,2304]{2,1,0:T(8,128)(2,1)} %bitcast.169), calls=%async_computation.1 | async-start | bytes 1769472 | tf_op jit(solution)/shard_map/all_to_all | solution.py:290
  267.8 1.1 fusion.143
  269.0 11.5 %all-to-all-done.1 = bf16[4,48,2304]{2,1,0:T(8,128)(2,1)} async-done(((bf16[4,48,2304]{2,1,0:T(8,128)(2,1)}), bf16[4,48,2304]{2,1,0:T(8,128)(2,1)}, u32[]{:S(2)}, u32[]{:S(2)}) %all-to-all-start.1) | async-done | bytes 884768 | tf_op jit(solution)/shard_map/all_to_all | solution.py:290
  280.5 2.5 bitcast_convert_fusion
  283.0 4.0 %gather_fusion = f32[128,2304]{1,0:T(8,128)} fusion(f32[192,2304]{1,0:T(8,128)} %bitcast_convert_fusion, s32[1024]{0:T(1024)S(1)} %pad_clamp_fusion), kind=kCustom, calls=%fused_computation | custom fusion | bytes 2359808 | tf_op jit(solution)/shard_map/jit(_take)/gather | solution.py:298
  287.1 3.0 gather.7
  290.1 1.4 copy_select_fusion
  291.5 2.0 fusion.56
  (119 shorter events, 40.9 us)
Async XLA Ops:
  7.2 110.6 %copy-start = (bf16[1,720,2304]{2,1,0:T(8,128)(2,1)S(1)}, bf16[1,720,2304]{2,1,0:T(8,128)(2,1)}, u32[]{:S(2)}) copy-start(bf16[1,720,2304]{2,1,0:T(8,128)(2,1)} %param.27) | copy-start | bytes 9953284
  7.2 42.6 %all-gather.2.cloned.1.call-start = ((), (), s32[]{:S(2)}) async-start(), calls=%async_computation.2 | async-start | bytes 5898240 | tf_op jit(solution)/shard_map/all_gather | solution.py:228
  63.7 8.1 %copy-start.16 = (f32[2304]{0:T(1024)S(1)}, f32[2304]{0:T(1024)}, u32[]{:S(2)}) copy-start(f32[2304]{0:T(1024)} %param.23) | copy-start | bytes 27652
  71.0 0.8 copy-start.1
  71.0 12.3 %copy-start.15 = (s32[64,2]{0,1:T(2,128)S(1)}, s32[64,2]{0,1:T(2,128)}, u32[]{:S(2)}) copy-start(s32[64,2]{0,1:T(2,128)} %param.25) | copy-start | bytes 1540
  71.9 0.7 copy-start.2
  78.9 17.0 %all-to-all-start = ((bf16[4,48,2304]{2,1,0:T(8,128)(2,1)}), bf16[4,48,2304]{2,1,0:T(8,128)(2,1)}, u32[]{:S(2)}, u32[]{:S(2)}) async-start(bf16[4,48,2304]{2,1,0:T(8,128)(2,1)} %bitcast.170), calls=%async_computation | async-start | bytes 1769472 | tf_op jit(solution)/shard_map/all_to_all | solution.py:272
  97.1 8.2 %copy-start.3 = (bf16[2,48,2304]{2,1,0:T(8,128)(2,1)}, bf16[2,48,2304]{2,1,0:T(8,128)(2,1)S(1)}, u32[]{:S(2)}) copy-start(bf16[2,48,2304]{2,1,0:T(8,128)(2,1)S(1)} %get-tuple-element.30) | copy-start | bytes 1327108
  97.1 8.2 %copy-start.4 = (bf16[2,48,2304]{2,1,0:T(8,128)(2,1)}, bf16[2,48,2304]{2,1,0:T(8,128)(2,1)S(1)}, u32[]{:S(2)}) copy-start(bf16[2,48,2304]{2,1,0:T(8,128)(2,1)S(1)} %get-tuple-element.31) | copy-start | bytes 1327108
  97.1 11.7 %collective-permute-start = (bf16[96,2304]{1,0:T(8,128)(2,1)S(1)}, bf16[96,2304]{1,0:T(8,128)(2,1)S(1)}, u32[]{:S(2)}, u32[]{:S(2)}) collective-permute-start(bf16[96,2304]{1,0:T(8,128)(2,1)S(1)} %bitcast.174), channel_id=1, source_target_pairs={{0,4},{4,12},{12,20},{20,28},{28,24},{24,16},{16,8},{8,0},{1,5},{5... | collective-permute-start | bytes 1327112 | tf_op jit(solution)/shard_map/ppermute | solution.py:180
  100.8 11.3 %collective-permute-start.1 = (bf16[96,2304]{1,0:T(8,128)(2,1)S(1)}, bf16[96,2304]{1,0:T(8,128)(2,1)S(1)}, u32[]{:S(2)}, u32[]{:S(2)}) collective-permute-start(bf16[96,2304]{1,0:T(8,128)(2,1)S(1)} %bitcast.171), channel_id=1, source_target_pairs={{0,8},{4,0},{12,4},{20,12},{28,20},{24,28},{16,24},{8,16},{1,9},{5... | collective-permute-start | bytes 1327112 | tf_op jit(solution)/shard_map/ppermute | solution.py:180
  108.8 3.4 %copy-start.5 = (bf16[96,2304]{1,0:T(8,128)(2,1)}, bf16[96,2304]{1,0:T(8,128)(2,1)S(1)}, u32[]{:S(2)}) copy-start(bf16[96,2304]{1,0:T(8,128)(2,1)S(1)} %collective-permute-done) | copy-start | bytes 1327108
  112.2 0.8 copy-start.6
  112.9 0.9 copy-start.13
  123.4 13.4 %collective-permute-start.3 = (bf16[96,2304]{1,0:T(8,128)(2,1)}, bf16[96,2304]{1,0:T(8,128)(2,1)}, u32[]{:S(2)}, u32[]{:S(2)}) collective-permute-start(bf16[96,2304]{1,0:T(8,128)(2,1)} %copy-done.5), channel_id=1, source_target_pairs={{0,4},{4,12},{12,20},{20,28},{28,24},{24,16},{16,8},{8,0},{1,5},{5... | collective-permute-start | bytes 1327112 | tf_op jit(solution)/shard_map/ppermute | solution.py:180
  124.9 13.4 %collective-permute-start.4 = (bf16[96,2304]{1,0:T(8,128)(2,1)}, bf16[96,2304]{1,0:T(8,128)(2,1)}, u32[]{:S(2)}, u32[]{:S(2)}) collective-permute-start(bf16[96,2304]{1,0:T(8,128)(2,1)} %copy-done.6), channel_id=1, source_target_pairs={{0,8},{4,0},{12,4},{20,12},{28,20},{24,28},{16,24},{8,16},{1,9},{5... | collective-permute-start | bytes 1327112 | tf_op jit(solution)/shard_map/ppermute | solution.py:180
  127.5 24.2 %collective-permute-start.2 = (bf16[96,2304]{1,0:T(8,128)(2,1)}, bf16[96,2304]{1,0:T(8,128)(2,1)}, u32[]{:S(2)}, u32[]{:S(2)}) collective-permute-start(bf16[96,2304]{1,0:T(8,128)(2,1)} %get-tuple-element.28), channel_id=1, source_target_pairs={{0,4},{4,12},{12,20},{20,28},{28,24},{24,16},{16,8},{8,0},{1,5},{5... | collective-permute-start | bytes 1327112 | tf_op jit(solution)/shard_map/ppermute | solution.py:190
  129.0 22.7 %collective-permute-start.21 = (bf16[96,2304]{1,0:T(8,128)(2,1)}, bf16[96,2304]{1,0:T(8,128)(2,1)}, u32[]{:S(2)}, u32[]{:S(2)}) collective-permute-start(bf16[96,2304]{1,0:T(8,128)(2,1)} %get-tuple-element.29), channel_id=1, source_target_pairs={{0,8},{4,0},{12,4},{20,12},{28,20},{24,28},{16,24},{8,16},{1,9},{5... | collective-permute-start | bytes 1327112 | tf_op jit(solution)/shard_map/ppermute | solution.py:190
  139.3 0.9 copy-start.8
  144.1 12.2 %collective-permute-start.6 = (bf16[96,2304]{1,0:T(8,128)(2,1)}, bf16[96,2304]{1,0:T(8,128)(2,1)}, u32[]{:S(2)}, u32[]{:S(2)}) collective-permute-start(bf16[96,2304]{1,0:T(8,128)(2,1)} %collective-permute-done.3), channel_id=1, source_target_pairs={{0,4},{4,12},{12,20},{20,28},{28,24},{24,16},{16,8},{8,0},{1,5},{5... | collective-permute-start | bytes 1327112 | tf_op jit(solution)/shard_map/ppermute | solution.py:180
  145.6 11.7 %collective-permute-start.7 = (bf16[96,2304]{1,0:T(8,128)(2,1)}, bf16[96,2304]{1,0:T(8,128)(2,1)}, u32[]{:S(2)}, u32[]{:S(2)}) collective-permute-start(bf16[96,2304]{1,0:T(8,128)(2,1)} %collective-permute-done.4), channel_id=1, source_target_pairs={{0,8},{4,0},{12,4},{20,12},{28,20},{24,28},{16,24},{8,16},{1,9},{5... | collective-permute-start | bytes 1327112 | tf_op jit(solution)/shard_map/ppermute | solution.py:180
  154.2 16.6 %collective-permute-start.5 = (bf16[96,2304]{1,0:T(8,128)(2,1)}, bf16[96,2304]{1,0:T(8,128)(2,1)}, u32[]{:S(2)}, u32[]{:S(2)}) collective-permute-start(bf16[96,2304]{1,0:T(8,128)(2,1)} %get-tuple-element.26), channel_id=1, source_target_pairs={{0,4},{4,12},{12,20},{20,28},{28,24},{24,16},{16,8},{8,0},{1,5},{5... | collective-permute-start | bytes 1327112 | tf_op jit(solution)/shard_map/ppermute | solution.py:190
  155.7 15.1 %collective-permute-start.22 = (bf16[96,2304]{1,0:T(8,128)(2,1)}, bf16[96,2304]{1,0:T(8,128)(2,1)}, u32[]{:S(2)}, u32[]{:S(2)}) collective-permute-start(bf16[96,2304]{1,0:T(8,128)(2,1)} %get-tuple-element.27), channel_id=1, source_target_pairs={{0,8},{4,0},{12,4},{20,12},{28,20},{24,28},{16,24},{8,16},{1,9},{5... | collective-permute-start | bytes 1327112 | tf_op jit(solution)/shard_map/ppermute | solution.py:190
  158.4 0.9 copy-start.9
  163.2 12.3 %collective-permute-start.9 = (bf16[96,2304]{1,0:T(8,128)(2,1)}, bf16[96,2304]{1,0:T(8,128)(2,1)}, u32[]{:S(2)}, u32[]{:S(2)}) collective-permute-start(bf16[96,2304]{1,0:T(8,128)(2,1)} %collective-permute-done.6), channel_id=1, source_target_pairs={{0,4},{4,12},{12,20},{20,28},{28,24},{24,16},{16,8},{8,0},{1,5},{5... | collective-permute-start | bytes 1327112 | tf_op jit(solution)/shard_map/ppermute | solution.py:180
  164.7 12.7 %collective-permute-start.10 = (bf16[96,2304]{1,0:T(8,128)(2,1)}, bf16[96,2304]{1,0:T(8,128)(2,1)}, u32[]{:S(2)}, u32[]{:S(2)}) collective-permute-start(bf16[96,2304]{1,0:T(8,128)(2,1)} %collective-permute-done.7), channel_id=1, source_target_pairs={{0,8},{4,0},{12,4},{20,12},{28,20},{24,28},{16,24},{8,16},{1,9},{5... | collective-permute-start | bytes 1327112 | tf_op jit(solution)/shard_map/ppermute | solution.py:180
  173.4 17.5 %collective-permute-start.8 = (bf16[96,2304]{1,0:T(8,128)(2,1)}, bf16[96,2304]{1,0:T(8,128)(2,1)}, u32[]{:S(2)}, u32[]{:S(2)}) collective-permute-start(bf16[96,2304]{1,0:T(8,128)(2,1)} %get-tuple-element.24), channel_id=1, source_target_pairs={{0,4},{4,12},{12,20},{20,28},{28,24},{24,16},{16,8},{8,0},{1,5},{5... | collective-permute-start | bytes 1327112 | tf_op jit(solution)/shard_map/ppermute | solution.py:190
  174.9 16.0 %collective-permute-start.23 = (bf16[96,2304]{1,0:T(8,128)(2,1)}, bf16[96,2304]{1,0:T(8,128)(2,1)}, u32[]{:S(2)}, u32[]{:S(2)}) collective-permute-start(bf16[96,2304]{1,0:T(8,128)(2,1)} %get-tuple-element.25), channel_id=1, source_target_pairs={{0,8},{4,0},{12,4},{20,12},{28,20},{24,28},{16,24},{8,16},{1,9},{5... | collective-permute-start | bytes 1327112 | tf_op jit(solution)/shard_map/ppermute | solution.py:190
  178.4 0.9 copy-start.10
  183.2 12.3 %collective-permute-start.12 = (bf16[96,2304]{1,0:T(8,128)(2,1)}, bf16[96,2304]{1,0:T(8,128)(2,1)}, u32[]{:S(2)}, u32[]{:S(2)}) collective-permute-start(bf16[96,2304]{1,0:T(8,128)(2,1)} %collective-permute-done.9), channel_id=1, source_target_pairs={{0,4},{4,12},{12,20},{20,28},{28,24},{24,16},{16,8},{8,0},{1,5},{5... | collective-permute-start | bytes 1327112 | tf_op jit(solution)/shard_map/ppermute | solution.py:180
  184.7 12.6 %collective-permute-start.13 = (bf16[96,2304]{1,0:T(8,128)(2,1)}, bf16[96,2304]{1,0:T(8,128)(2,1)}, u32[]{:S(2)}, u32[]{:S(2)}) collective-permute-start(bf16[96,2304]{1,0:T(8,128)(2,1)} %collective-permute-done.10), channel_id=1, source_target_pairs={{0,8},{4,0},{12,4},{20,12},{28,20},{24,28},{16,24},{8,16},{1,9},{5... | collective-permute-start | bytes 1327112 | tf_op jit(solution)/shard_map/ppermute | solution.py:180
  193.4 17.4 %collective-permute-start.11 = (bf16[96,2304]{1,0:T(8,128)(2,1)}, bf16[96,2304]{1,0:T(8,128)(2,1)}, u32[]{:S(2)}, u32[]{:S(2)}) collective-permute-start(bf16[96,2304]{1,0:T(8,128)(2,1)} %get-tuple-element.22), channel_id=1, source_target_pairs={{0,4},{4,12},{12,20},{20,28},{28,24},{24,16},{16,8},{8,0},{1,5},{5... | collective-permute-start | bytes 1327112 | tf_op jit(solution)/shard_map/ppermute | solution.py:190
  194.8 15.9 %collective-permute-start.24 = (bf16[96,2304]{1,0:T(8,128)(2,1)}, bf16[96,2304]{1,0:T(8,128)(2,1)}, u32[]{:S(2)}, u32[]{:S(2)}) collective-permute-start(bf16[96,2304]{1,0:T(8,128)(2,1)} %get-tuple-element.23), channel_id=1, source_target_pairs={{0,8},{4,0},{12,4},{20,12},{28,20},{24,28},{16,24},{8,16},{1,9},{5... | collective-permute-start | bytes 1327112 | tf_op jit(solution)/shard_map/ppermute | solution.py:190
  198.3 0.9 copy-start.11
  203.1 13.1 %collective-permute-start.15 = (bf16[96,2304]{1,0:T(8,128)(2,1)}, bf16[96,2304]{1,0:T(8,128)(2,1)}, u32[]{:S(2)}, u32[]{:S(2)}) collective-permute-start(bf16[96,2304]{1,0:T(8,128)(2,1)} %collective-permute-done.12), channel_id=1, source_target_pairs={{0,4},{4,12},{12,20},{20,28},{28,24},{24,16},{16,8},{8,0},{1,5},{5... | collective-permute-start | bytes 1327112 | tf_op jit(solution)/shard_map/ppermute | solution.py:180
  204.4 13.3 %collective-permute-start.16 = (bf16[96,2304]{1,0:T(8,128)(2,1)}, bf16[96,2304]{1,0:T(8,128)(2,1)}, u32[]{:S(2)}, u32[]{:S(2)}) collective-permute-start(bf16[96,2304]{1,0:T(8,128)(2,1)} %collective-permute-done.13), channel_id=1, source_target_pairs={{0,8},{4,0},{12,4},{20,12},{28,20},{24,28},{16,24},{8,16},{1,9},{5... | collective-permute-start | bytes 1327112 | tf_op jit(solution)/shard_map/ppermute | solution.py:180
  213.3 17.9 %collective-permute-start.14 = (bf16[96,2304]{1,0:T(8,128)(2,1)}, bf16[96,2304]{1,0:T(8,128)(2,1)}, u32[]{:S(2)}, u32[]{:S(2)}) collective-permute-start(bf16[96,2304]{1,0:T(8,128)(2,1)} %get-tuple-element.20), channel_id=1, source_target_pairs={{0,4},{4,12},{12,20},{20,28},{28,24},{24,16},{16,8},{8,0},{1,5},{5... | collective-permute-start | bytes 1327112 | tf_op jit(solution)/shard_map/ppermute | solution.py:190
  214.5 16.7 %collective-permute-start.25 = (bf16[96,2304]{1,0:T(8,128)(2,1)}, bf16[96,2304]{1,0:T(8,128)(2,1)}, u32[]{:S(2)}, u32[]{:S(2)}) collective-permute-start(bf16[96,2304]{1,0:T(8,128)(2,1)} %get-tuple-element.21), channel_id=1, source_target_pairs={{0,8},{4,0},{12,4},{20,12},{28,20},{24,28},{16,24},{8,16},{1,9},{5... | collective-permute-start | bytes 1327112 | tf_op jit(solution)/shard_map/ppermute | solution.py:190
  218.8 0.9 copy-start.12
  223.6 12.5 %collective-permute-start.18 = (bf16[96,2304]{1,0:T(8,128)(2,1)}, bf16[96,2304]{1,0:T(8,128)(2,1)}, u32[]{:S(2)}, u32[]{:S(2)}) collective-permute-start(bf16[96,2304]{1,0:T(8,128)(2,1)} %collective-permute-done.15), channel_id=1, source_target_pairs={{0,4},{4,12},{12,20},{20,28},{28,24},{24,16},{16,8},{8,0},{1,5},{5... | collective-permute-start | bytes 1327112 | tf_op jit(solution)/shard_map/ppermute | solution.py:180
  224.4 12.8 %collective-permute-start.19 = (bf16[96,2304]{1,0:T(8,128)(2,1)}, bf16[96,2304]{1,0:T(8,128)(2,1)}, u32[]{:S(2)}, u32[]{:S(2)}) collective-permute-start(bf16[96,2304]{1,0:T(8,128)(2,1)} %collective-permute-done.16), channel_id=1, source_target_pairs={{0,8},{4,0},{12,4},{20,12},{28,20},{24,28},{16,24},{8,16},{1,9},{5... | collective-permute-start | bytes 1327112 | tf_op jit(solution)/shard_map/ppermute | solution.py:180
  233.8 14.8 %collective-permute-start.17 = (bf16[96,2304]{1,0:T(8,128)(2,1)}, bf16[96,2304]{1,0:T(8,128)(2,1)}, u32[]{:S(2)}, u32[]{:S(2)}) collective-permute-start(bf16[96,2304]{1,0:T(8,128)(2,1)} %get-tuple-element.18), channel_id=1, source_target_pairs={{0,4},{4,12},{12,20},{20,28},{28,24},{24,16},{16,8},{8,0},{1,5},{5... | collective-permute-start | bytes 1327112 | tf_op jit(solution)/shard_map/ppermute | solution.py:190
  234.5 14.0 %collective-permute-start.26 = (bf16[96,2304]{1,0:T(8,128)(2,1)}, bf16[96,2304]{1,0:T(8,128)(2,1)}, u32[]{:S(2)}, u32[]{:S(2)}) collective-permute-start(bf16[96,2304]{1,0:T(8,128)(2,1)} %get-tuple-element.19), channel_id=1, source_target_pairs={{0,8},{4,0},{12,4},{20,12},{28,20},{24,28},{16,24},{8,16},{1,9},{5... | collective-permute-start | bytes 1327112 | tf_op jit(solution)/shard_map/ppermute | solution.py:190
  238.2 0.9 copy-start.7
  251.1 8.6 %collective-permute-start.20 = (bf16[96,2304]{1,0:T(8,128)(2,1)}, bf16[96,2304]{1,0:T(8,128)(2,1)}, u32[]{:S(2)}, u32[]{:S(2)}) collective-permute-start(bf16[96,2304]{1,0:T(8,128)(2,1)} %get-tuple-element.16), channel_id=1, source_target_pairs={{0,4},{4,12},{12,20},{20,28},{28,24},{24,16},{16,8},{8,0},{1,5},{5... | collective-permute-start | bytes 1327112 | tf_op jit(solution)/shard_map/ppermute | solution.py:192
  252.3 8.6 %collective-permute-start.27 = (bf16[96,2304]{1,0:T(8,128)(2,1)}, bf16[96,2304]{1,0:T(8,128)(2,1)}, u32[]{:S(2)}, u32[]{:S(2)}) collective-permute-start(bf16[96,2304]{1,0:T(8,128)(2,1)} %get-tuple-element.17), channel_id=1, source_target_pairs={{0,8},{4,0},{12,4},{20,12},{28,20},{24,28},{16,24},{8,16},{1,9},{5... | collective-permute-start | bytes 1327112 | tf_op jit(solution)/shard_map/ppermute | solution.py:192
  258.7 9.0 %copy-start.14 = (bf16[2304,4]{0,1:T(4,128)(2,1)S(1)}, bf16[2304,4]{0,1:T(4,128)(2,1)}, u32[]{:S(2)}) copy-start(bf16[2304,4]{0,1:T(4,128)(2,1)} %param.24) | copy-start | bytes 55300
  263.5 17.0 %all-to-all-start.1 = ((bf16[4,48,2304]{2,1,0:T(8,128)(2,1)}), bf16[4,48,2304]{2,1,0:T(8,128)(2,1)}, u32[]{:S(2)}, u32[]{:S(2)}) async-start(bf16[4,48,2304]{2,1,0:T(8,128)(2,1)} %bitcast.169), calls=%async_computation.1 | async-start | bytes 1769472 | tf_op jit(solution)/shard_map/all_to_all | solution.py:290
Sparse Core Ops, SparseCore 0:
  9.5 40.1 all-gather.1

commit v3 on v2

--- a/solution.py
+++ b/solution.py
@@ -5,6 +5,7 @@
 import jax.numpy as jnp
 from jax import lax
 from jax.experimental import pallas as pl
+from jax.experimental.pallas import tpu as pltpu
 from jax.sharding import PartitionSpec as P
 
 H = 36
@@ -147,6 +148,55 @@
     )(*operands)
 
 
+def expert_kernel(first_ref, second_ref, gate_ref, up_ref, down_ref, first_out, second_out, gate_acc, up_acc):
+    step = pl.program_id(0)
+
+    @pl.when(step == 0)
+    def _():
+        gate_acc[...] = jnp.zeros_like(gate_acc)
+        up_acc[...] = jnp.zeros_like(up_acc)
+
+    rows = jnp.concatenate([first_ref[...], second_ref[...]], axis=0)
+    gate_acc[...] += jnp.dot(rows, gate_ref[...], preferred_element_type=jnp.float32)
+    up_acc[...] += jnp.dot(rows, up_ref[...], preferred_element_type=jnp.float32)
+
+    @pl.when(step == pl.num_programs(0) - 1)
+    def _():
+        gate_act = gate_acc[...]
+        hidden_units = (gate_act / (1.0 + jnp.exp(-gate_act)) * up_acc[...]).astype(jnp.bfloat16)
+        partial = jnp.dot(hidden_units, down_ref[...], preferred_element_type=jnp.float32).astype(jnp.bfloat16)
+        half = first_out.shape[0]
+        first_out[...] = partial[:half]
+        second_out[...] = partial[half:]
+
+
+def expert_block(first, second, w_gate_up, w_down):
+    half, features = first.shape
+    units = w_gate_up.shape[3]
+    chunk = features // 3 if features % 384 == 0 else features
+    steps = features // chunk
+    row_spec = pl.BlockSpec((half, chunk), lambda k: (0, k))
+    out_spec = pl.BlockSpec((half, features), lambda k: (0, 0))
+    shape = jax.ShapeDtypeStruct((half, features), jnp.bfloat16)
+    return pl.pallas_call(
+        expert_kernel,
+        grid=(steps,),
+        in_specs=[
+            row_spec,
+            row_spec,
+            pl.BlockSpec((None, None, chunk, units), lambda k: (0, 0, k, 0)),
+            pl.BlockSpec((None, None, chunk, units), lambda k: (0, 1, k, 0)),
+            pl.BlockSpec((None, units, features), lambda k: (0, 0, 0)),
+        ],
+        out_specs=(out_spec, out_spec),
+        out_shape=(shape, shape),
+        scratch_shapes=[
+            pltpu.VMEM((2 * half, units), jnp.float32),
+            pltpu.VMEM((2 * half, units), jnp.float32),
+        ],
+    )(first, second, w_gate_up, w_gate_up, w_down)
+
+
 def dp_ring(mesh):
     count = mesh.shape["dp"]
     try:
@@ -277,13 +327,9 @@
     forward_out = []
     backward_out = []
     for index in range(len(ring)):
-        pooled = jnp.concatenate([forward[index], backward[index]], axis=0)
-        gate_act = jnp.dot(pooled, gate_cols, preferred_element_type=jnp.float32)
-        upper = jnp.dot(pooled, up_cols, preferred_element_type=jnp.float32)
-        hidden_units = (jax.nn.silu(gate_act) * upper).astype(jnp.bfloat16)
-        partial = jnp.dot(hidden_units, down_rows, preferred_element_type=jnp.float32).astype(jnp.bfloat16)
-        forward_out.append(partial[:half])
-        backward_out.append(partial[half:])
+        first_part, second_part = expert_block(forward[index], backward[index], w_gate_up, w_down)
+        forward_out.append(first_part)
+        backward_out.append(second_part)
     summed_rows = jnp.concatenate(
         [ring_reduce(forward_out, ring, 1), ring_reduce(backward_out, ring, -1)], axis=0
     )

time: 302 us -> 326 us (1.079)
  matrix products: 90.9 us -> 11.4 us
  Pallas kernels: 28.6 us -> 91.9 us
  waiting for transfers between devices: 61.9 us -> 121 us
  local copies, waits for them, and re-layouts: 40.1 us -> 28 us
  other arithmetic: 25.6 us -> 16.7 us
    dot_general x16 -> x0, matrix products: 76 us -> none  [the longest x8 44.8 us: local(): jnp.dot(hidden_units, down_rows, preferred_element_type=jnp.float32)]
    pallas_call x0 -> x8, Pallas kernels: none -> 63.3 us  [expert_block(): pl.pallas_call(expert_kernel, grid=(steps,), in_specs=[row_spec, row_spec...]
    ppermute x14, waiting for transfers between devices: 17.8 us -> 78.9 us  [ring_gather(): piece = lax.ppermute(piece, 'dp', pairs)]
    all_to_all x1, waiting for transfers between devices: 12.5 us -> 1.28 us  [local(): lax.all_to_all(outgoing, 'expert', split_axis=0, concat_axis=0, tiled=True)]
    concatenate x7 -> x0, local copies, waits for them, and re-layouts: 6.29 us -> none  [local(): pooled = jnp.concatenate([forward[index], backward[index]], axis=0)]
    ppermute x14, waiting for transfers between devices: 2.2 us -> 6.69 us  [ring_reduce(): received = lax.ppermute(moving, 'dp', pairs).astype(jnp.float32)]
    unnamed x42 -> x58, local copies, waits for them, and re-layouts: 15.7 us -> 19.8 us
    all_gather x1, waiting for transfers between devices: 17.2 us -> 20.8 us  [local(): shard_rows = lax.all_gather(prompt_kv, 'expert', axis=1, tiled=True)]
  transfers between devices with their start and end apart: 31 -> 31, of which waited for: 16 -> 14; matrix products, arithmetic and copies ran while one was open for 35% -> 9% of each run, Pallas kernels for 5% -> 22%
where the time goes in v3:
time: 326 us; the launch traced here: 324 us
  waiting for transfers between devices  121 us (37%)
  Pallas kernels  91.9 us (28%)
  starting transfers between devices  38.8 us (12%)
  local copies, waits for them, and re-layouts  28 us (9%)
  other arithmetic  16.7 us (5%)
  between operations  16.4 us (5%)
  matrix products  11.4 us (3%)
    ppermute x14, waiting for transfers between devices, ring_gather(): piece = lax.ppermute(piece, 'dp', pairs)  78.9 us
    pallas_call x8, Pallas kernels, expert_block(): pl.pallas_call(expert_kernel, grid=(steps,), in_specs=[row_spec, row_spec...  63.3 us
    pallas_call x2, Pallas kernels, attend(): pl.pallas_call(functools.partial(attend_kernel, count=len(sources), scale...  28.6 us
    all_gather x1, waiting for transfers between devices, local(): shard_rows = lax.all_gather(prompt_kv, 'expert', axis=1, tiled=True)  20.8 us
    unnamed x58, local copies, waits for them, and re-layouts  19.8 us
    ppermute x14, starting transfers between devices, ring_reduce(): received = lax.ppermute(moving, 'dp', pairs).astype(jnp.float32)  15 us
    ppermute x14, starting transfers between devices, ring_gather(): piece = lax.ppermute(piece, 'dp', pairs)  14.2 us
    convert_element_type x12, other arithmetic, ring_reduce(): moving = (received + blocks[index].astype(jnp.float32)).astype(jnp.bfloat16)  13.8 us
  transfers between devices with their start and end apart: 31, of which 14 were waited for; matrix products, arithmetic and copies ran while one was open for 9% of the time, Pallas kernels for 22%

profile of v3, /device:TPU:0, one launch (start us, length us, event | category | flops | bytes accessed | tf_op | source)
XLA Modules:
  0.0 324.2 jit_solution(10339549801603543985)
XLA Ops:
  7.9 1.7 slice.33.refs_0_
  13.6 15.2 %shard_map.152 = (f32[64,2304]{1,0:T(8,128)}, f32[64,2304]{1,0:T(8,128)}, f32[64,2304]{1,0:T(8,128)}) custom-call(bf16[64,2304]{1,0:T(8,128)(2,1)} %slice.33.refs_0_, bf16[512,4608]{1,0:T(8,128)(2,1)} %bitcast.66, bf16[512,4608]{1,0:T(8,128)(2,1)} %bitcast.67, f32[64,512]{1,0:T(8,128)} %broadcast_in_dim.42.refs_3_, bf16[64,6912]{1,0:T(8,128)(2,1)} %refs_5_.1, ...), custom_call_target="tpu_custom_call" | custom-call | tf_op jit(solution)/shard_map/pallas_call | solution.py:142
  29.0 20.8 %all-gather.2.cloned.1.call-done = bf16[1,512,4608]{2,1,0:T(8,128)(2,1)} async-done(((bf16[1,128,4608]{2,1,0:T(8,128)(2,1)}), bf16[1,512,4608]{2,1,0:T(8,128)(2,1)}) %all-gather.2.cloned.1.call-update) | async-done | bytes 4718608 | tf_op jit(solution)/shard_map/all_gather | solution.py:278
  50.5 13.4 %shard_map.153 = (f32[64,2304]{1,0:T(8,128)}, f32[64,2304]{1,0:T(8,128)}, f32[64,2304]{1,0:T(8,128)}) custom-call(bf16[64,2304]{1,0:T(8,128)(2,1)} %slice.33.refs_0_, bf16[512,4608]{1,0:T(8,128)(2,1)} %bitcast.68, bf16[512,4608]{1,0:T(8,128)(2,1)} %bitcast.69, f32[64,512]{1,0:T(8,128)} %broadcast_in_dim.47.refs_3_), custom_call_target="tpu_custom_call" | custom-call | tf_op jit(solution)/shard_map/pallas_call | solution.py:142
  64.0 6.8 %multiply_reduce_fusion = (f32[64]{0:T(128)S(1)}, f32[64,2304]{1,0:T(8,128)S(1)}) fusion(bf16[2304,2304]{1,0:T(8,128)(2,1)} %param.22, f32[64,2304]{1,0:T(8,128)} %get-tuple-element.29, f32[64,2304]{1,0:T(8,128)S(1)} %copy-done.6, f32[64,2304]{1,0:T(8,128)} %get-tuple-element.27, f32[64,2304]{1,0:T(8,128)} %get-tuple-element.26, ...), kind=kOutput, calls=%fused_computation.46 | convolution fusion | flops 681983936 | bytes 15040768 | tf_op jit(solution)/shard_map/dot_general | solution.py:291
  72.2 1.4 convolution_convert_fusion.1
  73.6 3.5 %all-to-all-start = ((bf16[4,48,2304]{2,1,0:T(8,128)(2,1)}), bf16[4,48,2304]{2,1,0:T(8,128)(2,1)S(1)}, u32[]{:S(2)}, u32[]{:S(2)}) async-start(bf16[4,48,2304]{2,1,0:T(8,128)(2,1)} %bitcast.7), calls=%async_computation | async-start | bytes 1769472 | tf_op jit(solution)/shard_map/all_to_all | solution.py:322
  77.1 10.2 %copy.81.gate_ref.up_ref = bf16[1,2,2304,720]{3,2,1,0:T(8,128)(2,1)} copy(bf16[1,2,2304,720]{2,3,1,0:T(8,128)(2,1)} %param.26) | data formatting | bytes 13271040 | tf_op args[12]
  88.4 1.3 all-to-all-done
  89.8 1.5 collective-permute-start
  92.1 1.2 fusion
  93.3 8.1 %collective-permute-done.first_ref = bf16[96,2304]{1,0:T(8,128)(2,1)S(1)} collective-permute-done((bf16[96,2304]{1,0:T(8,128)(2,1)S(1)}, bf16[96,2304]{1,0:T(8,128)(2,1)S(1)}, u32[]{:S(2)}, u32[]{:S(2)}) %collective-permute-start) | collective-permute-done | bytes 442400 | tf_op jit(solution)/shard_map/ppermute | solution.py:230
  101.5 1.1 collective-permute-done.1.second_ref
  103.4 7.9 %shard_map.154 = (bf16[96,2304]{1,0:T(8,128)(2,1)}, bf16[96,2304]{1,0:T(8,128)(2,1)}) custom-call(bf16[96,2304]{1,0:T(8,128)(2,1)} %copy-done.21, bf16[96,2304]{1,0:T(8,128)(2,1)} %copy-done.22, bf16[1,2,2304,720]{3,2,1,0:T(8,128)(2,1)} %copy.81.gate_ref.up_ref, bf16[1,2,2304,720]{3,2,1,0:T(8,128)(2,1)} %copy.81.gate_ref.up_ref, bf16[1,720,2304]{2,1,0:T(8,128)(2,1)} %down_ref.15), custom_call_target="tpu_custom_call" | custom-call | tf_op jit(solution)/shard_map/pallas_call | solution.py:181
  111.4 1.5 collective-permute-start.2
  112.9 1.5 collective-permute-start.3
  114.9 8.0 %shard_map.161 = (bf16[96,2304]{1,0:T(8,128)(2,1)}, bf16[96,2304]{1,0:T(8,128)(2,1)}) custom-call(bf16[96,2304]{1,0:T(8,128)(2,1)} %bitcast.73, bf16[96,2304]{1,0:T(8,128)(2,1)} %bitcast.71, bf16[1,2,2304,720]{3,2,1,0:T(8,128)(2,1)} %copy.81.gate_ref.up_ref, bf16[1,2,2304,720]{3,2,1,0:T(8,128)(2,1)} %copy.81.gate_ref.up_ref, bf16[1,720,2304]{2,1,0:T(8,128)(2,1)} %down_ref.15), custom_call_target="tpu_custom_call" | custom-call | tf_op jit(solution)/shard_map/pallas_call | solution.py:181
  123.5 8.1 %collective-permute-done.3.first_ref = bf16[96,2304]{1,0:T(8,128)(2,1)S(1)} collective-permute-done((bf16[96,2304]{1,0:T(8,128)(2,1)}, bf16[96,2304]{1,0:T(8,128)(2,1)S(1)}, u32[]{:S(2)}, u32[]{:S(2)}) %collective-permute-start.3) | collective-permute-done | bytes 442400 | tf_op jit(solution)/shard_map/ppermute | solution.py:230
  133.1 7.9 %shard_map.155 = (bf16[96,2304]{1,0:T(8,128)(2,1)}, bf16[96,2304]{1,0:T(8,128)(2,1)}) custom-call(bf16[96,2304]{1,0:T(8,128)(2,1)} %copy-done.13, bf16[96,2304]{1,0:T(8,128)(2,1)} %copy-done.14, bf16[1,2,2304,720]{3,2,1,0:T(8,128)(2,1)} %copy.81.gate_ref.up_ref, bf16[1,2,2304,720]{3,2,1,0:T(8,128)(2,1)} %copy.81.gate_ref.up_ref, bf16[1,720,2304]{2,1,0:T(8,128)(2,1)} %down_ref.15), custom_call_target="tpu_custom_call" | custom-call | tf_op jit(solution)/shard_map/pallas_call | solution.py:181
  141.0 1.1 add_convert_fusion.13
  142.2 1.5 collective-permute-start.5
  143.7 1.5 collective-permute-start.6
  145.7 1.1 add_convert_fusion.6
  147.7 13.7 %collective-permute-done.6.first_ref = bf16[96,2304]{1,0:T(8,128)(2,1)S(1)} collective-permute-done((bf16[96,2304]{1,0:T(8,128)(2,1)}, bf16[96,2304]{1,0:T(8,128)(2,1)S(1)}, u32[]{:S(2)}, u32[]{:S(2)}) %collective-permute-start.6) | collective-permute-done | bytes 442400 | tf_op jit(solution)/shard_map/ppermute | solution.py:230
  162.9 7.9 %shard_map.156 = (bf16[96,2304]{1,0:T(8,128)(2,1)}, bf16[96,2304]{1,0:T(8,128)(2,1)}) custom-call(bf16[96,2304]{1,0:T(8,128)(2,1)} %copy-done.11, bf16[96,2304]{1,0:T(8,128)(2,1)} %copy-done.19, bf16[1,2,2304,720]{3,2,1,0:T(8,128)(2,1)} %copy.81.gate_ref.up_ref, bf16[1,2,2304,720]{3,2,1,0:T(8,128)(2,1)} %copy.81.gate_ref.up_ref, bf16[1,720,2304]{2,1,0:T(8,128)(2,1)} %down_ref.15), custom_call_target="tpu_custom_call" | custom-call | tf_op jit(solution)/shard_map/pallas_call | solution.py:181
  170.8 1.1 add_convert_fusion.12
  171.9 1.5 collective-permute-start.8
  174.0 1.5 collective-permute-start.9
  175.5 1.1 add_convert_fusion.5
  177.2 9.5 %collective-permute-done.10.second_ref = bf16[96,2304]{1,0:T(8,128)(2,1)S(1)} collective-permute-done((bf16[96,2304]{1,0:T(8,128)(2,1)}, bf16[96,2304]{1,0:T(8,128)(2,1)S(1)}, u32[]{:S(2)}, u32[]{:S(2)}) %collective-permute-start.10) | collective-permute-done | bytes 442400 | tf_op jit(solution)/shard_map/ppermute | solution.py:230
  186.7 3.7 %collective-permute-done.9.first_ref = bf16[96,2304]{1,0:T(8,128)(2,1)S(1)} collective-permute-done((bf16[96,2304]{1,0:T(8,128)(2,1)}, bf16[96,2304]{1,0:T(8,128)(2,1)S(1)}, u32[]{:S(2)}, u32[]{:S(2)}) %collective-permute-start.9) | collective-permute-done | bytes 442400 | tf_op jit(solution)/shard_map/ppermute | solution.py:230
  190.4 0.8 copy-done.20
  191.2 7.9 %shard_map.157 = (bf16[96,2304]{1,0:T(8,128)(2,1)}, bf16[96,2304]{1,0:T(8,128)(2,1)}) custom-call(bf16[96,2304]{1,0:T(8,128)(2,1)} %copy-done.20, bf16[96,2304]{1,0:T(8,128)(2,1)} %copy-done.12, bf16[1,2,2304,720]{3,2,1,0:T(8,128)(2,1)} %copy.81.gate_ref.up_ref, bf16[1,2,2304,720]{3,2,1,0:T(8,128)(2,1)} %copy.81.gate_ref.up_ref, bf16[1,720,2304]{2,1,0:T(8,128)(2,1)} %down_ref.15), custom_call_target="tpu_custom_call" | custom-call | tf_op jit(solution)/shard_map/pallas_call | solution.py:181
  199.1 1.1 add_convert_fusion.11
  200.2 1.4 collective-permute-start.11
  201.6 1.5 collective-permute-start.12
  203.7 1.1 add_convert_fusion.4
  205.6 12.4 %collective-permute-done.12.first_ref = bf16[96,2304]{1,0:T(8,128)(2,1)S(1)} collective-permute-done((bf16[96,2304]{1,0:T(8,128)(2,1)}, bf16[96,2304]{1,0:T(8,128)(2,1)S(1)}, u32[]{:S(2)}, u32[]{:S(2)}) %collective-permute-start.12) | collective-permute-done | bytes 442400 | tf_op jit(solution)/shard_map/ppermute | solution.py:230
  219.5 7.9 %shard_map.158 = (bf16[96,2304]{1,0:T(8,128)(2,1)}, bf16[96,2304]{1,0:T(8,128)(2,1)}) custom-call(bf16[96,2304]{1,0:T(8,128)(2,1)} %copy-done.15, bf16[96,2304]{1,0:T(8,128)(2,1)} %copy-done.16, bf16[1,2,2304,720]{3,2,1,0:T(8,128)(2,1)} %copy.81.gate_ref.up_ref, bf16[1,2,2304,720]{3,2,1,0:T(8,128)(2,1)} %copy.81.gate_ref.up_ref, bf16[1,720,2304]{2,1,0:T(8,128)(2,1)} %down_ref.15), custom_call_target="tpu_custom_call" | custom-call | tf_op jit(solution)/shard_map/pallas_call | solution.py:181
  227.4 1.1 add_convert_fusion.10
  228.6 1.1 collective-permute-start.14
  229.7 1.5 collective-permute-start.15
  231.7 1.1 add_convert_fusion.3
  232.9 1.0 collective-permute-start.25
  233.9 11.6 %collective-permute-done.15.first_ref = bf16[96,2304]{1,0:T(8,128)(2,1)S(1)} collective-permute-done((bf16[96,2304]{1,0:T(8,128)(2,1)}, bf16[96,2304]{1,0:T(8,128)(2,1)S(1)}, u32[]{:S(2)}, u32[]{:S(2)}) %collective-permute-start.15) | collective-permute-done | bytes 442400 | tf_op jit(solution)/shard_map/ppermute | solution.py:230
  247.0 7.9 %shard_map.159 = (bf16[96,2304]{1,0:T(8,128)(2,1)}, bf16[96,2304]{1,0:T(8,128)(2,1)}) custom-call(bf16[96,2304]{1,0:T(8,128)(2,1)} %copy-done.17, bf16[96,2304]{1,0:T(8,128)(2,1)} %copy-done.18, bf16[1,2,2304,720]{3,2,1,0:T(8,128)(2,1)} %copy.81.gate_ref.up_ref, bf16[1,2,2304,720]{3,2,1,0:T(8,128)(2,1)} %copy.81.gate_ref.up_ref, bf16[1,720,2304]{2,1,0:T(8,128)(2,1)} %down_ref.15), custom_call_target="tpu_custom_call" | custom-call | tf_op jit(solution)/shard_map/pallas_call | solution.py:181
  254.9 1.1 add_convert_fusion.9
  256.1 0.8 collective-permute-start.17
  256.9 1.5 collective-permute-start.18
  258.9 1.1 add_convert_fusion.2
  260.1 1.3 collective-permute-start.26
  261.4 10.7 %collective-permute-done.18.first_ref = bf16[96,2304]{1,0:T(8,128)(2,1)S(1)} collective-permute-done((bf16[96,2304]{1,0:T(8,128)(2,1)}, bf16[96,2304]{1,0:T(8,128)(2,1)S(1)}, u32[]{:S(2)}, u32[]{:S(2)}) %collective-permute-start.18) | collective-permute-done | bytes 442400 | tf_op jit(solution)/shard_map/ppermute | solution.py:230
  272.9 7.9 %shard_map.160 = (bf16[96,2304]{1,0:T(8,128)(2,1)}, bf16[96,2304]{1,0:T(8,128)(2,1)}) custom-call(bf16[96,2304]{1,0:T(8,128)(2,1)} %copy-done.23, bf16[96,2304]{1,0:T(8,128)(2,1)} %collective-permute-done.19.second_ref, bf16[1,2,2304,720]{3,2,1,0:T(8,128)(2,1)} %copy.81.gate_ref.up_ref, bf16[1,2,2304,720]{3,2,1,0:T(8,128)(2,1)} %copy.81.gate_ref.up_ref, ...), custom_call_target="tpu_custom_call" | custom-call | tf_op jit(solution)/shard_map/pallas_call | solution.py:181
  280.8 1.2 add_convert_fusion.8
  282.6 1.1 add_convert_fusion.1
  283.8 1.6 collective-permute-start.27
  285.3 5.1 %collective-permute-done.20 = bf16[96,2304]{1,0:T(8,128)(2,1)S(1)} collective-permute-done((bf16[96,2304]{1,0:T(8,128)(2,1)S(1)}, bf16[96,2304]{1,0:T(8,128)(2,1)S(1)}, u32[]{:S(2)}, u32[]{:S(2)}) %collective-permute-start.20) | collective-permute-done | bytes 442400 | tf_op jit(solution)/shard_map/ppermute | solution.py:242
  290.5 1.6 collective-permute-done.27
  292.2 1.0 pad_maximum_fusion
  293.2 6.0 %all-to-all-start.1 = ((bf16[4,48,2304]{2,1,0:T(8,128)(2,1)}), bf16[4,48,2304]{2,1,0:T(8,128)(2,1)S(1)}, u32[]{:S(2)}, u32[]{:S(2)}) async-start(bf16[4,48,2304]{2,1,0:T(8,128)(2,1)} %bitcast.10), calls=%async_computation.1 | async-start | bytes 1769472 | tf_op jit(solution)/shard_map/all_to_all | solution.py:336
  299.5 12.4 %all-to-all-done.1 = bf16[4,48,2304]{2,1,0:T(8,128)(2,1)S(1)} async-done(((bf16[4,48,2304]{2,1,0:T(8,128)(2,1)}), bf16[4,48,2304]{2,1,0:T(8,128)(2,1)S(1)}, u32[]{:S(2)}, u32[]{:S(2)}) %all-to-all-start.1) | async-done | bytes 884768 | tf_op jit(solution)/shard_map/all_to_all | solution.py:336
  312.1 2.1 gather_fusion
  314.2 2.0 gather.7
  316.4 0.9 fusion.8
  (126 shorter events, 22.0 us)
Async XLA Ops:
  7.2 292.1 %copy-start = (bf16[2304,4]{0,1:T(4,128)(2,1)S(1)}, bf16[2304,4]{0,1:T(4,128)(2,1)}, u32[]{:S(2)}) copy-start(bf16[2304,4]{0,1:T(4,128)(2,1)} %param.24) | copy-start | bytes 55300
  7.2 3.8 %copy-start.25 = (s32[64,2]{0,1:T(2,128)S(1)}, s32[64,2]{0,1:T(2,128)}, u32[]{:S(2)}) copy-start(s32[64,2]{0,1:T(2,128)} %param.25) | copy-start | bytes 1540
  7.2 4.0 %copy-start.27 = (s32[1,64]{1,0:T(1,128)S(1)}, s32[1,64]{1,0:T(1,128)}, u32[]{:S(2)}) copy-start(s32[1,64]{1,0:T(1,128)} %param.20) | copy-start | bytes 772
  7.2 42.6 %all-gather.2.cloned.1.call-start = ((), (), s32[]{:S(2)}) async-start(), calls=%async_computation.2 | async-start | bytes 5898240 | tf_op jit(solution)/shard_map/all_gather | solution.py:278
  50.5 13.4 %copy-start.4 = (f32[64,2304]{1,0:T(8,128)S(1)}, f32[64,2304]{1,0:T(8,128)}, u32[]{:S(2)}) copy-start(f32[64,2304]{1,0:T(8,128)} %get-tuple-element.24) | copy-start | bytes 1769476
  50.5 13.4 %copy-start.5 = (f32[64,2304]{1,0:T(8,128)S(1)}, f32[64,2304]{1,0:T(8,128)}, u32[]{:S(2)}) copy-start(f32[64,2304]{1,0:T(8,128)} %get-tuple-element.25) | copy-start | bytes 1769476
  50.5 13.5 %copy-start.6 = (f32[64,2304]{1,0:T(8,128)S(1)}, f32[64,2304]{1,0:T(8,128)}, u32[]{:S(2)}) copy-start(f32[64,2304]{1,0:T(8,128)} %get-tuple-element.28) | copy-start | bytes 1769476
  50.5 13.5 %copy-start.24 = (bf16[64,2304]{1,0:T(8,128)(2,1)S(1)}, bf16[64,2304]{1,0:T(8,128)(2,1)}, u32[]{:S(2)}) copy-start(bf16[64,2304]{1,0:T(8,128)(2,1)} %param.14) | copy-start | bytes 884740
  63.9 6.8 %copy-start.26 = (f32[2304]{0:T(1024)S(1)}, f32[2304]{0:T(1024)}, u32[]{:S(2)}) copy-start(f32[2304]{0:T(1024)} %param.23) | copy-start | bytes 27652
  70.9 0.7 copy-start.2
  73.6 16.2 %all-to-all-start = ((bf16[4,48,2304]{2,1,0:T(8,128)(2,1)}), bf16[4,48,2304]{2,1,0:T(8,128)(2,1)S(1)}, u32[]{:S(2)}, u32[]{:S(2)}) async-start(bf16[4,48,2304]{2,1,0:T(8,128)(2,1)} %bitcast.7), calls=%async_computation | async-start | bytes 1769472 | tf_op jit(solution)/shard_map/all_to_all | solution.py:322
  87.3 4.8 %copy-start.1 = (bf16[64,6912]{1,0:T(8,128)(2,1)S(1)}, bf16[64,6912]{1,0:T(8,128)(2,1)}, u32[]{:S(2)}) copy-start(bf16[64,6912]{1,0:T(8,128)(2,1)} %refs_5_.1) | copy-start | bytes 2654212
  89.8 21.6 %copy-start.7 = (bf16[2,48,2304]{2,1,0:T(8,128)(2,1)}, bf16[2,48,2304]{2,1,0:T(8,128)(2,1)S(1)}, u32[]{:S(2)}) copy-start(bf16[2,48,2304]{2,1,0:T(8,128)(2,1)S(1)} %get-tuple-element.46) | copy-start | bytes 1327108
  89.8 21.6 %copy-start.8 = (bf16[2,48,2304]{2,1,0:T(8,128)(2,1)}, bf16[2,48,2304]{2,1,0:T(8,128)(2,1)S(1)}, u32[]{:S(2)}) copy-start(bf16[2,48,2304]{2,1,0:T(8,128)(2,1)S(1)} %get-tuple-element.47) | copy-start | bytes 1327108
  89.8 11.7 %collective-permute-start = (bf16[96,2304]{1,0:T(8,128)(2,1)S(1)}, bf16[96,2304]{1,0:T(8,128)(2,1)S(1)}, u32[]{:S(2)}, u32[]{:S(2)}) collective-permute-start(bf16[96,2304]{1,0:T(8,128)(2,1)S(1)} %bitcast.72), channel_id=1, source_target_pairs={{0,4},{4,12},{12,20},{20,28},{28,24},{24,16},{16,8},{8,0},{1,5},{5... | collective-permute-start | bytes 1327112 | tf_op jit(solution)/shard_map/ppermute | solution.py:230
  91.3 11.3 %collective-permute-start.1 = (bf16[96,2304]{1,0:T(8,128)(2,1)S(1)}, bf16[96,2304]{1,0:T(8,128)(2,1)S(1)}, u32[]{:S(2)}, u32[]{:S(2)}) collective-permute-start(bf16[96,2304]{1,0:T(8,128)(2,1)S(1)} %bitcast.70), channel_id=1, source_target_pairs={{0,8},{4,0},{12,4},{20,12},{28,20},{24,28},{16,24},{8,16},{1,9},{5... | collective-permute-start | bytes 1327112 | tf_op jit(solution)/shard_map/ppermute | solution.py:230
  101.5 1.1 copy-start.21
  102.6 0.8 copy-start.22
  111.4 29.7 %collective-permute-start.2 = (bf16[96,2304]{1,0:T(8,128)(2,1)}, bf16[96,2304]{1,0:T(8,128)(2,1)S(1)}, u32[]{:S(2)}, u32[]{:S(2)}) collective-permute-start(bf16[96,2304]{1,0:T(8,128)(2,1)} %get-tuple-element.30), channel_id=1, source_target_pairs={{0,4},{4,12},{12,20},{20,28},{28,24},{24,16},{16,8},{8,0},{1,5},{5... | collective-permute-start | bytes 1327112 | tf_op jit(solution)/shard_map/ppermute | solution.py:240
  112.9 18.7 %collective-permute-start.3 = (bf16[96,2304]{1,0:T(8,128)(2,1)}, bf16[96,2304]{1,0:T(8,128)(2,1)S(1)}, u32[]{:S(2)}, u32[]{:S(2)}) collective-permute-start(bf16[96,2304]{1,0:T(8,128)(2,1)} %copy-done.21), channel_id=1, source_target_pairs={{0,4},{4,12},{12,20},{20,28},{28,24},{24,16},{16,8},{8,0},{1,5},{5... | collective-permute-start | bytes 1327112 | tf_op jit(solution)/shard_map/ppermute | solution.py:230
  114.4 17.2 %collective-permute-start.4 = (bf16[96,2304]{1,0:T(8,128)(2,1)}, bf16[96,2304]{1,0:T(8,128)(2,1)S(1)}, u32[]{:S(2)}, u32[]{:S(2)}) collective-permute-start(bf16[96,2304]{1,0:T(8,128)(2,1)} %copy-done.22), channel_id=1, source_target_pairs={{0,8},{4,0},{12,4},{20,12},{28,20},{24,28},{16,24},{8,16},{1,9},{5... | collective-permute-start | bytes 1327112 | tf_op jit(solution)/shard_map/ppermute | solution.py:230
  122.9 22.8 %collective-permute-start.21 = (bf16[96,2304]{1,0:T(8,128)(2,1)}, bf16[96,2304]{1,0:T(8,128)(2,1)S(1)}, u32[]{:S(2)}, u32[]{:S(2)}) collective-permute-start(bf16[96,2304]{1,0:T(8,128)(2,1)} %get-tuple-element.38), channel_id=1, source_target_pairs={{0,8},{4,0},{12,4},{20,12},{28,20},{24,28},{16,24},{8,16},{1,9},{5... | collective-permute-start | bytes 1327112 | tf_op jit(solution)/shard_map/ppermute | solution.py:240
  131.6 0.8 copy-start.13
  132.3 0.8 copy-start.14
  142.2 28.6 %collective-permute-start.5 = (bf16[96,2304]{1,0:T(8,128)(2,1)S(1)}, bf16[96,2304]{1,0:T(8,128)(2,1)S(1)}, u32[]{:S(2)}, u32[]{:S(2)}) collective-permute-start(bf16[96,2304]{1,0:T(8,128)(2,1)S(1)} %add_convert_fusion.13), channel_id=1, source_target_pairs={{0,4},{4,12},{12,20},{20,28},{28,24},{24,16},{16,8},{8,0},{1,5},{5... | collective-permute-start | bytes 1327112 | tf_op jit(solution)/shard_map/ppermute | solution.py:240
  143.7 17.6 %collective-permute-start.6 = (bf16[96,2304]{1,0:T(8,128)(2,1)}, bf16[96,2304]{1,0:T(8,128)(2,1)S(1)}, u32[]{:S(2)}, u32[]{:S(2)}) collective-permute-start(bf16[96,2304]{1,0:T(8,128)(2,1)} %copy-done.13), channel_id=1, source_target_pairs={{0,4},{4,12},{12,20},{20,28},{28,24},{24,16},{16,8},{8,0},{1,5},{5... | collective-permute-start | bytes 1327112 | tf_op jit(solution)/shard_map/ppermute | solution.py:230
  145.2 16.1 %collective-permute-start.7 = (bf16[96,2304]{1,0:T(8,128)(2,1)}, bf16[96,2304]{1,0:T(8,128)(2,1)S(1)}, u32[]{:S(2)}, u32[]{:S(2)}) collective-permute-start(bf16[96,2304]{1,0:T(8,128)(2,1)} %copy-done.14), channel_id=1, source_target_pairs={{0,8},{4,0},{12,4},{20,12},{28,20},{24,28},{16,24},{8,16},{1,9},{5... | collective-permute-start | bytes 1327112 | tf_op jit(solution)/shard_map/ppermute | solution.py:230
  146.9 28.6 %collective-permute-start.22 = (bf16[96,2304]{1,0:T(8,128)(2,1)S(1)}, bf16[96,2304]{1,0:T(8,128)(2,1)S(1)}, u32[]{:S(2)}, u32[]{:S(2)}) collective-permute-start(bf16[96,2304]{1,0:T(8,128)(2,1)S(1)} %add_convert_fusion.6), channel_id=1, source_target_pairs={{0,8},{4,0},{12,4},{20,12},{28,20},{24,28},{16,24},{8,16},{1,9},{5... | collective-permute-start | bytes 1327112 | tf_op jit(solution)/shard_map/ppermute | solution.py:240
  161.3 0.8 copy-start.11
  162.1 0.8 copy-start.19
  171.9 27.2 %collective-permute-start.8 = (bf16[96,2304]{1,0:T(8,128)(2,1)S(1)}, bf16[96,2304]{1,0:T(8,128)(2,1)S(1)}, u32[]{:S(2)}, u32[]{:S(2)}) collective-permute-start(bf16[96,2304]{1,0:T(8,128)(2,1)S(1)} %add_convert_fusion.12), channel_id=1, source_target_pairs={{0,4},{4,12},{12,20},{20,28},{28,24},{24,16},{16,8},{8,0},{1,5},{5... | collective-permute-start | bytes 1327112 | tf_op jit(solution)/shard_map/ppermute | solution.py:240
  173.5 13.2 %collective-permute-start.10 = (bf16[96,2304]{1,0:T(8,128)(2,1)}, bf16[96,2304]{1,0:T(8,128)(2,1)S(1)}, u32[]{:S(2)}, u32[]{:S(2)}) collective-permute-start(bf16[96,2304]{1,0:T(8,128)(2,1)} %copy-done.19), channel_id=1, source_target_pairs={{0,8},{4,0},{12,4},{20,12},{28,20},{24,28},{16,24},{8,16},{1,9},{5... | collective-permute-start | bytes 1327112 | tf_op jit(solution)/shard_map/ppermute | solution.py:230
  174.0 16.4 %collective-permute-start.9 = (bf16[96,2304]{1,0:T(8,128)(2,1)}, bf16[96,2304]{1,0:T(8,128)(2,1)S(1)}, u32[]{:S(2)}, u32[]{:S(2)}) collective-permute-start(bf16[96,2304]{1,0:T(8,128)(2,1)} %copy-done.11), channel_id=1, source_target_pairs={{0,4},{4,12},{12,20},{20,28},{28,24},{24,16},{16,8},{8,0},{1,5},{5... | collective-permute-start | bytes 1327112 | tf_op jit(solution)/shard_map/ppermute | solution.py:230
  176.7 27.0 %collective-permute-start.23 = (bf16[96,2304]{1,0:T(8,128)(2,1)S(1)}, bf16[96,2304]{1,0:T(8,128)(2,1)S(1)}, u32[]{:S(2)}, u32[]{:S(2)}) collective-permute-start(bf16[96,2304]{1,0:T(8,128)(2,1)S(1)} %add_convert_fusion.5), channel_id=1, source_target_pairs={{0,8},{4,0},{12,4},{20,12},{28,20},{24,28},{16,24},{8,16},{1,9},{5... | collective-permute-start | bytes 1327112 | tf_op jit(solution)/shard_map/ppermute | solution.py:240
  186.7 3.7 %copy-start.12 = (bf16[96,2304]{1,0:T(8,128)(2,1)}, bf16[96,2304]{1,0:T(8,128)(2,1)S(1)}, u32[]{:S(2)}) copy-start(bf16[96,2304]{1,0:T(8,128)(2,1)S(1)} %collective-permute-done.10.second_ref) | copy-start | bytes 1327108
  190.4 0.8 copy-start.20
  200.2 27.2 %collective-permute-start.11 = (bf16[96,2304]{1,0:T(8,128)(2,1)S(1)}, bf16[96,2304]{1,0:T(8,128)(2,1)S(1)}, u32[]{:S(2)}, u32[]{:S(2)}) collective-permute-start(bf16[96,2304]{1,0:T(8,128)(2,1)S(1)} %add_convert_fusion.11), channel_id=1, source_target_pairs={{0,4},{4,12},{12,20},{20,28},{28,24},{24,16},{16,8},{8,0},{1,5},{5... | collective-permute-start | bytes 1327112 | tf_op jit(solution)/shard_map/ppermute | solution.py:240
  201.6 16.3 %collective-permute-start.12 = (bf16[96,2304]{1,0:T(8,128)(2,1)}, bf16[96,2304]{1,0:T(8,128)(2,1)S(1)}, u32[]{:S(2)}, u32[]{:S(2)}) collective-permute-start(bf16[96,2304]{1,0:T(8,128)(2,1)} %copy-done.20), channel_id=1, source_target_pairs={{0,4},{4,12},{12,20},{20,28},{28,24},{24,16},{16,8},{8,0},{1,5},{5... | collective-permute-start | bytes 1327112 | tf_op jit(solution)/shard_map/ppermute | solution.py:230
  203.1 14.8 %collective-permute-start.13 = (bf16[96,2304]{1,0:T(8,128)(2,1)}, bf16[96,2304]{1,0:T(8,128)(2,1)S(1)}, u32[]{:S(2)}, u32[]{:S(2)}) collective-permute-start(bf16[96,2304]{1,0:T(8,128)(2,1)} %copy-done.12), channel_id=1, source_target_pairs={{0,8},{4,0},{12,4},{20,12},{28,20},{24,28},{16,24},{8,16},{1,9},{5... | collective-permute-start | bytes 1327112 | tf_op jit(solution)/shard_map/ppermute | solution.py:230
  204.8 26.9 %collective-permute-start.24 = (bf16[96,2304]{1,0:T(8,128)(2,1)S(1)}, bf16[96,2304]{1,0:T(8,128)(2,1)S(1)}, u32[]{:S(2)}, u32[]{:S(2)}) collective-permute-start(bf16[96,2304]{1,0:T(8,128)(2,1)S(1)} %add_convert_fusion.4), channel_id=1, source_target_pairs={{0,8},{4,0},{12,4},{20,12},{28,20},{24,28},{16,24},{8,16},{1,9},{5... | collective-permute-start | bytes 1327112 | tf_op jit(solution)/shard_map/ppermute | solution.py:240
  218.0 0.8 copy-start.15
  218.8 0.8 copy-start.16
  228.6 26.3 %collective-permute-start.14 = (bf16[96,2304]{1,0:T(8,128)(2,1)S(1)}, bf16[96,2304]{1,0:T(8,128)(2,1)S(1)}, u32[]{:S(2)}, u32[]{:S(2)}) collective-permute-start(bf16[96,2304]{1,0:T(8,128)(2,1)S(1)} %add_convert_fusion.10), channel_id=1, source_target_pairs={{0,4},{4,12},{12,20},{20,28},{28,24},{24,16},{16,8},{8,0},{1,5},{5... | collective-permute-start | bytes 1327112 | tf_op jit(solution)/shard_map/ppermute | solution.py:240
  229.7 15.8 %collective-permute-start.15 = (bf16[96,2304]{1,0:T(8,128)(2,1)}, bf16[96,2304]{1,0:T(8,128)(2,1)S(1)}, u32[]{:S(2)}, u32[]{:S(2)}) collective-permute-start(bf16[96,2304]{1,0:T(8,128)(2,1)} %copy-done.15), channel_id=1, source_target_pairs={{0,4},{4,12},{12,20},{20,28},{28,24},{24,16},{16,8},{8,0},{1,5},{5... | collective-permute-start | bytes 1327112 | tf_op jit(solution)/shard_map/ppermute | solution.py:230
  231.2 14.3 %collective-permute-start.16 = (bf16[96,2304]{1,0:T(8,128)(2,1)}, bf16[96,2304]{1,0:T(8,128)(2,1)S(1)}, u32[]{:S(2)}, u32[]{:S(2)}) collective-permute-start(bf16[96,2304]{1,0:T(8,128)(2,1)} %copy-done.16), channel_id=1, source_target_pairs={{0,8},{4,0},{12,4},{20,12},{28,20},{24,28},{16,24},{8,16},{1,9},{5... | collective-permute-start | bytes 1327112 | tf_op jit(solution)/shard_map/ppermute | solution.py:230
  232.9 26.1 %collective-permute-start.25 = (bf16[96,2304]{1,0:T(8,128)(2,1)S(1)}, bf16[96,2304]{1,0:T(8,128)(2,1)S(1)}, u32[]{:S(2)}, u32[]{:S(2)}) collective-permute-start(bf16[96,2304]{1,0:T(8,128)(2,1)S(1)} %add_convert_fusion.3), channel_id=1, source_target_pairs={{0,8},{4,0},{12,4},{20,12},{28,20},{24,28},{16,24},{8,16},{1,9},{5... | collective-permute-start | bytes 1327112 | tf_op jit(solution)/shard_map/ppermute | solution.py:240
  245.5 0.8 copy-start.17
  246.3 0.8 copy-start.18
  256.1 24.7 %collective-permute-start.17 = (bf16[96,2304]{1,0:T(8,128)(2,1)S(1)}, bf16[96,2304]{1,0:T(8,128)(2,1)S(1)}, u32[]{:S(2)}, u32[]{:S(2)}) collective-permute-start(bf16[96,2304]{1,0:T(8,128)(2,1)S(1)} %add_convert_fusion.9), channel_id=1, source_target_pairs={{0,4},{4,12},{12,20},{20,28},{28,24},{24,16},{16,8},{8,0},{1,5},{5... | collective-permute-start | bytes 1327112 | tf_op jit(solution)/shard_map/ppermute | solution.py:240
  256.9 15.2 %collective-permute-start.18 = (bf16[96,2304]{1,0:T(8,128)(2,1)}, bf16[96,2304]{1,0:T(8,128)(2,1)S(1)}, u32[]{:S(2)}, u32[]{:S(2)}) collective-permute-start(bf16[96,2304]{1,0:T(8,128)(2,1)} %copy-done.17), channel_id=1, source_target_pairs={{0,4},{4,12},{12,20},{20,28},{28,24},{24,16},{16,8},{8,0},{1,5},{5... | collective-permute-start | bytes 1327112 | tf_op jit(solution)/shard_map/ppermute | solution.py:230
  258.4 13.7 %collective-permute-start.19 = (bf16[96,2304]{1,0:T(8,128)(2,1)}, bf16[96,2304]{1,0:T(8,128)(2,1)}, u32[]{:S(2)}, u32[]{:S(2)}) collective-permute-start(bf16[96,2304]{1,0:T(8,128)(2,1)} %copy-done.18), channel_id=1, source_target_pairs={{0,8},{4,0},{12,4},{20,12},{28,20},{24,28},{16,24},{8,16},{1,9},{5... | collective-permute-start | bytes 1327112 | tf_op jit(solution)/shard_map/ppermute | solution.py:230
  260.1 22.5 %collective-permute-start.26 = (bf16[96,2304]{1,0:T(8,128)(2,1)S(1)}, bf16[96,2304]{1,0:T(8,128)(2,1)S(1)}, u32[]{:S(2)}, u32[]{:S(2)}) collective-permute-start(bf16[96,2304]{1,0:T(8,128)(2,1)S(1)} %add_convert_fusion.2), channel_id=1, source_target_pairs={{0,8},{4,0},{12,4},{20,12},{28,20},{24,28},{16,24},{8,16},{1,9},{5... | collective-permute-start | bytes 1327112 | tf_op jit(solution)/shard_map/ppermute | solution.py:240
  272.1 0.8 copy-start.23
  280.8 9.6 %copy-start.10 = (bf16[96,2304]{1,0:T(8,128)(2,1)S(1)}, bf16[96,2304]{1,0:T(8,128)(2,1)}, u32[]{:S(2)}) copy-start(bf16[96,2304]{1,0:T(8,128)(2,1)} %get-tuple-element.37) | copy-start | bytes 1327108
  280.8 11.3 %copy-start.9 = (bf16[96,2304]{1,0:T(8,128)(2,1)S(1)}, bf16[96,2304]{1,0:T(8,128)(2,1)}, u32[]{:S(2)}) copy-start(bf16[96,2304]{1,0:T(8,128)(2,1)} %get-tuple-element.45) | copy-start | bytes 1327108
  282.1 8.4 %collective-permute-start.20 = (bf16[96,2304]{1,0:T(8,128)(2,1)S(1)}, bf16[96,2304]{1,0:T(8,128)(2,1)S(1)}, u32[]{:S(2)}, u32[]{:S(2)}) collective-permute-start(bf16[96,2304]{1,0:T(8,128)(2,1)S(1)} %add_convert_fusion.8), channel_id=1, source_target_pairs={{0,4},{4,12},{12,20},{20,28},{28,24},{24,16},{16,8},{8,0},{1,5},{5... | collective-permute-start | bytes 1327112 | tf_op jit(solution)/shard_map/ppermute | solution.py:242
  283.8 8.4 %collective-permute-start.27 = (bf16[96,2304]{1,0:T(8,128)(2,1)S(1)}, bf16[96,2304]{1,0:T(8,128)(2,1)S(1)}, u32[]{:S(2)}, u32[]{:S(2)}) collective-permute-start(bf16[96,2304]{1,0:T(8,128)(2,1)S(1)} %add_convert_fusion.1), channel_id=1, source_target_pairs={{0,8},{4,0},{12,4},{20,12},{28,20},{24,28},{16,24},{8,16},{1,9},{5... | collective-permute-start | bytes 1327112 | tf_op jit(solution)/shard_map/ppermute | solution.py:242
  292.2 7.1 %copy-start.3 = (bf16[64,2304]{1,0:T(8,128)(2,1)S(1)}, bf16[64,2304]{1,0:T(8,128)(2,1)}, u32[]{:S(2)}) copy-start(bf16[64,2304]{1,0:T(8,128)(2,1)} %copy-done.2) | copy-start | bytes 884740
  293.2 18.7 %all-to-all-start.1 = ((bf16[4,48,2304]{2,1,0:T(8,128)(2,1)}), bf16[4,48,2304]{2,1,0:T(8,128)(2,1)S(1)}, u32[]{:S(2)}, u32[]{:S(2)}) async-start(bf16[4,48,2304]{2,1,0:T(8,128)(2,1)} %bitcast.10), calls=%async_computation.1 | async-start | bytes 1769472 | tf_op jit(solution)/shard_map/all_to_all | solution.py:336
Sparse Core Ops, SparseCore 0:
  9.6 40.1 all-gather.1

commit v4 on v2

--- a/solution.py
+++ b/solution.py
@@ -269,11 +269,12 @@
     gate_cols = w_gate_up[0, 0]
     up_cols = w_gate_up[0, 1]
     down_rows = w_down[0]
-    arrived = lax.all_to_all(outgoing, "expert", split_axis=0, concat_axis=0, tiled=True)
-    arrived = arrived.reshape(experts * capacity, features)
-    half = experts * capacity // 2
-    forward = ring_gather(arrived[:half], ring, 1)
-    backward = ring_gather(arrived[half:], ring, -1)
+    split = capacity // 2
+    half = experts * split
+    first_rows = lax.all_to_all(outgoing[:, :split], "expert", split_axis=0, concat_axis=0, tiled=True)
+    second_rows = lax.all_to_all(outgoing[:, split:], "expert", split_axis=0, concat_axis=0, tiled=True)
+    forward = ring_gather(first_rows.reshape(half, features), ring, 1)
+    backward = ring_gather(second_rows.reshape(half, features), ring, -1)
     forward_out = []
     backward_out = []
     for index in range(len(ring)):
@@ -284,18 +285,23 @@
         partial = jnp.dot(hidden_units, down_rows, preferred_element_type=jnp.float32).astype(jnp.bfloat16)
         forward_out.append(partial[:half])
         backward_out.append(partial[half:])
-    summed_rows = jnp.concatenate(
-        [ring_reduce(forward_out, ring, 1), ring_reduce(backward_out, ring, -1)], axis=0
-    )
-    returned = lax.all_to_all(
-        summed_rows.reshape(experts, capacity, features).astype(jnp.bfloat16),
+    first_back = lax.all_to_all(
+        ring_reduce(forward_out, ring, 1).astype(jnp.bfloat16).reshape(experts, split, features),
         "expert",
         split_axis=0,
         concat_axis=0,
         tiled=True,
-    ).astype(jnp.float32)
-    flat_back = returned.reshape(experts * capacity, features)
-    fetched = jnp.take(flat_back, target, axis=0).reshape(row_count, 2, features)
+    )
+    second_back = lax.all_to_all(
+        ring_reduce(backward_out, ring, -1).astype(jnp.bfloat16).reshape(experts, split, features),
+        "expert",
+        split_axis=0,
+        concat_axis=0,
+        tiled=True,
+    )
+    flat_back = jnp.concatenate([first_back, second_back], axis=1).reshape(experts * capacity, features)
+    pick = (target[:, None] == jnp.arange(experts * capacity, dtype=jnp.int32)[None, :]).astype(jnp.bfloat16)
+    fetched = jnp.dot(pick, flat_back, preferred_element_type=jnp.float32).reshape(row_count, 2, features)
     layer_out = (
         middle32 + gate_first[:, None] * fetched[:, 0] + gate_second[:, None] * fetched[:, 1]
     ).astype(jnp.bfloat16)

time: 302 us -> 302 us (level)
  starting transfers between devices: 36.9 us -> 45.9 us
  local copies, waits for them, and re-layouts: 40.1 us -> 33.5 us
  other arithmetic: 25.6 us -> 21.1 us
    all_to_all x2 -> x4, starting transfers between devices: 8.45 us -> 16.5 us  [the longest x1 4.14 us: local(): lax.all_to_all(ring_reduce(backward_out, ring, -1).astype(jnp.bfloat16).r...]
    gather x2 -> x0, local copies, waits for them, and re-layouts: 7.04 us -> none  [local(): jnp.take(flat_back, target, axis=0).reshape(row_count, 2, features)]
    all_to_all x2 -> x4, waiting for transfers between devices: 24.1 us -> 26.8 us  [the longest x1 7.96 us: local(): lax.all_to_all(ring_reduce(forward_out, ring, 1).astype(jnp.bfloat16).res...]
    unnamed x42 -> x38, local copies, waits for them, and re-layouts: 15.7 us -> 16.7 us
  transfers between devices with their start and end apart: 31 -> 33, of which waited for: 16 -> 15; matrix products, arithmetic and copies ran while one was open for 35% -> 35% of each run, Pallas kernels for 5% -> 5%
where the time goes in v4:
time: 302 us; the launch traced here: 300 us
  matrix products  90.7 us (30%)
  waiting for transfers between devices  63.8 us (21%)
  starting transfers between devices  45.9 us (15%)
  local copies, waits for them, and re-layouts  33.5 us (11%)
  Pallas kernels  28.4 us (9%)
  other arithmetic  21.1 us (7%)
  between operations  16.4 us (5%)
    dot_general x8, matrix products, local(): jnp.dot(hidden_units, down_rows, preferred_element_type=jnp.float32)  45 us
    dot_general x8, matrix products, local(): gate_act = jnp.dot(pooled, gate_cols, preferred_element_type=jnp.float32)  31.4 us
    pallas_call x2, Pallas kernels, attend(): pl.pallas_call(functools.partial(attend_kernel, count=len(sources), scale...  28.4 us
    all_gather x1, waiting for transfers between devices, local(): shard_rows = lax.all_gather(prompt_kv, 'expert', axis=1, tiled=True)  18.3 us
    unnamed x38, local copies, waits for them, and re-layouts  16.7 us
    ppermute x14, waiting for transfers between devices, ring_gather(): piece = lax.ppermute(piece, 'dp', pairs)  15.6 us
    convert_element_type x6, other arithmetic, ring_reduce(): moving = (received + blocks[index].astype(jnp.float32)).astype(jnp.bfloat16)  15.3 us
    ppermute x14, starting transfers between devices, ring_gather(): piece = lax.ppermute(piece, 'dp', pairs)  15.2 us
  transfers between devices with their start and end apart: 33, of which 15 were waited for; matrix products, arithmetic and copies ran while one was open for 35% of the time, Pallas kernels for 5%

profile of v4, /device:TPU:0, one launch (start us, length us, event | category | flops | bytes accessed | tf_op | source)
XLA Modules:
  0.0 299.8 jit_solution(10249384702327187184)
XLA Ops:
  7.9 1.9 slice.81.refs_0_
  16.2 15.2 %shard_map.152 = (f32[64,2304]{1,0:T(8,128)}, f32[64,2304]{1,0:T(8,128)}, f32[64,2304]{1,0:T(8,128)}) custom-call(bf16[64,2304]{1,0:T(8,128)(2,1)} %slice.81.refs_0_, bf16[512,4608]{1,0:T(8,128)(2,1)} %bitcast.164, bf16[512,4608]{1,0:T(8,128)(2,1)} %bitcast.165, f32[64,512]{1,0:T(8,128)} %broadcast_in_dim.32.refs_3_, bf16[64,6912]{1,0:T(8,128)(2,1)} %refs_5_.1, ...), custom_call_target="tpu_custom_call" | custom-call | tf_op jit(solution)/shard_map/pallas_call | solution.py:141
  31.4 18.3 %all-gather.2.cloned.1.call-done = bf16[1,512,4608]{2,1,0:T(8,128)(2,1)} async-done(((bf16[1,128,4608]{2,1,0:T(8,128)(2,1)}), bf16[1,512,4608]{2,1,0:T(8,128)(2,1)}) %all-gather.2.cloned.1.call-update) | async-done | bytes 4718608 | tf_op jit(solution)/shard_map/all_gather | solution.py:228
  50.4 13.3 %shard_map.153 = (f32[64,2304]{1,0:T(8,128)}, f32[64,2304]{1,0:T(8,128)}, f32[64,2304]{1,0:T(8,128)}) custom-call(bf16[64,2304]{1,0:T(8,128)(2,1)} %slice.81.refs_0_, bf16[512,4608]{1,0:T(8,128)(2,1)} %bitcast.166, bf16[512,4608]{1,0:T(8,128)(2,1)} %bitcast.167, f32[64,512]{1,0:T(8,128)} %broadcast_in_dim.33.refs_3_), custom_call_target="tpu_custom_call" | custom-call | tf_op jit(solution)/shard_map/pallas_call | solution.py:141
  63.7 7.3 %multiply_reduce_fusion = (f32[64]{0:T(128)S(1)}, f32[64,2304]{1,0:T(8,128)S(1)}) fusion(bf16[2304,2304]{1,0:T(8,128)(2,1)} %param.22, f32[64,2304]{1,0:T(8,128)} %get-tuple-element.13, f32[64,2304]{1,0:T(8,128)} %get-tuple-element.12, f32[64,2304]{1,0:T(8,128)} %get-tuple-element.11, f32[64,2304]{1,0:T(8,128)} %get-tuple-element.10, ...), kind=kOutput, calls=%fused_computation.106 | convolution fusion | flops 681983936 | bytes 15040768 | tf_op jit(solution)/shard_map/dot_general | solution.py:241
  72.7 1.1 broadcast_in_dim.36
  73.8 2.7 reshape.304
  76.5 1.4 convolution_convert_fusion.1
  78.9 4.1 %all-to-all-start = ((bf16[4,24,2304]{2,1,0:T(8,128)(2,1)}), bf16[4,24,2304]{2,1,0:T(8,128)(2,1)}, u32[]{:S(2)}, u32[]{:S(2)}) async-start(bf16[4,24,2304]{2,1,0:T(8,128)(2,1)} %get-tuple-element.31), calls=%async_computation | async-start | bytes 884736 | tf_op jit(solution)/shard_map/all_to_all | solution.py:274
  83.3 7.8 %all-to-all-done = bf16[4,24,2304]{2,1,0:T(8,128)(2,1)} async-done(((bf16[4,24,2304]{2,1,0:T(8,128)(2,1)}), bf16[4,24,2304]{2,1,0:T(8,128)(2,1)}, u32[]{:S(2)}, u32[]{:S(2)}) %all-to-all-start) | async-done | bytes 442400 | tf_op jit(solution)/shard_map/all_to_all | solution.py:274
  91.1 4.1 %all-to-all-start.1 = ((bf16[4,24,2304]{2,1,0:T(8,128)(2,1)}), bf16[4,24,2304]{2,1,0:T(8,128)(2,1)}, u32[]{:S(2)}, u32[]{:S(2)}) async-start(bf16[4,24,2304]{2,1,0:T(8,128)(2,1)} %get-tuple-element.30), calls=%async_computation.1 | async-start | bytes 884736 | tf_op jit(solution)/shard_map/all_to_all | solution.py:275
  95.2 1.5 collective-permute-start
  96.8 6.4 %all-to-all-done.1 = bf16[4,24,2304]{2,1,0:T(8,128)(2,1)} async-done(((bf16[4,24,2304]{2,1,0:T(8,128)(2,1)}), bf16[4,24,2304]{2,1,0:T(8,128)(2,1)}, u32[]{:S(2)}, u32[]{:S(2)}) %all-to-all-start.1) | async-done | bytes 442400 | tf_op jit(solution)/shard_map/all_to_all | solution.py:275
  103.2 1.5 collective-permute-start.1
  104.7 4.2 %fusion.27 = f32[192,720]{1,0:T(8,128)} fusion(bf16[96,2304]{1,0:T(8,128)(2,1)} %bitcast.10, bf16[96,2304]{1,0:T(8,128)(2,1)} %bitcast.9, bf16[1,2,2304,720]{2,3,1,0:T(8,128)(2,1)} %param.26), kind=kOutput, calls=%fused_computation.38 | convolution fusion | flops 638779392 | bytes 4755456 | tf_op jit(solution)/shard_map/dot_general | solution.py:282
  108.9 1.0 constant_dynamic-update-slice_fusion.1
  109.9 5.1 %collective-permute-done.1 = bf16[96,2304]{1,0:T(8,128)(2,1)S(1)} collective-permute-done((bf16[96,2304]{1,0:T(8,128)(2,1)}, bf16[96,2304]{1,0:T(8,128)(2,1)S(1)}, u32[]{:S(2)}, u32[]{:S(2)}) %collective-permute-start.1) | collective-permute-done | bytes 442400 | tf_op jit(solution)/shard_map/ppermute | solution.py:180
  116.7 3.9 %fusion.41 = f32[192,720]{1,0:T(8,128)} fusion(bf16[192,2304]{1,0:T(8,128)(2,1)S(1)} %constant_dynamic-update-slice_fusion, bf16[1,2,2304,720]{2,3,1,0:T(8,128)(2,1)} %param.26), kind=kOutput, calls=%fused_computation.52 | convolution fusion | flops 637009920 | bytes 4755456 | tf_op jit(solution)/shard_map/dot_general | solution.py:282
  120.6 5.6 %convolution_convert_fusion.9 = bf16[192,2304]{1,0:T(8,128)(2,1)} fusion(bf16[1,720,2304]{2,1,0:T(8,128)(2,1)S(1)} %copy-done, f32[192,720]{1,0:T(8,128)} %fusion.41, bf16[192,2304]{1,0:T(8,128)(2,1)} %copy-done.11, bf16[1,2,2304,720]{2,3,1,0:T(8,128)(2,1)} %param.26), kind=kOutput, calls=%fused_computation.10 | convolution fusion | flops 1275291648 | bytes 8994816 | tf_op jit(solution)/shard_map/dot_general | solution.py:285
  126.2 1.5 collective-permute-start.3
  128.3 2.1 fusion.144
  130.4 1.5 collective-permute-start.2
  132.4 7.2 %collective-permute-done.3 = bf16[96,2304]{1,0:T(8,128)(2,1)} collective-permute-done((bf16[96,2304]{1,0:T(8,128)(2,1)}, bf16[96,2304]{1,0:T(8,128)(2,1)}, u32[]{:S(2)}, u32[]{:S(2)}) %collective-permute-start.3) | collective-permute-done | bytes 442400 | tf_op jit(solution)/shard_map/ppermute | solution.py:180
  143.0 3.9 %fusion.39 = f32[192,720]{1,0:T(8,128)} fusion(bf16[192,2304]{1,0:T(8,128)(2,1)S(1)} %constant_dynamic-update-slice_fusion.2, bf16[1,2,2304,720]{2,3,1,0:T(8,128)(2,1)} %param.26), kind=kOutput, calls=%fused_computation.50 | convolution fusion | flops 637009920 | bytes 4755456 | tf_op jit(solution)/shard_map/dot_general | solution.py:282
  146.9 1.5 collective-permute-start.6
  149.0 5.6 %convolution_convert_fusion.8 = bf16[192,2304]{1,0:T(8,128)(2,1)} fusion(bf16[1,720,2304]{2,1,0:T(8,128)(2,1)S(1)} %copy-done, f32[192,720]{1,0:T(8,128)} %fusion.39, bf16[192,2304]{1,0:T(8,128)(2,1)} %copy-done.6, bf16[1,2,2304,720]{2,3,1,0:T(8,128)(2,1)} %param.26), kind=kOutput, calls=%fused_computation.9 | convolution fusion | flops 1275291648 | bytes 8994816 | tf_op jit(solution)/shard_map/dot_general | solution.py:285
  154.6 2.6 add_convert_fusion.13
  157.1 1.5 collective-permute-start.5
  159.2 1.0 constant_dynamic-update-slice_fusion.5
  160.2 1.0 constant_dynamic-update-slice_fusion.4
  162.2 3.9 %fusion.37 = f32[192,720]{1,0:T(8,128)} fusion(bf16[192,2304]{1,0:T(8,128)(2,1)S(1)} %constant_dynamic-update-slice_fusion.4, bf16[1,2,2304,720]{2,3,1,0:T(8,128)(2,1)} %param.26), kind=kOutput, calls=%fused_computation.48 | convolution fusion | flops 637009920 | bytes 4755456 | tf_op jit(solution)/shard_map/dot_general | solution.py:282
  166.1 1.5 collective-permute-start.9
  168.1 5.6 %convolution_convert_fusion.7 = bf16[192,2304]{1,0:T(8,128)(2,1)} fusion(bf16[1,720,2304]{2,1,0:T(8,128)(2,1)S(1)} %copy-done, f32[192,720]{1,0:T(8,128)} %fusion.37, bf16[192,2304]{1,0:T(8,128)(2,1)} %copy-done.7, bf16[1,2,2304,720]{2,3,1,0:T(8,128)(2,1)} %param.26), kind=kOutput, calls=%fused_computation.8 | convolution fusion | flops 1275291648 | bytes 8994816 | tf_op jit(solution)/shard_map/dot_general | solution.py:285
  173.7 2.5 add_convert_fusion.12
  176.3 1.5 collective-permute-start.8
  181.6 3.9 %fusion.35 = f32[192,720]{1,0:T(8,128)} fusion(bf16[192,2304]{1,0:T(8,128)(2,1)S(1)} %constant_dynamic-update-slice_fusion.6, bf16[1,2,2304,720]{2,3,1,0:T(8,128)(2,1)} %param.26), kind=kOutput, calls=%fused_computation.46 | convolution fusion | flops 637009920 | bytes 4755456 | tf_op jit(solution)/shard_map/dot_general | solution.py:282
  185.4 1.6 collective-permute-start.12
  187.5 5.6 %convolution_convert_fusion.6 = bf16[192,2304]{1,0:T(8,128)(2,1)} fusion(bf16[1,720,2304]{2,1,0:T(8,128)(2,1)S(1)} %copy-done, f32[192,720]{1,0:T(8,128)} %fusion.35, bf16[192,2304]{1,0:T(8,128)(2,1)} %copy-done.8, bf16[1,2,2304,720]{2,3,1,0:T(8,128)(2,1)} %param.26), kind=kOutput, calls=%fused_computation.7 | convolution fusion | flops 1275291648 | bytes 8994816 | tf_op jit(solution)/shard_map/dot_general | solution.py:285
  193.1 2.5 add_convert_fusion.11
  195.6 1.6 collective-permute-start.11
  201.3 3.9 %fusion.33 = f32[192,720]{1,0:T(8,128)} fusion(bf16[192,2304]{1,0:T(8,128)(2,1)S(1)} %constant_dynamic-update-slice_fusion.8, bf16[1,2,2304,720]{2,3,1,0:T(8,128)(2,1)} %param.26), kind=kOutput, calls=%fused_computation.44 | convolution fusion | flops 637009920 | bytes 4755456 | tf_op jit(solution)/shard_map/dot_general | solution.py:282
  205.2 1.6 collective-permute-start.15
  207.3 5.6 %convolution_convert_fusion.5 = bf16[192,2304]{1,0:T(8,128)(2,1)} fusion(bf16[1,720,2304]{2,1,0:T(8,128)(2,1)S(1)} %copy-done, f32[192,720]{1,0:T(8,128)} %fusion.33, bf16[192,2304]{1,0:T(8,128)(2,1)} %copy-done.9, bf16[1,2,2304,720]{2,3,1,0:T(8,128)(2,1)} %param.26), kind=kOutput, calls=%fused_computation.6 | convolution fusion | flops 1275291648 | bytes 8994816 | tf_op jit(solution)/shard_map/dot_general | solution.py:285
  212.9 2.6 add_convert_fusion.10
  215.5 1.6 collective-permute-start.14
  221.6 3.9 %fusion.31 = f32[192,720]{1,0:T(8,128)} fusion(bf16[192,2304]{1,0:T(8,128)(2,1)S(1)} %constant_dynamic-update-slice_fusion.10, bf16[1,2,2304,720]{2,3,1,0:T(8,128)(2,1)} %param.26), kind=kOutput, calls=%fused_computation.42 | convolution fusion | flops 637009920 | bytes 4755456 | tf_op jit(solution)/shard_map/dot_general | solution.py:282
  225.5 1.4 collective-permute-start.18
  227.6 5.6 %convolution_convert_fusion.4 = bf16[192,2304]{1,0:T(8,128)(2,1)} fusion(bf16[1,720,2304]{2,1,0:T(8,128)(2,1)S(1)} %copy-done, f32[192,720]{1,0:T(8,128)} %fusion.31, bf16[192,2304]{1,0:T(8,128)(2,1)} %copy-done.10, bf16[1,2,2304,720]{2,3,1,0:T(8,128)(2,1)} %param.26), kind=kOutput, calls=%fused_computation.5 | convolution fusion | flops 1275291648 | bytes 8994816 | tf_op jit(solution)/shard_map/dot_general | solution.py:285
  233.2 2.5 add_convert_fusion.9
  235.7 1.4 collective-permute-start.17
  241.6 3.9 %fusion.29 = f32[192,720]{1,0:T(8,128)} fusion(bf16[192,2304]{1,0:T(8,128)(2,1)S(1)} %constant_dynamic-update-slice_fusion.12, bf16[1,2,2304,720]{2,3,1,0:T(8,128)(2,1)} %param.26), kind=kOutput, calls=%fused_computation.40 | convolution fusion | flops 637009920 | bytes 4755456 | tf_op jit(solution)/shard_map/dot_general | solution.py:282
  245.5 5.6 %convolution_convert_fusion.3 = bf16[192,2304]{1,0:T(8,128)(2,1)} fusion(bf16[1,720,2304]{2,1,0:T(8,128)(2,1)S(1)} %copy-done, f32[192,720]{1,0:T(8,128)} %fusion.29, bf16[192,2304]{1,0:T(8,128)(2,1)} %copy-done.5, bf16[1,2,2304,720]{2,3,1,0:T(8,128)(2,1)} %param.26), kind=kOutput, calls=%fused_computation.4 | convolution fusion | flops 1275291648 | bytes 8994816 | tf_op jit(solution)/shard_map/dot_general | solution.py:285
  251.1 2.5 add_convert_fusion.8
  253.6 1.4 collective-permute-start.20
  255.7 5.6 %convolution_convert_fusion.2 = bf16[192,2304]{1,0:T(8,128)(2,1)} fusion(bf16[1,720,2304]{2,1,0:T(8,128)(2,1)S(1)} %copy-done, f32[192,720]{1,0:T(8,128)} %fusion.27, bf16[96,2304]{1,0:T(8,128)(2,1)} %bitcast.10, bf16[96,2304]{1,0:T(8,128)(2,1)} %bitcast.9, bf16[1,2,2304,720]{2,3,1,0:T(8,128)(2,1)} %param.26), kind=kOutput, calls=%fused_computation.3 | convolution fusion | flops 1277061120 | bytes 8994816 | tf_op jit(solution)/shard_map/dot_general | solution.py:285
  262.3 1.4 collective-permute-done.27
  263.6 2.5 add_convert_fusion.7
  266.2 4.1 %all-to-all-start.3 = ((bf16[4,24,2304]{2,1,0:T(8,128)(2,1)}), bf16[4,24,2304]{2,1,0:T(8,128)(2,1)}, u32[]{:S(2)}, u32[]{:S(2)}) async-start(bf16[4,24,2304]{2,1,0:T(8,128)(2,1)} %bitcast.171), calls=%async_computation.3 | async-start | bytes 884736 | tf_op jit(solution)/shard_map/all_to_all | solution.py:295
  270.3 2.2 fusion
  272.6 1.1 fusion.146
  273.7 4.6 %all-to-all-done.3 = bf16[4,24,2304]{2,1,0:T(8,128)(2,1)} async-done(((bf16[4,24,2304]{2,1,0:T(8,128)(2,1)}), bf16[4,24,2304]{2,1,0:T(8,128)(2,1)}, u32[]{:S(2)}, u32[]{:S(2)}) %all-to-all-start.3) | async-done | bytes 442400 | tf_op jit(solution)/shard_map/all_to_all | solution.py:295
  278.3 4.1 %all-to-all-start.2 = ((bf16[4,24,2304]{2,1,0:T(8,128)(2,1)}), bf16[4,24,2304]{2,1,0:T(8,128)(2,1)}, u32[]{:S(2)}, u32[]{:S(2)}) async-start(bf16[4,24,2304]{2,1,0:T(8,128)(2,1)} %bitcast.170), calls=%async_computation.2 | async-start | bytes 884736 | tf_op jit(solution)/shard_map/all_to_all | solution.py:288
  282.5 8.0 %all-to-all-done.2 = bf16[4,24,2304]{2,1,0:T(8,128)(2,1)} async-done(((bf16[4,24,2304]{2,1,0:T(8,128)(2,1)}), bf16[4,24,2304]{2,1,0:T(8,128)(2,1)}, u32[]{:S(2)}, u32[]{:S(2)}) %all-to-all-start.2) | async-done | bytes 442400 | tf_op jit(solution)/shard_map/all_to_all | solution.py:288
  290.5 1.3 pad_maximum_fusion.1
  (111 shorter events, 38.7 us)
Async XLA Ops:
  7.2 113.5 %copy-start = (bf16[1,720,2304]{2,1,0:T(8,128)(2,1)S(1)}, bf16[1,720,2304]{2,1,0:T(8,128)(2,1)}, u32[]{:S(2)}) copy-start(bf16[1,720,2304]{2,1,0:T(8,128)(2,1)} %param.27) | copy-start | bytes 9953284
  7.2 42.6 %all-gather.2.cloned.1.call-start = ((), (), s32[]{:S(2)}) async-start(), calls=%async_computation.4 | async-start | bytes 5898240 | tf_op jit(solution)/shard_map/all_gather | solution.py:228
  63.7 8.1 %copy-start.13 = (f32[2304]{0:T(1024)S(1)}, f32[2304]{0:T(1024)}, u32[]{:S(2)}) copy-start(f32[2304]{0:T(1024)} %param.23) | copy-start | bytes 27652
  71.0 0.8 copy-start.1
  71.9 0.7 copy-start.3
  73.8 21.4 %copy-start.14 = (s32[64,2]{0,1:T(2,128)S(1)}, s32[64,2]{0,1:T(2,128)}, u32[]{:S(2)}) copy-start(s32[64,2]{0,1:T(2,128)} %param.25) | copy-start | bytes 1540
  78.9 12.1 %all-to-all-start = ((bf16[4,24,2304]{2,1,0:T(8,128)(2,1)}), bf16[4,24,2304]{2,1,0:T(8,128)(2,1)}, u32[]{:S(2)}, u32[]{:S(2)}) async-start(bf16[4,24,2304]{2,1,0:T(8,128)(2,1)} %get-tuple-element.31), calls=%async_computation | async-start | bytes 884736 | tf_op jit(solution)/shard_map/all_to_all | solution.py:274
  91.1 12.1 %all-to-all-start.1 = ((bf16[4,24,2304]{2,1,0:T(8,128)(2,1)}), bf16[4,24,2304]{2,1,0:T(8,128)(2,1)}, u32[]{:S(2)}, u32[]{:S(2)}) async-start(bf16[4,24,2304]{2,1,0:T(8,128)(2,1)} %get-tuple-element.30), calls=%async_computation.1 | async-start | bytes 884736 | tf_op jit(solution)/shard_map/all_to_all | solution.py:275
  95.2 13.7 %collective-permute-start = (bf16[96,2304]{1,0:T(8,128)(2,1)}, bf16[96,2304]{1,0:T(8,128)(2,1)}, u32[]{:S(2)}, u32[]{:S(2)}) collective-permute-start(bf16[96,2304]{1,0:T(8,128)(2,1)} %bitcast.9), channel_id=1, source_target_pairs={{0,4},{4,12},{12,20},{20,28},{28,24},{24,16},{16,8},{8,0},{1,5},{5... | collective-permute-start | bytes 1327112 | tf_op jit(solution)/shard_map/ppermute | solution.py:180
  103.2 11.8 %collective-permute-start.1 = (bf16[96,2304]{1,0:T(8,128)(2,1)}, bf16[96,2304]{1,0:T(8,128)(2,1)S(1)}, u32[]{:S(2)}, u32[]{:S(2)}) collective-permute-start(bf16[96,2304]{1,0:T(8,128)(2,1)} %bitcast.10), channel_id=1, source_target_pairs={{0,8},{4,0},{12,4},{20,12},{28,20},{24,28},{16,24},{8,16},{1,9},{5... | collective-permute-start | bytes 1327112 | tf_op jit(solution)/shard_map/ppermute | solution.py:180
  115.0 0.8 copy-start.4
  115.8 0.9 copy-start.11
  126.2 13.4 %collective-permute-start.3 = (bf16[96,2304]{1,0:T(8,128)(2,1)}, bf16[96,2304]{1,0:T(8,128)(2,1)}, u32[]{:S(2)}, u32[]{:S(2)}) collective-permute-start(bf16[96,2304]{1,0:T(8,128)(2,1)} %collective-permute-done), channel_id=1, source_target_pairs={{0,4},{4,12},{12,20},{20,28},{28,24},{24,16},{16,8},{8,0},{1,5},{5... | collective-permute-start | bytes 1327112 | tf_op jit(solution)/shard_map/ppermute | solution.py:180
  127.7 13.4 %collective-permute-start.4 = (bf16[96,2304]{1,0:T(8,128)(2,1)}, bf16[96,2304]{1,0:T(8,128)(2,1)}, u32[]{:S(2)}, u32[]{:S(2)}) collective-permute-start(bf16[96,2304]{1,0:T(8,128)(2,1)} %copy-done.4), channel_id=1, source_target_pairs={{0,8},{4,0},{12,4},{20,12},{28,20},{24,28},{16,24},{8,16},{1,9},{5... | collective-permute-start | bytes 1327112 | tf_op jit(solution)/shard_map/ppermute | solution.py:180
  130.4 24.2 %collective-permute-start.2 = (bf16[96,2304]{1,0:T(8,128)(2,1)}, bf16[96,2304]{1,0:T(8,128)(2,1)}, u32[]{:S(2)}, u32[]{:S(2)}) collective-permute-start(bf16[96,2304]{1,0:T(8,128)(2,1)} %get-tuple-element.28), channel_id=1, source_target_pairs={{0,4},{4,12},{12,20},{20,28},{28,24},{24,16},{16,8},{8,0},{1,5},{5... | collective-permute-start | bytes 1327112 | tf_op jit(solution)/shard_map/ppermute | solution.py:190
  131.9 22.7 %collective-permute-start.21 = (bf16[96,2304]{1,0:T(8,128)(2,1)}, bf16[96,2304]{1,0:T(8,128)(2,1)}, u32[]{:S(2)}, u32[]{:S(2)}) collective-permute-start(bf16[96,2304]{1,0:T(8,128)(2,1)} %get-tuple-element.29), channel_id=1, source_target_pairs={{0,8},{4,0},{12,4},{20,12},{28,20},{24,28},{16,24},{8,16},{1,9},{5... | collective-permute-start | bytes 1327112 | tf_op jit(solution)/shard_map/ppermute | solution.py:190
  142.1 0.9 copy-start.6
  146.9 12.3 %collective-permute-start.6 = (bf16[96,2304]{1,0:T(8,128)(2,1)}, bf16[96,2304]{1,0:T(8,128)(2,1)}, u32[]{:S(2)}, u32[]{:S(2)}) collective-permute-start(bf16[96,2304]{1,0:T(8,128)(2,1)} %collective-permute-done.3), channel_id=1, source_target_pairs={{0,4},{4,12},{12,20},{20,28},{28,24},{24,16},{16,8},{8,0},{1,5},{5... | collective-permute-start | bytes 1327112 | tf_op jit(solution)/shard_map/ppermute | solution.py:180
  148.4 11.8 %collective-permute-start.7 = (bf16[96,2304]{1,0:T(8,128)(2,1)}, bf16[96,2304]{1,0:T(8,128)(2,1)}, u32[]{:S(2)}, u32[]{:S(2)}) collective-permute-start(bf16[96,2304]{1,0:T(8,128)(2,1)} %collective-permute-done.4), channel_id=1, source_target_pairs={{0,8},{4,0},{12,4},{20,12},{28,20},{24,28},{16,24},{8,16},{1,9},{5... | collective-permute-start | bytes 1327112 | tf_op jit(solution)/shard_map/ppermute | solution.py:180
  157.1 16.6 %collective-permute-start.5 = (bf16[96,2304]{1,0:T(8,128)(2,1)}, bf16[96,2304]{1,0:T(8,128)(2,1)}, u32[]{:S(2)}, u32[]{:S(2)}) collective-permute-start(bf16[96,2304]{1,0:T(8,128)(2,1)} %get-tuple-element.26), channel_id=1, source_target_pairs={{0,4},{4,12},{12,20},{20,28},{28,24},{24,16},{16,8},{8,0},{1,5},{5... | collective-permute-start | bytes 1327112 | tf_op jit(solution)/shard_map/ppermute | solution.py:190
  158.6 15.1 %collective-permute-start.22 = (bf16[96,2304]{1,0:T(8,128)(2,1)}, bf16[96,2304]{1,0:T(8,128)(2,1)}, u32[]{:S(2)}, u32[]{:S(2)}) collective-permute-start(bf16[96,2304]{1,0:T(8,128)(2,1)} %get-tuple-element.27), channel_id=1, source_target_pairs={{0,8},{4,0},{12,4},{20,12},{28,20},{24,28},{16,24},{8,16},{1,9},{5... | collective-permute-start | bytes 1327112 | tf_op jit(solution)/shard_map/ppermute | solution.py:190
  161.3 0.9 copy-start.7
  166.1 12.2 %collective-permute-start.9 = (bf16[96,2304]{1,0:T(8,128)(2,1)}, bf16[96,2304]{1,0:T(8,128)(2,1)}, u32[]{:S(2)}, u32[]{:S(2)}) collective-permute-start(bf16[96,2304]{1,0:T(8,128)(2,1)} %collective-permute-done.6), channel_id=1, source_target_pairs={{0,4},{4,12},{12,20},{20,28},{28,24},{24,16},{16,8},{8,0},{1,5},{5... | collective-permute-start | bytes 1327112 | tf_op jit(solution)/shard_map/ppermute | solution.py:180
  167.5 12.1 %collective-permute-start.10 = (bf16[96,2304]{1,0:T(8,128)(2,1)}, bf16[96,2304]{1,0:T(8,128)(2,1)}, u32[]{:S(2)}, u32[]{:S(2)}) collective-permute-start(bf16[96,2304]{1,0:T(8,128)(2,1)} %collective-permute-done.7), channel_id=1, source_target_pairs={{0,8},{4,0},{12,4},{20,12},{28,20},{24,28},{16,24},{8,16},{1,9},{5... | collective-permute-start | bytes 1327112 | tf_op jit(solution)/shard_map/ppermute | solution.py:180
  176.3 16.8 %collective-permute-start.8 = (bf16[96,2304]{1,0:T(8,128)(2,1)}, bf16[96,2304]{1,0:T(8,128)(2,1)}, u32[]{:S(2)}, u32[]{:S(2)}) collective-permute-start(bf16[96,2304]{1,0:T(8,128)(2,1)} %get-tuple-element.24), channel_id=1, source_target_pairs={{0,4},{4,12},{12,20},{20,28},{28,24},{24,16},{16,8},{8,0},{1,5},{5... | collective-permute-start | bytes 1327112 | tf_op jit(solution)/shard_map/ppermute | solution.py:190
  177.7 15.4 %collective-permute-start.23 = (bf16[96,2304]{1,0:T(8,128)(2,1)}, bf16[96,2304]{1,0:T(8,128)(2,1)}, u32[]{:S(2)}, u32[]{:S(2)}) collective-permute-start(bf16[96,2304]{1,0:T(8,128)(2,1)} %get-tuple-element.25), channel_id=1, source_target_pairs={{0,8},{4,0},{12,4},{20,12},{28,20},{24,28},{16,24},{8,16},{1,9},{5... | collective-permute-start | bytes 1327112 | tf_op jit(solution)/shard_map/ppermute | solution.py:190
  180.6 0.9 copy-start.8
  185.4 12.3 %collective-permute-start.12 = (bf16[96,2304]{1,0:T(8,128)(2,1)}, bf16[96,2304]{1,0:T(8,128)(2,1)}, u32[]{:S(2)}, u32[]{:S(2)}) collective-permute-start(bf16[96,2304]{1,0:T(8,128)(2,1)} %collective-permute-done.9), channel_id=1, source_target_pairs={{0,4},{4,12},{12,20},{20,28},{28,24},{24,16},{16,8},{8,0},{1,5},{5... | collective-permute-start | bytes 1327112 | tf_op jit(solution)/shard_map/ppermute | solution.py:180
  187.0 12.4 %collective-permute-start.13 = (bf16[96,2304]{1,0:T(8,128)(2,1)}, bf16[96,2304]{1,0:T(8,128)(2,1)}, u32[]{:S(2)}, u32[]{:S(2)}) collective-permute-start(bf16[96,2304]{1,0:T(8,128)(2,1)} %collective-permute-done.10), channel_id=1, source_target_pairs={{0,8},{4,0},{12,4},{20,12},{28,20},{24,28},{16,24},{8,16},{1,9},{5... | collective-permute-start | bytes 1327112 | tf_op jit(solution)/shard_map/ppermute | solution.py:180
  195.6 17.2 %collective-permute-start.11 = (bf16[96,2304]{1,0:T(8,128)(2,1)}, bf16[96,2304]{1,0:T(8,128)(2,1)}, u32[]{:S(2)}, u32[]{:S(2)}) collective-permute-start(bf16[96,2304]{1,0:T(8,128)(2,1)} %get-tuple-element.22), channel_id=1, source_target_pairs={{0,4},{4,12},{12,20},{20,28},{28,24},{24,16},{16,8},{8,0},{1,5},{5... | collective-permute-start | bytes 1327112 | tf_op jit(solution)/shard_map/ppermute | solution.py:190
  197.2 15.7 %collective-permute-start.24 = (bf16[96,2304]{1,0:T(8,128)(2,1)}, bf16[96,2304]{1,0:T(8,128)(2,1)}, u32[]{:S(2)}, u32[]{:S(2)}) collective-permute-start(bf16[96,2304]{1,0:T(8,128)(2,1)} %get-tuple-element.23), channel_id=1, source_target_pairs={{0,8},{4,0},{12,4},{20,12},{28,20},{24,28},{16,24},{8,16},{1,9},{5... | collective-permute-start | bytes 1327112 | tf_op jit(solution)/shard_map/ppermute | solution.py:190
  200.4 0.9 copy-start.9
  205.2 12.6 %collective-permute-start.15 = (bf16[96,2304]{1,0:T(8,128)(2,1)}, bf16[96,2304]{1,0:T(8,128)(2,1)}, u32[]{:S(2)}, u32[]{:S(2)}) collective-permute-start(bf16[96,2304]{1,0:T(8,128)(2,1)} %collective-permute-done.12), channel_id=1, source_target_pairs={{0,4},{4,12},{12,20},{20,28},{28,24},{24,16},{16,8},{8,0},{1,5},{5... | collective-permute-start | bytes 1327112 | tf_op jit(solution)/shard_map/ppermute | solution.py:180
  206.8 12.8 %collective-permute-start.16 = (bf16[96,2304]{1,0:T(8,128)(2,1)}, bf16[96,2304]{1,0:T(8,128)(2,1)}, u32[]{:S(2)}, u32[]{:S(2)}) collective-permute-start(bf16[96,2304]{1,0:T(8,128)(2,1)} %collective-permute-done.13), channel_id=1, source_target_pairs={{0,8},{4,0},{12,4},{20,12},{28,20},{24,28},{16,24},{8,16},{1,9},{5... | collective-permute-start | bytes 1327112 | tf_op jit(solution)/shard_map/ppermute | solution.py:180
  215.5 17.7 %collective-permute-start.14 = (bf16[96,2304]{1,0:T(8,128)(2,1)}, bf16[96,2304]{1,0:T(8,128)(2,1)}, u32[]{:S(2)}, u32[]{:S(2)}) collective-permute-start(bf16[96,2304]{1,0:T(8,128)(2,1)} %get-tuple-element.20), channel_id=1, source_target_pairs={{0,4},{4,12},{12,20},{20,28},{28,24},{24,16},{16,8},{8,0},{1,5},{5... | collective-permute-start | bytes 1327112 | tf_op jit(solution)/shard_map/ppermute | solution.py:190
  217.1 16.1 %collective-permute-start.25 = (bf16[96,2304]{1,0:T(8,128)(2,1)}, bf16[96,2304]{1,0:T(8,128)(2,1)}, u32[]{:S(2)}, u32[]{:S(2)}) collective-permute-start(bf16[96,2304]{1,0:T(8,128)(2,1)} %get-tuple-element.21), channel_id=1, source_target_pairs={{0,8},{4,0},{12,4},{20,12},{28,20},{24,28},{16,24},{8,16},{1,9},{5... | collective-permute-start | bytes 1327112 | tf_op jit(solution)/shard_map/ppermute | solution.py:190
  220.7 0.9 copy-start.10
  225.5 13.0 %collective-permute-start.18 = (bf16[96,2304]{1,0:T(8,128)(2,1)}, bf16[96,2304]{1,0:T(8,128)(2,1)}, u32[]{:S(2)}, u32[]{:S(2)}) collective-permute-start(bf16[96,2304]{1,0:T(8,128)(2,1)} %collective-permute-done.15), channel_id=1, source_target_pairs={{0,4},{4,12},{12,20},{20,28},{28,24},{24,16},{16,8},{8,0},{1,5},{5... | collective-permute-start | bytes 1327112 | tf_op jit(solution)/shard_map/ppermute | solution.py:180
  227.0 12.7 %collective-permute-start.19 = (bf16[96,2304]{1,0:T(8,128)(2,1)}, bf16[96,2304]{1,0:T(8,128)(2,1)}, u32[]{:S(2)}, u32[]{:S(2)}) collective-permute-start(bf16[96,2304]{1,0:T(8,128)(2,1)} %collective-permute-done.16), channel_id=1, source_target_pairs={{0,8},{4,0},{12,4},{20,12},{28,20},{24,28},{16,24},{8,16},{1,9},{5... | collective-permute-start | bytes 1327112 | tf_op jit(solution)/shard_map/ppermute | solution.py:180
  235.7 15.4 %collective-permute-start.17 = (bf16[96,2304]{1,0:T(8,128)(2,1)}, bf16[96,2304]{1,0:T(8,128)(2,1)}, u32[]{:S(2)}, u32[]{:S(2)}) collective-permute-start(bf16[96,2304]{1,0:T(8,128)(2,1)} %get-tuple-element.18), channel_id=1, source_target_pairs={{0,4},{4,12},{12,20},{20,28},{28,24},{24,16},{16,8},{8,0},{1,5},{5... | collective-permute-start | bytes 1327112 | tf_op jit(solution)/shard_map/ppermute | solution.py:190
  237.2 14.0 %collective-permute-start.26 = (bf16[96,2304]{1,0:T(8,128)(2,1)}, bf16[96,2304]{1,0:T(8,128)(2,1)}, u32[]{:S(2)}, u32[]{:S(2)}) collective-permute-start(bf16[96,2304]{1,0:T(8,128)(2,1)} %get-tuple-element.19), channel_id=1, source_target_pairs={{0,8},{4,0},{12,4},{20,12},{28,20},{24,28},{16,24},{8,16},{1,9},{5... | collective-permute-start | bytes 1327112 | tf_op jit(solution)/shard_map/ppermute | solution.py:190
  240.7 0.9 copy-start.5
  253.6 8.6 %collective-permute-start.20 = (bf16[96,2304]{1,0:T(8,128)(2,1)}, bf16[96,2304]{1,0:T(8,128)(2,1)}, u32[]{:S(2)}, u32[]{:S(2)}) collective-permute-start(bf16[96,2304]{1,0:T(8,128)(2,1)} %get-tuple-element.16), channel_id=1, source_target_pairs={{0,4},{4,12},{12,20},{20,28},{28,24},{24,16},{16,8},{8,0},{1,5},{5... | collective-permute-start | bytes 1327112 | tf_op jit(solution)/shard_map/ppermute | solution.py:192
  255.0 8.6 %collective-permute-start.27 = (bf16[96,2304]{1,0:T(8,128)(2,1)}, bf16[96,2304]{1,0:T(8,128)(2,1)}, u32[]{:S(2)}, u32[]{:S(2)}) collective-permute-start(bf16[96,2304]{1,0:T(8,128)(2,1)} %get-tuple-element.17), channel_id=1, source_target_pairs={{0,8},{4,0},{12,4},{20,12},{28,20},{24,28},{16,24},{8,16},{1,9},{5... | collective-permute-start | bytes 1327112 | tf_op jit(solution)/shard_map/ppermute | solution.py:192
  261.3 11.3 %copy-start.12 = (bf16[2304,4]{0,1:T(4,128)(2,1)S(1)}, bf16[2304,4]{0,1:T(4,128)(2,1)}, u32[]{:S(2)}) copy-start(bf16[2304,4]{0,1:T(4,128)(2,1)} %param.24) | copy-start | bytes 55300
  266.2 12.1 %all-to-all-start.3 = ((bf16[4,24,2304]{2,1,0:T(8,128)(2,1)}), bf16[4,24,2304]{2,1,0:T(8,128)(2,1)}, u32[]{:S(2)}, u32[]{:S(2)}) async-start(bf16[4,24,2304]{2,1,0:T(8,128)(2,1)} %bitcast.171), calls=%async_computation.3 | async-start | bytes 884736 | tf_op jit(solution)/shard_map/all_to_all | solution.py:295
  278.3 12.1 %all-to-all-start.2 = ((bf16[4,24,2304]{2,1,0:T(8,128)(2,1)}), bf16[4,24,2304]{2,1,0:T(8,128)(2,1)}, u32[]{:S(2)}, u32[]{:S(2)}) async-start(bf16[4,24,2304]{2,1,0:T(8,128)(2,1)} %bitcast.170), calls=%async_computation.2 | async-start | bytes 884736 | tf_op jit(solution)/shard_map/all_to_all | solution.py:288
  290.5 1.6 copy-start.2
Sparse Core Ops, SparseCore 0:
  9.5 40.1 all-gather.1

commit v5 on v2

--- a/solution.py
+++ b/solution.py
@@ -256,7 +256,9 @@
     earlier = (assign_ids[None, :] < assign_ids[:, None]).astype(jnp.float32)
     before = jnp.dot(earlier, onehot, precision=HIGH)
     slot_rank = jnp.sum(before * onehot, axis=1).astype(jnp.int32)
-    target = routes.reshape(2 * row_count) * capacity + slot_rank
+    own = lax.axis_index("expert")
+    shift_of = (routes.reshape(2 * row_count) - own) % experts
+    target = shift_of * capacity + slot_rank
     select = (jnp.arange(experts * capacity, dtype=jnp.int32)[:, None] == target[None, :]).astype(
         jnp.bfloat16
     )
@@ -269,11 +271,15 @@
     gate_cols = w_gate_up[0, 0]
     up_cols = w_gate_up[0, 1]
     down_rows = w_down[0]
-    arrived = lax.all_to_all(outgoing, "expert", split_axis=0, concat_axis=0, tiled=True)
-    arrived = arrived.reshape(experts * capacity, features)
+    def shifted(rows, shift):
+        if shift % experts == 0:
+            return rows
+        return lax.ppermute(rows, "expert", [(j, (j + shift) % experts) for j in range(experts)])
+
+    arrived = [shifted(outgoing[shift], shift) for shift in range(experts)]
     half = experts * capacity // 2
-    forward = ring_gather(arrived[:half], ring, 1)
-    backward = ring_gather(arrived[half:], ring, -1)
+    forward = ring_gather(jnp.concatenate(arrived[: experts // 2], axis=0), ring, 1)
+    backward = ring_gather(jnp.concatenate(arrived[experts // 2 :], axis=0), ring, -1)
     forward_out = []
     backward_out = []
     for index in range(len(ring)):
@@ -286,16 +292,12 @@
         backward_out.append(partial[half:])
     summed_rows = jnp.concatenate(
         [ring_reduce(forward_out, ring, 1), ring_reduce(backward_out, ring, -1)], axis=0
-    )
-    returned = lax.all_to_all(
-        summed_rows.reshape(experts, capacity, features).astype(jnp.bfloat16),
-        "expert",
-        split_axis=0,
-        concat_axis=0,
-        tiled=True,
-    ).astype(jnp.float32)
-    flat_back = returned.reshape(experts * capacity, features)
-    fetched = jnp.take(flat_back, target, axis=0).reshape(row_count, 2, features)
+    ).astype(jnp.bfloat16).reshape(experts, capacity, features)
+    flat_back = jnp.concatenate(
+        [shifted(summed_rows[shift], -shift) for shift in range(experts)], axis=0
+    )
+    pick = (target[:, None] == jnp.arange(experts * capacity, dtype=jnp.int32)[None, :]).astype(jnp.bfloat16)
+    fetched = jnp.dot(pick, flat_back, preferred_element_type=jnp.float32).reshape(row_count, 2, features)
     layer_out = (
         middle32 + gate_first[:, None] * fetched[:, 0] + gate_second[:, None] * fetched[:, 1]
     ).astype(jnp.bfloat16)

time: 302 us -> 280 us (0.927)
  waiting for transfers between devices: 61.9 us -> 50.3 us
  other arithmetic: 25.6 us -> 20 us
  starting transfers between devices: 36.9 us -> 33.1 us
    all_to_all x2 -> x0, waiting for transfers between devices: 24.1 us -> none  [the longest x1 12.5 us: local(): lax.all_to_all(outgoing, 'expert', split_axis=0, concat_axis=0, tiled=True)]
    ppermute x0 -> x6, waiting for transfers between devices: none -> 15.1 us  [shifted(): lax.ppermute(rows, 'expert', [(j, (j + shift) % experts) for j in range(e...]
    all_to_all x2 -> x0, starting transfers between devices: 8.45 us -> none  [the longest x1 4.23 us: local(): lax.all_to_all(summed_rows.reshape(experts, capacity, features).astype(jn...]
    gather x2 -> x0, local copies, waits for them, and re-layouts: 7.04 us -> none  [local(): jnp.take(flat_back, target, axis=0).reshape(row_count, 2, features)]
    ppermute x0 -> x6, starting transfers between devices: none -> 3.93 us  [shifted(): lax.ppermute(rows, 'expert', [(j, (j + shift) % experts) for j in range(e...]
    unnamed x42 -> x46, local copies, waits for them, and re-layouts: 15.7 us -> 16.5 us
  transfers between devices with their start and end apart: 31 -> 35, of which waited for: 16 -> 16; matrix products, arithmetic and copies ran while one was open for 35% -> 38% of each run, Pallas kernels for 5% -> 6%
where the time goes in v5:
time: 280 us; the launch traced here: 276 us
  matrix products  89.5 us (32%)
  waiting for transfers between devices  50.3 us (18%)
  local copies, waits for them, and re-layouts  37.9 us (14%)
  starting transfers between devices  33.1 us (12%)
  Pallas kernels  28.4 us (10%)
  other arithmetic  20 us (7%)
  between operations  16.4 us (6%)
    dot_general x8, matrix products, local(): jnp.dot(hidden_units, down_rows, preferred_element_type=jnp.float32)  44.8 us
    dot_general x8, matrix products, local(): gate_act = jnp.dot(pooled, gate_cols, preferred_element_type=jnp.float32)  29.2 us
    pallas_call x2, Pallas kernels, attend(): pl.pallas_call(functools.partial(attend_kernel, count=len(sources), scale...  28.4 us
    unnamed x46, local copies, waits for them, and re-layouts  16.5 us
    ppermute x14, waiting for transfers between devices, ring_gather(): piece = lax.ppermute(piece, 'dp', pairs)  16.2 us
    all_gather x1, waiting for transfers between devices, local(): shard_rows = lax.all_gather(prompt_kv, 'expert', axis=1, tiled=True)  16.1 us
    convert_element_type x6, other arithmetic, ring_reduce(): moving = (received + blocks[index].astype(jnp.float32)).astype(jnp.bfloat16)  15.2 us
    ppermute x6, waiting for transfers between devices, shifted(): lax.ppermute(rows, 'expert', [(j, (j + shift) % experts) for j in range(e...  15.1 us
  transfers between devices with their start and end apart: 35, of which 16 were waited for; matrix products, arithmetic and copies ran while one was open for 38% of the time, Pallas kernels for 6%

profile of v5, /device:TPU:0, one launch (start us, length us, event | category | flops | bytes accessed | tf_op | source)
XLA Modules:
  0.0 275.5 jit_solution(17163175593806111303)
XLA Ops:
  7.9 1.9 slice.111.refs_0_
  15.8 15.2 %shard_map.152 = (f32[64,2304]{1,0:T(8,128)}, f32[64,2304]{1,0:T(8,128)}, f32[64,2304]{1,0:T(8,128)}) custom-call(bf16[64,2304]{1,0:T(8,128)(2,1)} %slice.111.refs_0_, bf16[512,4608]{1,0:T(8,128)(2,1)} %bitcast.150, bf16[512,4608]{1,0:T(8,128)(2,1)} %bitcast.151, f32[64,512]{1,0:T(8,128)} %broadcast_in_dim.32.refs_3_, bf16[64,6912]{1,0:T(8,128)(2,1)} %refs_5_.1, ...), custom_call_target="tpu_custom_call" | custom-call | tf_op jit(solution)/shard_map/pallas_call | solution.py:141
  31.4 2.3 fusion
  33.7 16.1 %all-gather.2.cloned.1.call-done = bf16[1,512,4608]{2,1,0:T(8,128)(2,1)} async-done(((bf16[1,128,4608]{2,1,0:T(8,128)(2,1)}), bf16[1,512,4608]{2,1,0:T(8,128)(2,1)}) %all-gather.2.cloned.1.call-update) | async-done | bytes 4718608 | tf_op jit(solution)/shard_map/all_gather | solution.py:228
  50.4 13.3 %shard_map.153 = (f32[64,2304]{1,0:T(8,128)}, f32[64,2304]{1,0:T(8,128)}, f32[64,2304]{1,0:T(8,128)}) custom-call(bf16[64,2304]{1,0:T(8,128)(2,1)} %slice.111.refs_0_, bf16[512,4608]{1,0:T(8,128)(2,1)} %bitcast.152, bf16[512,4608]{1,0:T(8,128)(2,1)} %bitcast.153, f32[64,512]{1,0:T(8,128)} %broadcast_in_dim.33.refs_3_), custom_call_target="tpu_custom_call" | custom-call | tf_op jit(solution)/shard_map/pallas_call | solution.py:141
  63.7 7.3 %multiply_reduce_fusion = (f32[64]{0:T(128)S(1)}, f32[64,2304]{1,0:T(8,128)S(1)}) fusion(bf16[2304,2304]{1,0:T(8,128)(2,1)} %param.22, f32[64,2304]{1,0:T(8,128)} %get-tuple-element.13, f32[64,2304]{1,0:T(8,128)} %get-tuple-element.12, f32[64,2304]{1,0:T(8,128)} %get-tuple-element.11, f32[64,2304]{1,0:T(8,128)} %get-tuple-element.10, ...), kind=kOutput, calls=%fused_computation.107 | convolution fusion | flops 681983936 | bytes 15040768 | tf_op jit(solution)/shard_map/dot_general | solution.py:241
  72.7 1.1 broadcast_in_dim.36
  73.8 2.7 reshape.309
  76.5 1.4 convolution_convert_fusion.1
  78.4 1.5 collective-permute-start.3
  80.2 1.1 fusion.148
  81.3 3.9 %collective-permute-done = bf16[48,2304]{1,0:T(8,128)(2,1)S(1)} collective-permute-done((bf16[48,2304]{1,0:T(8,128)(2,1)S(1)}, bf16[48,2304]{1,0:T(8,128)(2,1)S(1)}, u32[]{:S(2)}, u32[]{:S(2)}) %collective-permute-start) | collective-permute-done | bytes 221216 | tf_op jit(solution)/shard_map/ppermute | solution.py:277
  85.3 1.2 collective-permute-start.1
  86.5 4.1 %collective-permute-done.2 = bf16[48,2304]{1,0:T(8,128)(2,1)S(1)} collective-permute-done((bf16[48,2304]{1,0:T(8,128)(2,1)S(1)}, bf16[48,2304]{1,0:T(8,128)(2,1)S(1)}, u32[]{:S(2)}, u32[]{:S(2)}) %collective-permute-start.2) | collective-permute-done | bytes 221216 | tf_op jit(solution)/shard_map/ppermute | solution.py:277
  90.6 1.5 collective-permute-start.4
  92.2 3.9 %fusion.27 = f32[192,720]{1,0:T(8,128)} fusion(bf16[1,2,2304,720]{2,3,1,0:T(8,128)(2,1)} %param.26, bf16[48,2304]{1,0:T(8,128)(2,1)S(1)} %collective-permute-done.3, bf16[48,2304]{1,0:T(8,128)(2,1)S(1)} %collective-permute-done.2, bf16[48,2304]{1,0:T(8,128)(2,1)S(1)} %collective-permute-done, bf16[48,2304]{1,0:T(8,128)(2,1)S(1)} %get-tuple-element.35), kind=kOutput, calls=%fused_computation.38 | convolution fusion | flops 640548864 | bytes 4755456 | tf_op jit(solution)/shard_map/dot_general | solution.py:287
  96.9 5.4 %collective-permute-done.4 = bf16[96,2304]{1,0:T(8,128)(2,1)S(1)} collective-permute-done((bf16[96,2304]{1,0:T(8,128)(2,1)S(1)}, bf16[96,2304]{1,0:T(8,128)(2,1)S(1)}, u32[]{:S(2)}, u32[]{:S(2)}) %collective-permute-start.4) | collective-permute-done | bytes 442400 | tf_op jit(solution)/shard_map/ppermute | solution.py:180
  104.0 2.0 fusion.41
  106.0 5.6 %convolution_convert_fusion.9 = bf16[192,2304]{1,0:T(8,128)(2,1)} fusion(bf16[1,720,2304]{2,1,0:T(8,128)(2,1)S(1)} %copy-done, f32[192,720]{1,0:T(8,128)} %fusion.41, bf16[192,2304]{1,0:T(8,128)(2,1)} %copy-done.9, bf16[1,2,2304,720]{2,3,1,0:T(8,128)(2,1)} %param.26), kind=kOutput, calls=%fused_computation.10 | convolution fusion | flops 1275291648 | bytes 8994816 | tf_op jit(solution)/shard_map/dot_general | solution.py:290
  111.6 1.2 collective-permute-start.6
  113.6 2.1 fusion.144
  115.7 1.2 collective-permute-start.5
  117.8 7.2 %collective-permute-done.6 = bf16[96,2304]{1,0:T(8,128)(2,1)} collective-permute-done((bf16[96,2304]{1,0:T(8,128)(2,1)}, bf16[96,2304]{1,0:T(8,128)(2,1)}, u32[]{:S(2)}, u32[]{:S(2)}) %collective-permute-start.6) | collective-permute-done | bytes 442400 | tf_op jit(solution)/shard_map/ppermute | solution.py:180
  128.1 3.9 %fusion.39 = f32[192,720]{1,0:T(8,128)} fusion(bf16[192,2304]{1,0:T(8,128)(2,1)S(1)} %constant_dynamic-update-slice_fusion.2, bf16[1,2,2304,720]{2,3,1,0:T(8,128)(2,1)} %param.26), kind=kOutput, calls=%fused_computation.50 | convolution fusion | flops 637009920 | bytes 4755456 | tf_op jit(solution)/shard_map/dot_general | solution.py:287
  132.0 1.5 collective-permute-start.9
  134.0 5.6 %convolution_convert_fusion.8 = bf16[192,2304]{1,0:T(8,128)(2,1)} fusion(bf16[1,720,2304]{2,1,0:T(8,128)(2,1)S(1)} %copy-done, f32[192,720]{1,0:T(8,128)} %fusion.39, bf16[192,2304]{1,0:T(8,128)(2,1)} %copy-done.10, bf16[1,2,2304,720]{2,3,1,0:T(8,128)(2,1)} %param.26), kind=kOutput, calls=%fused_computation.9 | convolution fusion | flops 1275291648 | bytes 8994816 | tf_op jit(solution)/shard_map/dot_general | solution.py:290
  139.6 2.5 add_convert_fusion.13
  142.1 1.5 collective-permute-start.8
  144.2 1.0 constant_dynamic-update-slice_fusion.5
  145.2 1.0 constant_dynamic-update-slice_fusion.4
  147.2 3.9 %fusion.37 = f32[192,720]{1,0:T(8,128)} fusion(bf16[192,2304]{1,0:T(8,128)(2,1)S(1)} %constant_dynamic-update-slice_fusion.4, bf16[1,2,2304,720]{2,3,1,0:T(8,128)(2,1)} %param.26), kind=kOutput, calls=%fused_computation.48 | convolution fusion | flops 637009920 | bytes 4755456 | tf_op jit(solution)/shard_map/dot_general | solution.py:287
  151.1 1.5 collective-permute-start.12
  153.1 5.6 %convolution_convert_fusion.7 = bf16[192,2304]{1,0:T(8,128)(2,1)} fusion(bf16[1,720,2304]{2,1,0:T(8,128)(2,1)S(1)} %copy-done, f32[192,720]{1,0:T(8,128)} %fusion.37, bf16[192,2304]{1,0:T(8,128)(2,1)} %copy-done.11, bf16[1,2,2304,720]{2,3,1,0:T(8,128)(2,1)} %param.26), kind=kOutput, calls=%fused_computation.8 | convolution fusion | flops 1275291648 | bytes 8994816 | tf_op jit(solution)/shard_map/dot_general | solution.py:290
  158.7 2.5 add_convert_fusion.12
  161.3 1.5 collective-permute-start.11
  167.2 3.9 %fusion.35 = f32[192,720]{1,0:T(8,128)} fusion(bf16[192,2304]{1,0:T(8,128)(2,1)S(1)} %constant_dynamic-update-slice_fusion.6, bf16[1,2,2304,720]{2,3,1,0:T(8,128)(2,1)} %param.26), kind=kOutput, calls=%fused_computation.46 | convolution fusion | flops 637009920 | bytes 4755456 | tf_op jit(solution)/shard_map/dot_general | solution.py:287
  171.1 1.6 collective-permute-start.15
  173.1 5.6 %convolution_convert_fusion.6 = bf16[192,2304]{1,0:T(8,128)(2,1)} fusion(bf16[1,720,2304]{2,1,0:T(8,128)(2,1)S(1)} %copy-done, f32[192,720]{1,0:T(8,128)} %fusion.35, bf16[192,2304]{1,0:T(8,128)(2,1)} %copy-done.12, bf16[1,2,2304,720]{2,3,1,0:T(8,128)(2,1)} %param.26), kind=kOutput, calls=%fused_computation.7 | convolution fusion | flops 1275291648 | bytes 8994816 | tf_op jit(solution)/shard_map/dot_general | solution.py:290
  178.7 2.5 add_convert_fusion.11
  181.3 1.6 collective-permute-start.14
  187.3 3.9 %fusion.33 = f32[192,720]{1,0:T(8,128)} fusion(bf16[192,2304]{1,0:T(8,128)(2,1)S(1)} %constant_dynamic-update-slice_fusion.8, bf16[1,2,2304,720]{2,3,1,0:T(8,128)(2,1)} %param.26), kind=kOutput, calls=%fused_computation.44 | convolution fusion | flops 637009920 | bytes 4755456 | tf_op jit(solution)/shard_map/dot_general | solution.py:287
  191.1 1.1 collective-permute-start.18
  193.2 5.6 %convolution_convert_fusion.5 = bf16[192,2304]{1,0:T(8,128)(2,1)} fusion(bf16[1,720,2304]{2,1,0:T(8,128)(2,1)S(1)} %copy-done, f32[192,720]{1,0:T(8,128)} %fusion.33, bf16[192,2304]{1,0:T(8,128)(2,1)} %copy-done.13, bf16[1,2,2304,720]{2,3,1,0:T(8,128)(2,1)} %param.26), kind=kOutput, calls=%fused_computation.6 | convolution fusion | flops 1275291648 | bytes 8994816 | tf_op jit(solution)/shard_map/dot_general | solution.py:290
  198.8 2.6 add_convert_fusion.10
  201.3 1.1 collective-permute-start.17
  207.5 3.9 %fusion.31 = f32[192,720]{1,0:T(8,128)} fusion(bf16[192,2304]{1,0:T(8,128)(2,1)S(1)} %constant_dynamic-update-slice_fusion.10, bf16[1,2,2304,720]{2,3,1,0:T(8,128)(2,1)} %param.26), kind=kOutput, calls=%fused_computation.42 | convolution fusion | flops 637009920 | bytes 4755456 | tf_op jit(solution)/shard_map/dot_general | solution.py:287
  211.4 1.3 collective-permute-start.21
  213.4 5.6 %convolution_convert_fusion.4 = bf16[192,2304]{1,0:T(8,128)(2,1)} fusion(bf16[1,720,2304]{2,1,0:T(8,128)(2,1)S(1)} %copy-done, f32[192,720]{1,0:T(8,128)} %fusion.31, bf16[192,2304]{1,0:T(8,128)(2,1)} %copy-done.14, bf16[1,2,2304,720]{2,3,1,0:T(8,128)(2,1)} %param.26), kind=kOutput, calls=%fused_computation.5 | convolution fusion | flops 1275291648 | bytes 8994816 | tf_op jit(solution)/shard_map/dot_general | solution.py:290
  219.0 2.5 add_convert_fusion.9
  221.6 1.3 collective-permute-start.20
  227.1 3.9 %fusion.29 = f32[192,720]{1,0:T(8,128)} fusion(bf16[192,2304]{1,0:T(8,128)(2,1)S(1)} %constant_dynamic-update-slice_fusion.12, bf16[1,2,2304,720]{2,3,1,0:T(8,128)(2,1)} %param.26), kind=kOutput, calls=%fused_computation.40 | convolution fusion | flops 637009920 | bytes 4755456 | tf_op jit(solution)/shard_map/dot_general | solution.py:287
  231.0 5.6 %convolution_convert_fusion.3 = bf16[192,2304]{1,0:T(8,128)(2,1)} fusion(bf16[1,720,2304]{2,1,0:T(8,128)(2,1)S(1)} %copy-done, f32[192,720]{1,0:T(8,128)} %fusion.29, bf16[192,2304]{1,0:T(8,128)(2,1)} %copy-done.8, bf16[1,2,2304,720]{2,3,1,0:T(8,128)(2,1)} %param.26), kind=kOutput, calls=%fused_computation.4 | convolution fusion | flops 1275291648 | bytes 8994816 | tf_op jit(solution)/shard_map/dot_general | solution.py:290
  236.6 2.5 add_convert_fusion.8
  239.1 1.3 collective-permute-start.23
  241.1 5.6 %convolution_convert_fusion.2 = bf16[192,2304]{1,0:T(8,128)(2,1)} fusion(bf16[1,720,2304]{2,1,0:T(8,128)(2,1)S(1)} %copy-done, f32[192,720]{1,0:T(8,128)} %fusion.27, bf16[1,2,2304,720]{2,3,1,0:T(8,128)(2,1)} %param.26, bf16[48,2304]{1,0:T(8,128)(2,1)} %copy-done.6, bf16[48,2304]{1,0:T(8,128)(2,1)} %copy-done.7, bf16[48,2304]{1,0:T(8,128)(2,1)} %copy-done.5, ...), kind=kOutput, calls=%fused_computation.3 | convolution fusion | flops 1278830592 | bytes 8994816 | tf_op jit(solution)/shard_map/dot_general | solution.py:290
  247.7 1.3 collective-permute-done.31
  249.1 1.6 add_convert_fusion.7
  250.9 1.7 collective-permute-start.24
  252.6 5.2 %collective-permute-done.33 = bf16[48,2304]{1,0:T(8,128)(2,1)S(1)} collective-permute-done((bf16[48,2304]{1,0:T(8,128)(2,1)S(1)}, bf16[48,2304]{1,0:T(8,128)(2,1)S(1)}, u32[]{:S(2)}, u32[]{:S(2)}) %collective-permute-start.33) | collective-permute-done | bytes 221216 | tf_op jit(solution)/shard_map/ppermute | solution.py:277
  257.8 1.3 collective-permute-done.32
  259.7 1.4 fusion.44
  261.1 2.9 %reshape.310 = f32[64,2,2304]{2,1,0:T(2,128)} reshape(f32[128,2304]{1,0:T(8,128)} %fusion.44) | data formatting | bytes 2359296 | tf_op jit(solution)/shard_map/reshape | solution.py:300
  264.1 2.6 fusion.143
  266.7 2.0 fusion.56
  (125 shorter events, 40.8 us)
Async XLA Ops:
  7.2 98.8 %copy-start = (bf16[1,720,2304]{2,1,0:T(8,128)(2,1)S(1)}, bf16[1,720,2304]{2,1,0:T(8,128)(2,1)}, u32[]{:S(2)}) copy-start(bf16[1,720,2304]{2,1,0:T(8,128)(2,1)} %param.27) | copy-start | bytes 9953284
  7.2 42.6 %all-gather.2.cloned.1.call-start = ((), (), s32[]{:S(2)}) async-start(), calls=%async_computation | async-start | bytes 5898240 | tf_op jit(solution)/shard_map/all_gather | solution.py:228
  63.7 8.1 %copy-start.15 = (f32[2304]{0:T(1024)S(1)}, f32[2304]{0:T(1024)}, u32[]{:S(2)}) copy-start(f32[2304]{0:T(1024)} %param.23) | copy-start | bytes 27652
  71.0 0.8 copy-start.1
  71.0 10.2 %copy-start.16 = (s32[64,2]{0,1:T(2,128)S(1)}, s32[64,2]{0,1:T(2,128)}, u32[]{:S(2)}) copy-start(s32[64,2]{0,1:T(2,128)} %param.25) | copy-start | bytes 1540
  72.0 0.7 copy-start.2
  78.1 7.2 %collective-permute-start = (bf16[48,2304]{1,0:T(8,128)(2,1)S(1)}, bf16[48,2304]{1,0:T(8,128)(2,1)S(1)}, u32[]{:S(2)}, u32[]{:S(2)}) collective-permute-start(bf16[48,2304]{1,0:T(8,128)(2,1)S(1)} %get-tuple-element.34), channel_id=1, source_target_pairs={{0,1},{1,2},{2,3},{3,0},{4,5},{5,6},{6,7},{7,4},{8,9},{9,10},{10,1... | collective-permute-start | bytes 663560 | tf_op jit(solution)/shard_map/ppermute | solution.py:277
  78.4 8.2 %collective-permute-start.3 = (bf16[48,2304]{1,0:T(8,128)(2,1)S(1)}, bf16[48,2304]{1,0:T(8,128)(2,1)S(1)}, u32[]{:S(2)}, u32[]{:S(2)}) collective-permute-start(bf16[48,2304]{1,0:T(8,128)(2,1)S(1)} %get-tuple-element.33), channel_id=1, source_target_pairs={{0,3},{1,0},{2,1},{3,2},{4,7},{5,4},{6,5},{7,6},{8,11},{9,8},{10,9... | collective-permute-start | bytes 663560 | tf_op jit(solution)/shard_map/ppermute | solution.py:277
  79.9 10.7 %collective-permute-start.2 = (bf16[48,2304]{1,0:T(8,128)(2,1)S(1)}, bf16[48,2304]{1,0:T(8,128)(2,1)S(1)}, u32[]{:S(2)}, u32[]{:S(2)}) collective-permute-start(bf16[48,2304]{1,0:T(8,128)(2,1)S(1)} %get-tuple-element.32), channel_id=1, source_target_pairs={{0,2},{1,3},{2,0},{3,1},{4,6},{5,7},{6,4},{7,5},{8,10},{9,11},{10,... | collective-permute-start | bytes 663560 | tf_op jit(solution)/shard_map/ppermute | solution.py:277
  85.2 10.8 %copy-start.5 = (bf16[48,2304]{1,0:T(8,128)(2,1)}, bf16[48,2304]{1,0:T(8,128)(2,1)S(1)}, u32[]{:S(2)}) copy-start(bf16[48,2304]{1,0:T(8,128)(2,1)S(1)} %collective-permute-done) | copy-start | bytes 663556
  85.2 18.8 %slice-start = ((s8[6635520]{0:T(1024)(128)(4,1)}), s8[4194304]{0:T(1024)(128)(4,1)S(1)}, s32[]{:S(2)}) async-start(s8[6635520]{0:T(1024)(128)(4,1)} %bitcast.156), calls=%async_computation.1 | async-start | bytes 8388608
  85.3 10.8 %collective-permute-start.1 = (bf16[96,2304]{1,0:T(8,128)(2,1)S(1)}, bf16[96,2304]{1,0:T(8,128)(2,1)S(1)}, u32[]{:S(2)}, u32[]{:S(2)}) collective-permute-start(bf16[96,2304]{1,0:T(8,128)(2,1)S(1)} %pad_maximum_fusion.1), channel_id=1, source_target_pairs={{0,4},{4,12},{12,20},{20,28},{28,24},{24,16},{16,8},{8,0},{1,5},{5... | collective-permute-start | bytes 1327112 | tf_op jit(solution)/shard_map/ppermute | solution.py:180
  86.5 9.6 %copy-start.6 = (bf16[48,2304]{1,0:T(8,128)(2,1)}, bf16[48,2304]{1,0:T(8,128)(2,1)S(1)}, u32[]{:S(2)}) copy-start(bf16[48,2304]{1,0:T(8,128)(2,1)S(1)} %collective-permute-done.3) | copy-start | bytes 663556
  90.6 5.5 %copy-start.7 = (bf16[48,2304]{1,0:T(8,128)(2,1)}, bf16[48,2304]{1,0:T(8,128)(2,1)S(1)}, u32[]{:S(2)}) copy-start(bf16[48,2304]{1,0:T(8,128)(2,1)S(1)} %collective-permute-done.2) | copy-start | bytes 663556
  90.6 13.4 %slice-start.1 = ((s8[6635520]{0:T(1024)(128)(4,1)}), s8[2441216]{0:T(1024)(128)(4,1)S(1)}, s32[]{:S(2)}) async-start(s8[6635520]{0:T(1024)(128)(4,1)} %bitcast.156), calls=%async_computation.2 | async-start | bytes 4882432
  90.6 11.6 %collective-permute-start.4 = (bf16[96,2304]{1,0:T(8,128)(2,1)S(1)}, bf16[96,2304]{1,0:T(8,128)(2,1)S(1)}, u32[]{:S(2)}, u32[]{:S(2)}) collective-permute-start(bf16[96,2304]{1,0:T(8,128)(2,1)S(1)} %pad_maximum_fusion.2), channel_id=1, source_target_pairs={{0,8},{4,0},{12,4},{20,12},{28,20},{24,28},{16,24},{8,16},{1,9},{5... | collective-permute-start | bytes 1327112 | tf_op jit(solution)/shard_map/ppermute | solution.py:180
  96.1 0.8 copy-start.3
  102.3 0.8 copy-start.4
  103.1 0.9 copy-start.9
  111.6 13.4 %collective-permute-start.6 = (bf16[96,2304]{1,0:T(8,128)(2,1)}, bf16[96,2304]{1,0:T(8,128)(2,1)}, u32[]{:S(2)}, u32[]{:S(2)}) collective-permute-start(bf16[96,2304]{1,0:T(8,128)(2,1)} %copy-done.3), channel_id=1, source_target_pairs={{0,4},{4,12},{12,20},{20,28},{28,24},{24,16},{16,8},{8,0},{1,5},{5... | collective-permute-start | bytes 1327112 | tf_op jit(solution)/shard_map/ppermute | solution.py:180
  112.8 13.4 %collective-permute-start.7 = (bf16[96,2304]{1,0:T(8,128)(2,1)}, bf16[96,2304]{1,0:T(8,128)(2,1)}, u32[]{:S(2)}, u32[]{:S(2)}) collective-permute-start(bf16[96,2304]{1,0:T(8,128)(2,1)} %copy-done.4), channel_id=1, source_target_pairs={{0,8},{4,0},{12,4},{20,12},{28,20},{24,28},{16,24},{8,16},{1,9},{5... | collective-permute-start | bytes 1327112 | tf_op jit(solution)/shard_map/ppermute | solution.py:180
  115.7 23.9 %collective-permute-start.5 = (bf16[96,2304]{1,0:T(8,128)(2,1)}, bf16[96,2304]{1,0:T(8,128)(2,1)}, u32[]{:S(2)}, u32[]{:S(2)}) collective-permute-start(bf16[96,2304]{1,0:T(8,128)(2,1)} %get-tuple-element.30), channel_id=1, source_target_pairs={{0,4},{4,12},{12,20},{20,28},{28,24},{24,16},{16,8},{8,0},{1,5},{5... | collective-permute-start | bytes 1327112 | tf_op jit(solution)/shard_map/ppermute | solution.py:190
  116.9 22.7 %collective-permute-start.25 = (bf16[96,2304]{1,0:T(8,128)(2,1)}, bf16[96,2304]{1,0:T(8,128)(2,1)}, u32[]{:S(2)}, u32[]{:S(2)}) collective-permute-start(bf16[96,2304]{1,0:T(8,128)(2,1)} %get-tuple-element.31), channel_id=1, source_target_pairs={{0,8},{4,0},{12,4},{20,12},{28,20},{24,28},{16,24},{8,16},{1,9},{5... | collective-permute-start | bytes 1327112 | tf_op jit(solution)/shard_map/ppermute | solution.py:190
  127.2 0.9 copy-start.10
  132.0 12.2 %collective-permute-start.9 = (bf16[96,2304]{1,0:T(8,128)(2,1)}, bf16[96,2304]{1,0:T(8,128)(2,1)}, u32[]{:S(2)}, u32[]{:S(2)}) collective-permute-start(bf16[96,2304]{1,0:T(8,128)(2,1)} %collective-permute-done.6), channel_id=1, source_target_pairs={{0,4},{4,12},{12,20},{20,28},{28,24},{24,16},{16,8},{8,0},{1,5},{5... | collective-permute-start | bytes 1327112 | tf_op jit(solution)/shard_map/ppermute | solution.py:180
  133.5 11.8 %collective-permute-start.10 = (bf16[96,2304]{1,0:T(8,128)(2,1)}, bf16[96,2304]{1,0:T(8,128)(2,1)}, u32[]{:S(2)}, u32[]{:S(2)}) collective-permute-start(bf16[96,2304]{1,0:T(8,128)(2,1)} %collective-permute-done.7), channel_id=1, source_target_pairs={{0,8},{4,0},{12,4},{20,12},{28,20},{24,28},{16,24},{8,16},{1,9},{5... | collective-permute-start | bytes 1327112 | tf_op jit(solution)/shard_map/ppermute | solution.py:180
  142.1 16.6 %collective-permute-start.8 = (bf16[96,2304]{1,0:T(8,128)(2,1)}, bf16[96,2304]{1,0:T(8,128)(2,1)}, u32[]{:S(2)}, u32[]{:S(2)}) collective-permute-start(bf16[96,2304]{1,0:T(8,128)(2,1)} %get-tuple-element.28), channel_id=1, source_target_pairs={{0,4},{4,12},{12,20},{20,28},{28,24},{24,16},{16,8},{8,0},{1,5},{5... | collective-permute-start | bytes 1327112 | tf_op jit(solution)/shard_map/ppermute | solution.py:190
  143.6 15.1 %collective-permute-start.26 = (bf16[96,2304]{1,0:T(8,128)(2,1)}, bf16[96,2304]{1,0:T(8,128)(2,1)}, u32[]{:S(2)}, u32[]{:S(2)}) collective-permute-start(bf16[96,2304]{1,0:T(8,128)(2,1)} %get-tuple-element.29), channel_id=1, source_target_pairs={{0,8},{4,0},{12,4},{20,12},{28,20},{24,28},{16,24},{8,16},{1,9},{5... | collective-permute-start | bytes 1327112 | tf_op jit(solution)/shard_map/ppermute | solution.py:190
  146.3 0.9 copy-start.11
  151.1 12.2 %collective-permute-start.12 = (bf16[96,2304]{1,0:T(8,128)(2,1)}, bf16[96,2304]{1,0:T(8,128)(2,1)}, u32[]{:S(2)}, u32[]{:S(2)}) collective-permute-start(bf16[96,2304]{1,0:T(8,128)(2,1)} %collective-permute-done.9), channel_id=1, source_target_pairs={{0,4},{4,12},{12,20},{20,28},{28,24},{24,16},{16,8},{8,0},{1,5},{5... | collective-permute-start | bytes 1327112 | tf_op jit(solution)/shard_map/ppermute | solution.py:180
  152.6 12.7 %collective-permute-start.13 = (bf16[96,2304]{1,0:T(8,128)(2,1)}, bf16[96,2304]{1,0:T(8,128)(2,1)}, u32[]{:S(2)}, u32[]{:S(2)}) collective-permute-start(bf16[96,2304]{1,0:T(8,128)(2,1)} %collective-permute-done.10), channel_id=1, source_target_pairs={{0,8},{4,0},{12,4},{20,12},{28,20},{24,28},{16,24},{8,16},{1,9},{5... | collective-permute-start | bytes 1327112 | tf_op jit(solution)/shard_map/ppermute | solution.py:180
  161.3 17.5 %collective-permute-start.11 = (bf16[96,2304]{1,0:T(8,128)(2,1)}, bf16[96,2304]{1,0:T(8,128)(2,1)}, u32[]{:S(2)}, u32[]{:S(2)}) collective-permute-start(bf16[96,2304]{1,0:T(8,128)(2,1)} %get-tuple-element.26), channel_id=1, source_target_pairs={{0,4},{4,12},{12,20},{20,28},{28,24},{24,16},{16,8},{8,0},{1,5},{5... | collective-permute-start | bytes 1327112 | tf_op jit(solution)/shard_map/ppermute | solution.py:190
  162.8 16.0 %collective-permute-start.27 = (bf16[96,2304]{1,0:T(8,128)(2,1)}, bf16[96,2304]{1,0:T(8,128)(2,1)}, u32[]{:S(2)}, u32[]{:S(2)}) collective-permute-start(bf16[96,2304]{1,0:T(8,128)(2,1)} %get-tuple-element.27), channel_id=1, source_target_pairs={{0,8},{4,0},{12,4},{20,12},{28,20},{24,28},{16,24},{8,16},{1,9},{5... | collective-permute-start | bytes 1327112 | tf_op jit(solution)/shard_map/ppermute | solution.py:190
  166.3 0.9 copy-start.12
  171.1 12.2 %collective-permute-start.15 = (bf16[96,2304]{1,0:T(8,128)(2,1)}, bf16[96,2304]{1,0:T(8,128)(2,1)}, u32[]{:S(2)}, u32[]{:S(2)}) collective-permute-start(bf16[96,2304]{1,0:T(8,128)(2,1)} %collective-permute-done.12), channel_id=1, source_target_pairs={{0,4},{4,12},{12,20},{20,28},{28,24},{24,16},{16,8},{8,0},{1,5},{5... | collective-permute-start | bytes 1327112 | tf_op jit(solution)/shard_map/ppermute | solution.py:180
  172.7 12.6 %collective-permute-start.16 = (bf16[96,2304]{1,0:T(8,128)(2,1)}, bf16[96,2304]{1,0:T(8,128)(2,1)}, u32[]{:S(2)}, u32[]{:S(2)}) collective-permute-start(bf16[96,2304]{1,0:T(8,128)(2,1)} %collective-permute-done.13), channel_id=1, source_target_pairs={{0,8},{4,0},{12,4},{20,12},{28,20},{24,28},{16,24},{8,16},{1,9},{5... | collective-permute-start | bytes 1327112 | tf_op jit(solution)/shard_map/ppermute | solution.py:180
  181.3 17.5 %collective-permute-start.14 = (bf16[96,2304]{1,0:T(8,128)(2,1)}, bf16[96,2304]{1,0:T(8,128)(2,1)}, u32[]{:S(2)}, u32[]{:S(2)}) collective-permute-start(bf16[96,2304]{1,0:T(8,128)(2,1)} %get-tuple-element.24), channel_id=1, source_target_pairs={{0,4},{4,12},{12,20},{20,28},{28,24},{24,16},{16,8},{8,0},{1,5},{5... | collective-permute-start | bytes 1327112 | tf_op jit(solution)/shard_map/ppermute | solution.py:190
  182.8 16.0 %collective-permute-start.28 = (bf16[96,2304]{1,0:T(8,128)(2,1)}, bf16[96,2304]{1,0:T(8,128)(2,1)}, u32[]{:S(2)}, u32[]{:S(2)}) collective-permute-start(bf16[96,2304]{1,0:T(8,128)(2,1)} %get-tuple-element.25), channel_id=1, source_target_pairs={{0,8},{4,0},{12,4},{20,12},{28,20},{24,28},{16,24},{8,16},{1,9},{5... | collective-permute-start | bytes 1327112 | tf_op jit(solution)/shard_map/ppermute | solution.py:190
  186.3 0.9 copy-start.13
  191.1 13.0 %collective-permute-start.18 = (bf16[96,2304]{1,0:T(8,128)(2,1)}, bf16[96,2304]{1,0:T(8,128)(2,1)}, u32[]{:S(2)}, u32[]{:S(2)}) collective-permute-start(bf16[96,2304]{1,0:T(8,128)(2,1)} %collective-permute-done.15), channel_id=1, source_target_pairs={{0,4},{4,12},{12,20},{20,28},{28,24},{24,16},{16,8},{8,0},{1,5},{5... | collective-permute-start | bytes 1327112 | tf_op jit(solution)/shard_map/ppermute | solution.py:180
  192.2 13.4 %collective-permute-start.19 = (bf16[96,2304]{1,0:T(8,128)(2,1)}, bf16[96,2304]{1,0:T(8,128)(2,1)}, u32[]{:S(2)}, u32[]{:S(2)}) collective-permute-start(bf16[96,2304]{1,0:T(8,128)(2,1)} %collective-permute-done.16), channel_id=1, source_target_pairs={{0,8},{4,0},{12,4},{20,12},{28,20},{24,28},{16,24},{8,16},{1,9},{5... | collective-permute-start | bytes 1327112 | tf_op jit(solution)/shard_map/ppermute | solution.py:180
  201.3 17.7 %collective-permute-start.17 = (bf16[96,2304]{1,0:T(8,128)(2,1)}, bf16[96,2304]{1,0:T(8,128)(2,1)}, u32[]{:S(2)}, u32[]{:S(2)}) collective-permute-start(bf16[96,2304]{1,0:T(8,128)(2,1)} %get-tuple-element.22), channel_id=1, source_target_pairs={{0,4},{4,12},{12,20},{20,28},{28,24},{24,16},{16,8},{8,0},{1,5},{5... | collective-permute-start | bytes 1327112 | tf_op jit(solution)/shard_map/ppermute | solution.py:190
  202.4 16.7 %collective-permute-start.29 = (bf16[96,2304]{1,0:T(8,128)(2,1)}, bf16[96,2304]{1,0:T(8,128)(2,1)}, u32[]{:S(2)}, u32[]{:S(2)}) collective-permute-start(bf16[96,2304]{1,0:T(8,128)(2,1)} %get-tuple-element.23), channel_id=1, source_target_pairs={{0,8},{4,0},{12,4},{20,12},{28,20},{24,28},{16,24},{8,16},{1,9},{5... | collective-permute-start | bytes 1327112 | tf_op jit(solution)/shard_map/ppermute | solution.py:190
  206.6 0.9 copy-start.14
  211.4 12.2 %collective-permute-start.21 = (bf16[96,2304]{1,0:T(8,128)(2,1)}, bf16[96,2304]{1,0:T(8,128)(2,1)}, u32[]{:S(2)}, u32[]{:S(2)}) collective-permute-start(bf16[96,2304]{1,0:T(8,128)(2,1)} %collective-permute-done.18), channel_id=1, source_target_pairs={{0,4},{4,12},{12,20},{20,28},{28,24},{24,16},{16,8},{8,0},{1,5},{5... | collective-permute-start | bytes 1327112 | tf_op jit(solution)/shard_map/ppermute | solution.py:180
  212.7 12.4 %collective-permute-start.22 = (bf16[96,2304]{1,0:T(8,128)(2,1)}, bf16[96,2304]{1,0:T(8,128)(2,1)}, u32[]{:S(2)}, u32[]{:S(2)}) collective-permute-start(bf16[96,2304]{1,0:T(8,128)(2,1)} %collective-permute-done.19), channel_id=1, source_target_pairs={{0,8},{4,0},{12,4},{20,12},{28,20},{24,28},{16,24},{8,16},{1,9},{5... | collective-permute-start | bytes 1327112 | tf_op jit(solution)/shard_map/ppermute | solution.py:180
  221.6 15.0 %collective-permute-start.20 = (bf16[96,2304]{1,0:T(8,128)(2,1)}, bf16[96,2304]{1,0:T(8,128)(2,1)}, u32[]{:S(2)}, u32[]{:S(2)}) collective-permute-start(bf16[96,2304]{1,0:T(8,128)(2,1)} %get-tuple-element.20), channel_id=1, source_target_pairs={{0,4},{4,12},{12,20},{20,28},{28,24},{24,16},{16,8},{8,0},{1,5},{5... | collective-permute-start | bytes 1327112 | tf_op jit(solution)/shard_map/ppermute | solution.py:190
  222.9 13.7 %collective-permute-start.30 = (bf16[96,2304]{1,0:T(8,128)(2,1)}, bf16[96,2304]{1,0:T(8,128)(2,1)}, u32[]{:S(2)}, u32[]{:S(2)}) collective-permute-start(bf16[96,2304]{1,0:T(8,128)(2,1)} %get-tuple-element.21), channel_id=1, source_target_pairs={{0,8},{4,0},{12,4},{20,12},{28,20},{24,28},{16,24},{8,16},{1,9},{5... | collective-permute-start | bytes 1327112 | tf_op jit(solution)/shard_map/ppermute | solution.py:190
  226.1 0.9 copy-start.8
  239.1 8.6 %collective-permute-start.23 = (bf16[96,2304]{1,0:T(8,128)(2,1)}, bf16[96,2304]{1,0:T(8,128)(2,1)}, u32[]{:S(2)}, u32[]{:S(2)}) collective-permute-start(bf16[96,2304]{1,0:T(8,128)(2,1)} %get-tuple-element.18), channel_id=1, source_target_pairs={{0,4},{4,12},{12,20},{20,28},{28,24},{24,16},{16,8},{8,0},{1,5},{5... | collective-permute-start | bytes 1327112 | tf_op jit(solution)/shard_map/ppermute | solution.py:192
  240.4 8.6 %collective-permute-start.31 = (bf16[96,2304]{1,0:T(8,128)(2,1)}, bf16[96,2304]{1,0:T(8,128)(2,1)}, u32[]{:S(2)}, u32[]{:S(2)}) collective-permute-start(bf16[96,2304]{1,0:T(8,128)(2,1)} %get-tuple-element.19), channel_id=1, source_target_pairs={{0,8},{4,0},{12,4},{20,12},{28,20},{24,28},{16,24},{8,16},{1,9},{5... | collective-permute-start | bytes 1327112 | tf_op jit(solution)/shard_map/ppermute | solution.py:192
  250.7 7.1 %collective-permute-start.33 = (bf16[48,2304]{1,0:T(8,128)(2,1)S(1)}, bf16[48,2304]{1,0:T(8,128)(2,1)S(1)}, u32[]{:S(2)}, u32[]{:S(2)}) collective-permute-start(bf16[48,2304]{1,0:T(8,128)(2,1)S(1)} %get-tuple-element.39), channel_id=1, source_target_pairs={{0,1},{1,2},{2,3},{3,0},{4,5},{5,6},{6,7},{7,4},{8,9},{9,10},{10,1... | collective-permute-start | bytes 663560 | tf_op jit(solution)/shard_map/ppermute | solution.py:277
  250.8 8.4 %collective-permute-start.32 = (bf16[48,2304]{1,0:T(8,128)(2,1)S(1)}, bf16[48,2304]{1,0:T(8,128)(2,1)S(1)}, u32[]{:S(2)}, u32[]{:S(2)}) collective-permute-start(bf16[48,2304]{1,0:T(8,128)(2,1)S(1)} %get-tuple-element.38), channel_id=1, source_target_pairs={{0,2},{1,3},{2,0},{3,1},{4,6},{5,7},{6,4},{7,5},{8,10},{9,11},{10,... | collective-permute-start | bytes 663560 | tf_op jit(solution)/shard_map/ppermute | solution.py:277
  250.9 8.8 %collective-permute-start.24 = (bf16[48,2304]{1,0:T(8,128)(2,1)S(1)}, bf16[48,2304]{1,0:T(8,128)(2,1)S(1)}, u32[]{:S(2)}, u32[]{:S(2)}) collective-permute-start(bf16[48,2304]{1,0:T(8,128)(2,1)S(1)} %get-tuple-element.37), channel_id=1, source_target_pairs={{0,3},{1,0},{2,1},{3,2},{4,7},{5,4},{6,5},{7,6},{8,11},{9,8},{10,9... | collective-permute-start | bytes 663560 | tf_op jit(solution)/shard_map/ppermute | solution.py:277
Sparse Core Ops, SparseCore 0:
  9.5 40.1 all-gather.1

commit v6 on v5

--- a/solution.py
+++ b/solution.py
@@ -195,6 +195,7 @@
 
 def local(
     ring,
+    expert_count,
     hidden,
     tree_qkv,
     prompt_kv,
@@ -218,20 +219,39 @@
     blocks = features // ((4 if (features // HD) % 4 == 0 else 2) * HD)
     private_slots = jnp.arange(private_kv.shape[1], dtype=jnp.int32)
     private_ok = jnp.broadcast_to(private_slots[None, :] < priv_len[0], (row_count, private_kv.shape[1]))
-    local_acc, local_top, local_total = attend(
-        tree_qkv[:, :features],
-        [
-            (private_kv[0], 0, blocks, private_ok),
-            (tree_qkv, blocks, 2 * blocks, reached[0] > 0.5),
-        ],
-    )
-    shard_rows = lax.all_gather(prompt_kv, "expert", axis=1, tiled=True)
-    piece_len = shard_rows.shape[1]
+    piece = prompt_kv[0]
+    piece_len = piece.shape[0]
+    own = lax.axis_index("expert")
     places = jnp.arange(piece_len, dtype=jnp.int32)
-    prompt_ok = jnp.broadcast_to((places < prompt_len[0])[None, :], (row_count, piece_len))
-    prompt_acc, prompt_top, prompt_total = attend(
-        tree_qkv[:, :features], [(shard_rows[0], 0, blocks, prompt_ok)]
-    )
+
+    def prompt_ok(source):
+        return jnp.broadcast_to((source * piece_len + places < prompt_len[0])[None, :], (row_count, piece_len))
+
+    local_sources = [
+        (private_kv[0], 0, blocks, private_ok),
+        (tree_qkv, blocks, 2 * blocks, reached[0] > 0.5),
+    ]
+    if expert_count == 4:
+        def swap(rows, mask):
+            return lax.ppermute(rows, "expert", [(j, j ^ mask) for j in range(expert_count)])
+
+        near = swap(piece, 1)
+        far = swap(piece, 2)
+        corner = swap(far, 1)
+        local_sources.append((piece, 0, blocks, prompt_ok(own)))
+        remote_sources = [
+            (near, 0, blocks, prompt_ok(own ^ 1)),
+            (far, 0, blocks, prompt_ok(own ^ 2)),
+            (corner, 0, blocks, prompt_ok(own ^ 3)),
+        ]
+    else:
+        gathered = lax.all_gather(prompt_kv, "expert", axis=1, tiled=True)[0]
+        whole = jnp.arange(gathered.shape[0], dtype=jnp.int32)
+        remote_sources = [
+            (gathered, 0, blocks, jnp.broadcast_to((whole < prompt_len[0])[None, :], (row_count, gathered.shape[0])))
+        ]
+    local_acc, local_top, local_total = attend(tree_qkv[:, :features], local_sources)
+    prompt_acc, prompt_top, prompt_total = attend(tree_qkv[:, :features], remote_sources)
     highest = jnp.maximum(local_top, prompt_top)
     scale_local = jnp.exp(local_top - highest)
     scale_prompt = jnp.exp(prompt_top - highest)
@@ -324,7 +344,7 @@
     )
     ring = dp_ring(mesh)
     return jax.shard_map(
-        functools.partial(local, ring),
+        functools.partial(local, ring, mesh.shape["expert"]),
         mesh=mesh,
         in_specs=placed,
         out_specs=(P(("dp", "expert"), None), P(("dp", "expert"), None, None)),

time: 280 us -> 281 us (level); the launches traced: 276 us -> 279 us
  between operations: 16.4 us -> 3.01 us
  starting transfers between devices: 33.1 us -> 41.4 us
  waiting for transfers between devices: 50.3 us -> 54.7 us
    ppermute x0 -> x3, waiting for transfers between devices: none -> 23.1 us  [swap(): lax.ppermute(rows, 'expert', [(j, j ^ mask) for j in range(expert_count)])]
    all_gather x1 -> x0, waiting for transfers between devices: 16.1 us -> none  [local(): shard_rows = lax.all_gather(prompt_kv, 'expert', axis=1, tiled=True)]
    ppermute x6, starting transfers between devices: 3.93 us -> 8.4 us  [shifted(): lax.ppermute(rows, 'expert', [(j, (j + shift) % experts) for j in range(e...]
    ppermute x0 -> x3, starting transfers between devices: none -> 3.15 us  [swap(): lax.ppermute(rows, 'expert', [(j, j ^ mask) for j in range(expert_count)])]
  transfers between devices with their start and end apart: 35 -> 37, of which waited for: 16 -> 16; matrix products, arithmetic and copies ran while one was open for 38% -> 37% of each run, Pallas kernels for 6% -> 6%
where the time goes in v6:
time: 281 us; the launch traced here: 279 us
  matrix products  89.4 us (32%)
  waiting for transfers between devices  54.7 us (19%)
  starting transfers between devices  41.4 us (15%)
  local copies, waits for them, and re-layouts  39.5 us (14%)
  Pallas kernels  31.2 us (11%)
  other arithmetic  20 us (7%)
  between operations  3.01 us (1%)
    dot_general x8, matrix products, local(): jnp.dot(hidden_units, down_rows, preferred_element_type=jnp.float32)  44.8 us
    pallas_call x2, Pallas kernels, attend(): pl.pallas_call(functools.partial(attend_kernel, count=len(sources), scale...  31.2 us
    dot_general x8, matrix products, local(): gate_act = jnp.dot(pooled, gate_cols, preferred_element_type=jnp.float32)  29.2 us
    ppermute x3, waiting for transfers between devices, swap(): lax.ppermute(rows, 'expert', [(j, j ^ mask) for j in range(expert_count)])  23.1 us
    unnamed x46, local copies, waits for them, and re-layouts  16.6 us
    ppermute x14, starting transfers between devices, ring_gather(): piece = lax.ppermute(piece, 'dp', pairs)  15.7 us
    convert_element_type x6, other arithmetic, ring_reduce(): moving = (received + blocks[index].astype(jnp.float32)).astype(jnp.bfloat16)  15.3 us
    ppermute x14, waiting for transfers between devices, ring_gather(): piece = lax.ppermute(piece, 'dp', pairs)  14.7 us
  transfers between devices with their start and end apart: 37, of which 16 were waited for; matrix products, arithmetic and copies ran while one was open for 37% of the time, Pallas kernels for 6%

profile of v6, /device:TPU:0, one launch (start us, length us, event | category | flops | bytes accessed | tf_op | source)
XLA Modules:
  0.0 279.4 jit_solution(11663751106198116422)
XLA Ops:
  1.2 2.6 collective-permute-start.1
  7.5 23.1 %collective-permute-done.1.refs_4_.refs_5_ = bf16[128,4608]{1,0:T(8,128)(2,1)} collective-permute-done((bf16[128,4608]{1,0:T(8,128)(2,1)}, bf16[128,4608]{1,0:T(8,128)(2,1)}, u32[]{:S(2)}, u32[]{:S(2)}) %collective-permute-start.1) | collective-permute-done | bytes 1179680 | tf_op jit(solution)/shard_map/ppermute | solution.py:236
  30.7 1.7 slice.111.refs_0_
  35.2 16.2 %shard_map.152 = (f32[64,2304]{1,0:T(8,128)}, f32[64,2304]{1,0:T(8,128)}, f32[64,2304]{1,0:T(8,128)}) custom-call(bf16[64,2304]{1,0:T(8,128)(2,1)} %slice.111.refs_0_, bf16[512,4608]{1,0:T(8,128)(2,1)} %bitcast.152, bf16[512,4608]{1,0:T(8,128)(2,1)} %bitcast.153, f32[64,512]{1,0:T(8,128)} %broadcast_in_dim.38.refs_3_, bf16[64,6912]{1,0:T(8,128)(2,1)} %refs_5_.1, ...), custom_call_target="tpu_custom_call" | custom-call | tf_op jit(solution)/shard_map/pallas_call | solution.py:141
  51.9 2.3 fusion
  56.0 15.0 %shard_map.153 = (f32[64,2304]{1,0:T(8,128)}, f32[64,2304]{1,0:T(8,128)}, f32[64,2304]{1,0:T(8,128)}) custom-call(bf16[64,2304]{1,0:T(8,128)(2,1)} %slice.111.refs_0_, bf16[128,4608]{1,0:T(8,128)(2,1)} %collective-permute-done.refs_1_.refs_2_, bf16[128,4608]{1,0:T(8,128)(2,1)} %collective-permute-done.refs_1_.refs_2_, f32[64,128]{1,0:T(8,128)} %broadcast_in_dim.40.refs_3_, ...), custom_call_target="tpu_custom_call" | custom-call | tf_op jit(solution)/shard_map/pallas_call | solution.py:141
  71.1 7.3 %multiply_reduce_fusion = (f32[64]{0:T(128)S(1)}, f32[64,2304]{1,0:T(8,128)S(1)}) fusion(bf16[2304,2304]{1,0:T(8,128)(2,1)} %param.22, f32[64,2304]{1,0:T(8,128)} %get-tuple-element.13, f32[64,2304]{1,0:T(8,128)} %get-tuple-element.12, f32[64,2304]{1,0:T(8,128)} %get-tuple-element.11, f32[64,2304]{1,0:T(8,128)} %get-tuple-element.10, ...), kind=kOutput, calls=%fused_computation.107 | convolution fusion | flops 681983936 | bytes 15040768 | tf_op jit(solution)/shard_map/dot_general | solution.py:261
  80.0 1.1 broadcast_in_dim.45
  81.2 2.7 reshape.325
  83.9 1.4 convolution_convert_fusion.1
  85.9 1.4 collective-permute-start.6
  87.3 1.6 collective-permute-start.5
  90.1 1.3 collective-permute-done.3
  91.4 1.8 collective-permute-start.4
  93.2 4.8 %collective-permute-done.5 = bf16[48,2304]{1,0:T(8,128)(2,1)S(1)} collective-permute-done((bf16[48,2304]{1,0:T(8,128)(2,1)S(1)}, bf16[48,2304]{1,0:T(8,128)(2,1)S(1)}, u32[]{:S(2)}, u32[]{:S(2)}) %collective-permute-start.5) | collective-permute-done | bytes 221216 | tf_op jit(solution)/shard_map/ppermute | solution.py:297
  98.1 1.7 collective-permute-start.7
  99.8 3.9 %fusion.27 = f32[192,720]{1,0:T(8,128)} fusion(bf16[1,2,2304,720]{2,3,1,0:T(8,128)(2,1)} %param.26, bf16[48,2304]{1,0:T(8,128)(2,1)S(1)} %collective-permute-done.6, bf16[48,2304]{1,0:T(8,128)(2,1)S(1)} %collective-permute-done.5, bf16[48,2304]{1,0:T(8,128)(2,1)S(1)} %collective-permute-done.3, bf16[48,2304]{1,0:T(8,128)(2,1)S(1)} %get-tuple-element.35), kind=kOutput, calls=%fused_computation.38 | convolution fusion | flops 640548864 | bytes 4755456 | tf_op jit(solution)/shard_map/dot_general | solution.py:307
  104.7 3.9 %collective-permute-done.7 = bf16[96,2304]{1,0:T(8,128)(2,1)S(1)} collective-permute-done((bf16[96,2304]{1,0:T(8,128)(2,1)S(1)}, bf16[96,2304]{1,0:T(8,128)(2,1)S(1)}, u32[]{:S(2)}, u32[]{:S(2)}) %collective-permute-start.7) | collective-permute-done | bytes 442400 | tf_op jit(solution)/shard_map/ppermute | solution.py:180
  110.4 2.0 fusion.41
  112.4 5.6 %convolution_convert_fusion.9 = bf16[192,2304]{1,0:T(8,128)(2,1)} fusion(bf16[1,720,2304]{2,1,0:T(8,128)(2,1)S(1)} %copy-done, f32[192,720]{1,0:T(8,128)} %fusion.41, bf16[192,2304]{1,0:T(8,128)(2,1)} %copy-done.9, bf16[1,2,2304,720]{2,3,1,0:T(8,128)(2,1)} %param.26), kind=kOutput, calls=%fused_computation.10 | convolution fusion | flops 1275291648 | bytes 8994816 | tf_op jit(solution)/shard_map/dot_general | solution.py:310
  118.0 1.5 collective-permute-start.9
  120.0 2.1 fusion.143
  122.2 1.5 collective-permute-start.8
  124.2 7.2 %collective-permute-done.9 = bf16[96,2304]{1,0:T(8,128)(2,1)} collective-permute-done((bf16[96,2304]{1,0:T(8,128)(2,1)}, bf16[96,2304]{1,0:T(8,128)(2,1)}, u32[]{:S(2)}, u32[]{:S(2)}) %collective-permute-start.9) | collective-permute-done | bytes 442400 | tf_op jit(solution)/shard_map/ppermute | solution.py:180
  134.8 3.9 %fusion.39 = f32[192,720]{1,0:T(8,128)} fusion(bf16[192,2304]{1,0:T(8,128)(2,1)S(1)} %constant_dynamic-update-slice_fusion.2, bf16[1,2,2304,720]{2,3,1,0:T(8,128)(2,1)} %param.26), kind=kOutput, calls=%fused_computation.50 | convolution fusion | flops 637009920 | bytes 4755456 | tf_op jit(solution)/shard_map/dot_general | solution.py:307
  138.7 1.6 collective-permute-start.12
  140.7 5.6 %convolution_convert_fusion.8 = bf16[192,2304]{1,0:T(8,128)(2,1)} fusion(bf16[1,720,2304]{2,1,0:T(8,128)(2,1)S(1)} %copy-done, f32[192,720]{1,0:T(8,128)} %fusion.39, bf16[192,2304]{1,0:T(8,128)(2,1)} %copy-done.10, bf16[1,2,2304,720]{2,3,1,0:T(8,128)(2,1)} %param.26), kind=kOutput, calls=%fused_computation.9 | convolution fusion | flops 1275291648 | bytes 8994816 | tf_op jit(solution)/shard_map/dot_general | solution.py:310
  146.3 2.6 add_convert_fusion.13
  148.9 1.6 collective-permute-start.11
  154.6 3.9 %fusion.37 = f32[192,720]{1,0:T(8,128)} fusion(bf16[192,2304]{1,0:T(8,128)(2,1)S(1)} %constant_dynamic-update-slice_fusion.4, bf16[1,2,2304,720]{2,3,1,0:T(8,128)(2,1)} %param.26), kind=kOutput, calls=%fused_computation.48 | convolution fusion | flops 637009920 | bytes 4755456 | tf_op jit(solution)/shard_map/dot_general | solution.py:307
  158.5 1.5 collective-permute-start.15
  160.5 5.6 %convolution_convert_fusion.7 = bf16[192,2304]{1,0:T(8,128)(2,1)} fusion(bf16[1,720,2304]{2,1,0:T(8,128)(2,1)S(1)} %copy-done, f32[192,720]{1,0:T(8,128)} %fusion.37, bf16[192,2304]{1,0:T(8,128)(2,1)} %copy-done.11, bf16[1,2,2304,720]{2,3,1,0:T(8,128)(2,1)} %param.26), kind=kOutput, calls=%fused_computation.8 | convolution fusion | flops 1275291648 | bytes 8994816 | tf_op jit(solution)/shard_map/dot_general | solution.py:310
  166.1 2.5 add_convert_fusion.12
  168.7 1.5 collective-permute-start.14
  174.8 3.9 %fusion.35 = f32[192,720]{1,0:T(8,128)} fusion(bf16[192,2304]{1,0:T(8,128)(2,1)S(1)} %constant_dynamic-update-slice_fusion.6, bf16[1,2,2304,720]{2,3,1,0:T(8,128)(2,1)} %param.26), kind=kOutput, calls=%fused_computation.46 | convolution fusion | flops 637009920 | bytes 4755456 | tf_op jit(solution)/shard_map/dot_general | solution.py:307
  178.7 1.4 collective-permute-start.18
  180.7 5.6 %convolution_convert_fusion.6 = bf16[192,2304]{1,0:T(8,128)(2,1)} fusion(bf16[1,720,2304]{2,1,0:T(8,128)(2,1)S(1)} %copy-done, f32[192,720]{1,0:T(8,128)} %fusion.35, bf16[192,2304]{1,0:T(8,128)(2,1)} %copy-done.12, bf16[1,2,2304,720]{2,3,1,0:T(8,128)(2,1)} %param.26), kind=kOutput, calls=%fused_computation.7 | convolution fusion | flops 1275291648 | bytes 8994816 | tf_op jit(solution)/shard_map/dot_general | solution.py:310
  186.3 2.5 add_convert_fusion.11
  188.9 1.4 collective-permute-start.17
  194.3 3.9 %fusion.33 = f32[192,720]{1,0:T(8,128)} fusion(bf16[192,2304]{1,0:T(8,128)(2,1)S(1)} %constant_dynamic-update-slice_fusion.8, bf16[1,2,2304,720]{2,3,1,0:T(8,128)(2,1)} %param.26), kind=kOutput, calls=%fused_computation.44 | convolution fusion | flops 637009920 | bytes 4755456 | tf_op jit(solution)/shard_map/dot_general | solution.py:307
  198.2 1.2 collective-permute-start.21
  200.3 5.6 %convolution_convert_fusion.5 = bf16[192,2304]{1,0:T(8,128)(2,1)} fusion(bf16[1,720,2304]{2,1,0:T(8,128)(2,1)S(1)} %copy-done, f32[192,720]{1,0:T(8,128)} %fusion.33, bf16[192,2304]{1,0:T(8,128)(2,1)} %copy-done.13, bf16[1,2,2304,720]{2,3,1,0:T(8,128)(2,1)} %param.26), kind=kOutput, calls=%fused_computation.6 | convolution fusion | flops 1275291648 | bytes 8994816 | tf_op jit(solution)/shard_map/dot_general | solution.py:310
  205.9 2.6 add_convert_fusion.10
  208.4 1.2 collective-permute-start.20
  214.2 3.9 %fusion.31 = f32[192,720]{1,0:T(8,128)} fusion(bf16[192,2304]{1,0:T(8,128)(2,1)S(1)} %constant_dynamic-update-slice_fusion.10, bf16[1,2,2304,720]{2,3,1,0:T(8,128)(2,1)} %param.26), kind=kOutput, calls=%fused_computation.42 | convolution fusion | flops 637009920 | bytes 4755456 | tf_op jit(solution)/shard_map/dot_general | solution.py:307
  218.1 1.4 collective-permute-start.24
  220.2 5.6 %convolution_convert_fusion.4 = bf16[192,2304]{1,0:T(8,128)(2,1)} fusion(bf16[1,720,2304]{2,1,0:T(8,128)(2,1)S(1)} %copy-done, f32[192,720]{1,0:T(8,128)} %fusion.31, bf16[192,2304]{1,0:T(8,128)(2,1)} %copy-done.14, bf16[1,2,2304,720]{2,3,1,0:T(8,128)(2,1)} %param.26), kind=kOutput, calls=%fused_computation.5 | convolution fusion | flops 1275291648 | bytes 8994816 | tf_op jit(solution)/shard_map/dot_general | solution.py:310
  225.8 2.5 add_convert_fusion.9
  228.3 1.4 collective-permute-start.23
  233.4 3.9 %fusion.29 = f32[192,720]{1,0:T(8,128)} fusion(bf16[192,2304]{1,0:T(8,128)(2,1)S(1)} %constant_dynamic-update-slice_fusion.12, bf16[1,2,2304,720]{2,3,1,0:T(8,128)(2,1)} %param.26), kind=kOutput, calls=%fused_computation.40 | convolution fusion | flops 637009920 | bytes 4755456 | tf_op jit(solution)/shard_map/dot_general | solution.py:307
  237.2 5.6 %convolution_convert_fusion.3 = bf16[192,2304]{1,0:T(8,128)(2,1)} fusion(bf16[1,720,2304]{2,1,0:T(8,128)(2,1)S(1)} %copy-done, f32[192,720]{1,0:T(8,128)} %fusion.29, bf16[192,2304]{1,0:T(8,128)(2,1)} %copy-done.8, bf16[1,2,2304,720]{2,3,1,0:T(8,128)(2,1)} %param.26), kind=kOutput, calls=%fused_computation.4 | convolution fusion | flops 1275291648 | bytes 8994816 | tf_op jit(solution)/shard_map/dot_general | solution.py:310
  242.8 2.6 add_convert_fusion.8
  245.4 1.4 collective-permute-start.26
  247.4 5.6 %convolution_convert_fusion.2 = bf16[192,2304]{1,0:T(8,128)(2,1)} fusion(bf16[1,720,2304]{2,1,0:T(8,128)(2,1)S(1)} %copy-done, f32[192,720]{1,0:T(8,128)} %fusion.27, bf16[1,2,2304,720]{2,3,1,0:T(8,128)(2,1)} %param.26, bf16[48,2304]{1,0:T(8,128)(2,1)} %copy-done.6, bf16[48,2304]{1,0:T(8,128)(2,1)} %copy-done.7, bf16[48,2304]{1,0:T(8,128)(2,1)} %copy-done.5, ...), kind=kOutput, calls=%fused_computation.3 | convolution fusion | flops 1278830592 | bytes 8994816 | tf_op jit(solution)/shard_map/dot_general | solution.py:310
  254.0 1.4 collective-permute-done.34
  255.4 1.6 add_convert_fusion.7
  257.1 3.4 %collective-permute-start.35 = (bf16[48,2304]{1,0:T(8,128)(2,1)S(1)}, bf16[48,2304]{1,0:T(8,128)(2,1)S(1)}, u32[]{:S(2)}, u32[]{:S(2)}) collective-permute-start(bf16[48,2304]{1,0:T(8,128)(2,1)S(1)} %get-tuple-element.38), channel_id=1, source_target_pairs={{0,2},{1,3},{2,0},{3,1},{4,6},{5,7},{6,4},{7,5},{8,10},{9,11},{10,... | collective-permute-start | bytes 663560 | tf_op jit(solution)/shard_map/ppermute | solution.py:297
  260.5 1.4 collective-permute-start.27
  262.9 3.7 %collective-permute-done.35 = bf16[48,2304]{1,0:T(8,128)(2,1)S(1)} collective-permute-done((bf16[48,2304]{1,0:T(8,128)(2,1)S(1)}, bf16[48,2304]{1,0:T(8,128)(2,1)S(1)}, u32[]{:S(2)}, u32[]{:S(2)}) %collective-permute-start.35) | collective-permute-done | bytes 221216 | tf_op jit(solution)/shard_map/ppermute | solution.py:297
  266.5 3.9 %collective-permute-done.27 = bf16[48,2304]{1,0:T(8,128)(2,1)S(1)} collective-permute-done((bf16[48,2304]{1,0:T(8,128)(2,1)S(1)}, bf16[48,2304]{1,0:T(8,128)(2,1)S(1)}, u32[]{:S(2)}, u32[]{:S(2)}) %collective-permute-start.27) | collective-permute-done | bytes 221216 | tf_op jit(solution)/shard_map/ppermute | solution.py:297
  270.4 1.4 fusion.44
  271.8 2.9 %reshape.326 = f32[64,2,2304]{2,1,0:T(2,128)} reshape(f32[128,2304]{1,0:T(8,128)} %fusion.44) | data formatting | bytes 2359296 | tf_op jit(solution)/shard_map/reshape | solution.py:320
  274.8 2.6 fusion.142
  277.4 2.0 fusion.56
  (133 shorter events, 45.0 us)
Async XLA Ops:
  0.6 111.8 %copy-start = (bf16[1,720,2304]{2,1,0:T(8,128)(2,1)S(1)}, bf16[1,720,2304]{2,1,0:T(8,128)(2,1)}, u32[]{:S(2)}) copy-start(bf16[1,720,2304]{2,1,0:T(8,128)(2,1)} %param.27) | copy-start | bytes 9953284
  0.6 53.5 %collective-permute-start = (bf16[128,4608]{1,0:T(8,128)(2,1)}, bf16[128,4608]{1,0:T(8,128)(2,1)}, u32[]{:S(2)}, u32[]{:S(2)}) collective-permute-start(bf16[128,4608]{1,0:T(8,128)(2,1)} %bitcast.154), channel_id=1, source_target_pairs={{0,1},{1,0},{2,3},{3,2},{4,5},{5,4},{6,7},{7,6},{8,9},{9,8},{10,11... | collective-permute-start | bytes 3538952 | tf_op jit(solution)/shard_map/ppermute | solution.py:236
  1.2 29.5 %collective-permute-start.1 = (bf16[128,4608]{1,0:T(8,128)(2,1)}, bf16[128,4608]{1,0:T(8,128)(2,1)}, u32[]{:S(2)}, u32[]{:S(2)}) collective-permute-start(bf16[128,4608]{1,0:T(8,128)(2,1)} %bitcast.155), channel_id=1, source_target_pairs={{0,2},{1,3},{2,0},{3,1},{4,6},{5,7},{6,4},{7,5},{8,10},{9,11},{10,... | collective-permute-start | bytes 3538952 | tf_op jit(solution)/shard_map/ppermute | solution.py:236
  30.7 23.5 %collective-permute-start.2 = (bf16[128,4608]{1,0:T(8,128)(2,1)}, bf16[128,4608]{1,0:T(8,128)(2,1)}, u32[]{:S(2)}, u32[]{:S(2)}) collective-permute-start(bf16[128,4608]{1,0:T(8,128)(2,1)} %collective-permute-done.1.refs_4_.refs_5_), channel_id=1, source_target_pairs={{0,1},{1,0},{2,3},{3,2},{4,5},{5,4},{6,7},{7,6},{8,9},{9,8},{10,11... | collective-permute-start | bytes 3538952 | tf_op jit(solution)/shard_map/ppermute | solution.py:236
  71.1 8.1 %copy-start.15 = (f32[2304]{0:T(1024)S(1)}, f32[2304]{0:T(1024)}, u32[]{:S(2)}) copy-start(f32[2304]{0:T(1024)} %param.23) | copy-start | bytes 27652
  78.4 0.8 copy-start.1
  78.4 11.7 %copy-start.16 = (s32[64,2]{0,1:T(2,128)S(1)}, s32[64,2]{0,1:T(2,128)}, u32[]{:S(2)}) copy-start(s32[64,2]{0,1:T(2,128)} %param.25) | copy-start | bytes 1540
  79.3 0.7 copy-start.2
  85.4 6.0 %collective-permute-start.3 = (bf16[48,2304]{1,0:T(8,128)(2,1)S(1)}, bf16[48,2304]{1,0:T(8,128)(2,1)S(1)}, u32[]{:S(2)}, u32[]{:S(2)}) collective-permute-start(bf16[48,2304]{1,0:T(8,128)(2,1)S(1)} %get-tuple-element.34), channel_id=1, source_target_pairs={{0,1},{1,2},{2,3},{3,0},{4,5},{5,6},{6,7},{7,4},{8,9},{9,10},{10,1... | collective-permute-start | bytes 663560 | tf_op jit(solution)/shard_map/ppermute | solution.py:297
  85.9 7.2 %collective-permute-start.6 = (bf16[48,2304]{1,0:T(8,128)(2,1)S(1)}, bf16[48,2304]{1,0:T(8,128)(2,1)S(1)}, u32[]{:S(2)}, u32[]{:S(2)}) collective-permute-start(bf16[48,2304]{1,0:T(8,128)(2,1)S(1)} %get-tuple-element.33), channel_id=1, source_target_pairs={{0,3},{1,0},{2,1},{3,2},{4,7},{5,4},{6,5},{7,6},{8,11},{9,8},{10,9... | collective-permute-start | bytes 663560 | tf_op jit(solution)/shard_map/ppermute | solution.py:297
  87.3 10.7 %collective-permute-start.5 = (bf16[48,2304]{1,0:T(8,128)(2,1)S(1)}, bf16[48,2304]{1,0:T(8,128)(2,1)S(1)}, u32[]{:S(2)}, u32[]{:S(2)}) collective-permute-start(bf16[48,2304]{1,0:T(8,128)(2,1)S(1)} %get-tuple-element.32), channel_id=1, source_target_pairs={{0,2},{1,3},{2,0},{3,1},{4,6},{5,7},{6,4},{7,5},{8,10},{9,11},{10,... | collective-permute-start | bytes 663560 | tf_op jit(solution)/shard_map/ppermute | solution.py:297
  91.3 12.4 %copy-start.5 = (bf16[48,2304]{1,0:T(8,128)(2,1)}, bf16[48,2304]{1,0:T(8,128)(2,1)S(1)}, u32[]{:S(2)}) copy-start(bf16[48,2304]{1,0:T(8,128)(2,1)S(1)} %collective-permute-done.3) | copy-start | bytes 663556
  91.3 19.1 %slice-start = ((s8[6635520]{0:T(1024)(128)(4,1)}), s8[4194304]{0:T(1024)(128)(4,1)S(1)}, s32[]{:S(2)}) async-start(s8[6635520]{0:T(1024)(128)(4,1)} %bitcast.160), calls=%async_computation | async-start | bytes 8388608
  91.4 12.6 %collective-permute-start.4 = (bf16[96,2304]{1,0:T(8,128)(2,1)S(1)}, bf16[96,2304]{1,0:T(8,128)(2,1)S(1)}, u32[]{:S(2)}, u32[]{:S(2)}) collective-permute-start(bf16[96,2304]{1,0:T(8,128)(2,1)S(1)} %pad_maximum_fusion.1), channel_id=1, source_target_pairs={{0,4},{4,12},{12,20},{20,28},{28,24},{24,16},{16,8},{8,0},{1,5},{5... | collective-permute-start | bytes 1327112 | tf_op jit(solution)/shard_map/ppermute | solution.py:180
  93.2 10.6 %copy-start.6 = (bf16[48,2304]{1,0:T(8,128)(2,1)}, bf16[48,2304]{1,0:T(8,128)(2,1)S(1)}, u32[]{:S(2)}) copy-start(bf16[48,2304]{1,0:T(8,128)(2,1)S(1)} %collective-permute-done.6) | copy-start | bytes 663556
  98.0 5.7 %copy-start.7 = (bf16[48,2304]{1,0:T(8,128)(2,1)}, bf16[48,2304]{1,0:T(8,128)(2,1)S(1)}, u32[]{:S(2)}) copy-start(bf16[48,2304]{1,0:T(8,128)(2,1)S(1)} %collective-permute-done.5) | copy-start | bytes 663556
  98.0 12.4 %slice-start.1 = ((s8[6635520]{0:T(1024)(128)(4,1)}), s8[2441216]{0:T(1024)(128)(4,1)S(1)}, s32[]{:S(2)}) async-start(s8[6635520]{0:T(1024)(128)(4,1)} %bitcast.160), calls=%async_computation.1 | async-start | bytes 4882432
  98.1 10.6 %collective-permute-start.7 = (bf16[96,2304]{1,0:T(8,128)(2,1)S(1)}, bf16[96,2304]{1,0:T(8,128)(2,1)S(1)}, u32[]{:S(2)}, u32[]{:S(2)}) collective-permute-start(bf16[96,2304]{1,0:T(8,128)(2,1)S(1)} %pad_maximum_fusion.2), channel_id=1, source_target_pairs={{0,8},{4,0},{12,4},{20,12},{28,20},{24,28},{16,24},{8,16},{1,9},{5... | collective-permute-start | bytes 1327112 | tf_op jit(solution)/shard_map/ppermute | solution.py:180
  103.9 0.8 copy-start.3
  108.7 0.8 copy-start.4
  109.5 0.9 copy-start.9
  118.0 13.4 %collective-permute-start.9 = (bf16[96,2304]{1,0:T(8,128)(2,1)}, bf16[96,2304]{1,0:T(8,128)(2,1)}, u32[]{:S(2)}, u32[]{:S(2)}) collective-permute-start(bf16[96,2304]{1,0:T(8,128)(2,1)} %copy-done.3), channel_id=1, source_target_pairs={{0,4},{4,12},{12,20},{20,28},{28,24},{24,16},{16,8},{8,0},{1,5},{5... | collective-permute-start | bytes 1327112 | tf_op jit(solution)/shard_map/ppermute | solution.py:180
  119.4 13.4 %collective-permute-start.10 = (bf16[96,2304]{1,0:T(8,128)(2,1)}, bf16[96,2304]{1,0:T(8,128)(2,1)}, u32[]{:S(2)}, u32[]{:S(2)}) collective-permute-start(bf16[96,2304]{1,0:T(8,128)(2,1)} %copy-done.4), channel_id=1, source_target_pairs={{0,8},{4,0},{12,4},{20,12},{28,20},{24,28},{16,24},{8,16},{1,9},{5... | collective-permute-start | bytes 1327112 | tf_op jit(solution)/shard_map/ppermute | solution.py:180
  122.2 24.1 %collective-permute-start.8 = (bf16[96,2304]{1,0:T(8,128)(2,1)}, bf16[96,2304]{1,0:T(8,128)(2,1)}, u32[]{:S(2)}, u32[]{:S(2)}) collective-permute-start(bf16[96,2304]{1,0:T(8,128)(2,1)} %get-tuple-element.30), channel_id=1, source_target_pairs={{0,4},{4,12},{12,20},{20,28},{28,24},{24,16},{16,8},{8,0},{1,5},{5... | collective-permute-start | bytes 1327112 | tf_op jit(solution)/shard_map/ppermute | solution.py:190
  123.6 22.7 %collective-permute-start.28 = (bf16[96,2304]{1,0:T(8,128)(2,1)}, bf16[96,2304]{1,0:T(8,128)(2,1)}, u32[]{:S(2)}, u32[]{:S(2)}) collective-permute-start(bf16[96,2304]{1,0:T(8,128)(2,1)} %get-tuple-element.31), channel_id=1, source_target_pairs={{0,8},{4,0},{12,4},{20,12},{28,20},{24,28},{16,24},{8,16},{1,9},{5... | collective-permute-start | bytes 1327112 | tf_op jit(solution)/shard_map/ppermute | solution.py:190
  133.8 0.9 copy-start.10
  138.7 12.2 %collective-permute-start.12 = (bf16[96,2304]{1,0:T(8,128)(2,1)}, bf16[96,2304]{1,0:T(8,128)(2,1)}, u32[]{:S(2)}, u32[]{:S(2)}) collective-permute-start(bf16[96,2304]{1,0:T(8,128)(2,1)} %collective-permute-done.9), channel_id=1, source_target_pairs={{0,4},{4,12},{12,20},{20,28},{28,24},{24,16},{16,8},{8,0},{1,5},{5... | collective-permute-start | bytes 1327112 | tf_op jit(solution)/shard_map/ppermute | solution.py:180
  140.3 12.4 %collective-permute-start.13 = (bf16[96,2304]{1,0:T(8,128)(2,1)}, bf16[96,2304]{1,0:T(8,128)(2,1)}, u32[]{:S(2)}, u32[]{:S(2)}) collective-permute-start(bf16[96,2304]{1,0:T(8,128)(2,1)} %collective-permute-done.10), channel_id=1, source_target_pairs={{0,8},{4,0},{12,4},{20,12},{28,20},{24,28},{16,24},{8,16},{1,9},{5... | collective-permute-start | bytes 1327112 | tf_op jit(solution)/shard_map/ppermute | solution.py:180
  148.9 17.3 %collective-permute-start.11 = (bf16[96,2304]{1,0:T(8,128)(2,1)}, bf16[96,2304]{1,0:T(8,128)(2,1)}, u32[]{:S(2)}, u32[]{:S(2)}) collective-permute-start(bf16[96,2304]{1,0:T(8,128)(2,1)} %get-tuple-element.28), channel_id=1, source_target_pairs={{0,4},{4,12},{12,20},{20,28},{28,24},{24,16},{16,8},{8,0},{1,5},{5... | collective-permute-start | bytes 1327112 | tf_op jit(solution)/shard_map/ppermute | solution.py:190
  150.4 15.7 %collective-permute-start.29 = (bf16[96,2304]{1,0:T(8,128)(2,1)}, bf16[96,2304]{1,0:T(8,128)(2,1)}, u32[]{:S(2)}, u32[]{:S(2)}) collective-permute-start(bf16[96,2304]{1,0:T(8,128)(2,1)} %get-tuple-element.29), channel_id=1, source_target_pairs={{0,8},{4,0},{12,4},{20,12},{28,20},{24,28},{16,24},{8,16},{1,9},{5... | collective-permute-start | bytes 1327112 | tf_op jit(solution)/shard_map/ppermute | solution.py:190
  153.7 0.9 copy-start.11
  158.5 13.3 %collective-permute-start.15 = (bf16[96,2304]{1,0:T(8,128)(2,1)}, bf16[96,2304]{1,0:T(8,128)(2,1)}, u32[]{:S(2)}, u32[]{:S(2)}) collective-permute-start(bf16[96,2304]{1,0:T(8,128)(2,1)} %collective-permute-done.12), channel_id=1, source_target_pairs={{0,4},{4,12},{12,20},{20,28},{28,24},{24,16},{16,8},{8,0},{1,5},{5... | collective-permute-start | bytes 1327112 | tf_op jit(solution)/shard_map/ppermute | solution.py:180
  160.0 12.8 %collective-permute-start.16 = (bf16[96,2304]{1,0:T(8,128)(2,1)}, bf16[96,2304]{1,0:T(8,128)(2,1)}, u32[]{:S(2)}, u32[]{:S(2)}) collective-permute-start(bf16[96,2304]{1,0:T(8,128)(2,1)} %collective-permute-done.13), channel_id=1, source_target_pairs={{0,8},{4,0},{12,4},{20,12},{28,20},{24,28},{16,24},{8,16},{1,9},{5... | collective-permute-start | bytes 1327112 | tf_op jit(solution)/shard_map/ppermute | solution.py:180
  168.7 17.7 %collective-permute-start.14 = (bf16[96,2304]{1,0:T(8,128)(2,1)}, bf16[96,2304]{1,0:T(8,128)(2,1)}, u32[]{:S(2)}, u32[]{:S(2)}) collective-permute-start(bf16[96,2304]{1,0:T(8,128)(2,1)} %get-tuple-element.26), channel_id=1, source_target_pairs={{0,4},{4,12},{12,20},{20,28},{28,24},{24,16},{16,8},{8,0},{1,5},{5... | collective-permute-start | bytes 1327112 | tf_op jit(solution)/shard_map/ppermute | solution.py:190
  170.1 16.2 %collective-permute-start.30 = (bf16[96,2304]{1,0:T(8,128)(2,1)}, bf16[96,2304]{1,0:T(8,128)(2,1)}, u32[]{:S(2)}, u32[]{:S(2)}) collective-permute-start(bf16[96,2304]{1,0:T(8,128)(2,1)} %get-tuple-element.27), channel_id=1, source_target_pairs={{0,8},{4,0},{12,4},{20,12},{28,20},{24,28},{16,24},{8,16},{1,9},{5... | collective-permute-start | bytes 1327112 | tf_op jit(solution)/shard_map/ppermute | solution.py:190
  173.9 0.9 copy-start.12
  178.7 12.6 %collective-permute-start.18 = (bf16[96,2304]{1,0:T(8,128)(2,1)}, bf16[96,2304]{1,0:T(8,128)(2,1)}, u32[]{:S(2)}, u32[]{:S(2)}) collective-permute-start(bf16[96,2304]{1,0:T(8,128)(2,1)} %collective-permute-done.15), channel_id=1, source_target_pairs={{0,4},{4,12},{12,20},{20,28},{28,24},{24,16},{16,8},{8,0},{1,5},{5... | collective-permute-start | bytes 1327112 | tf_op jit(solution)/shard_map/ppermute | solution.py:180
  180.1 12.2 %collective-permute-start.19 = (bf16[96,2304]{1,0:T(8,128)(2,1)}, bf16[96,2304]{1,0:T(8,128)(2,1)}, u32[]{:S(2)}, u32[]{:S(2)}) collective-permute-start(bf16[96,2304]{1,0:T(8,128)(2,1)} %collective-permute-done.16), channel_id=1, source_target_pairs={{0,8},{4,0},{12,4},{20,12},{28,20},{24,28},{16,24},{8,16},{1,9},{5... | collective-permute-start | bytes 1327112 | tf_op jit(solution)/shard_map/ppermute | solution.py:180
  188.9 17.0 %collective-permute-start.17 = (bf16[96,2304]{1,0:T(8,128)(2,1)}, bf16[96,2304]{1,0:T(8,128)(2,1)}, u32[]{:S(2)}, u32[]{:S(2)}) collective-permute-start(bf16[96,2304]{1,0:T(8,128)(2,1)} %get-tuple-element.24), channel_id=1, source_target_pairs={{0,4},{4,12},{12,20},{20,28},{28,24},{24,16},{16,8},{8,0},{1,5},{5... | collective-permute-start | bytes 1327112 | tf_op jit(solution)/shard_map/ppermute | solution.py:190
  190.3 15.6 %collective-permute-start.31 = (bf16[96,2304]{1,0:T(8,128)(2,1)}, bf16[96,2304]{1,0:T(8,128)(2,1)}, u32[]{:S(2)}, u32[]{:S(2)}) collective-permute-start(bf16[96,2304]{1,0:T(8,128)(2,1)} %get-tuple-element.25), channel_id=1, source_target_pairs={{0,8},{4,0},{12,4},{20,12},{28,20},{24,28},{16,24},{8,16},{1,9},{5... | collective-permute-start | bytes 1327112 | tf_op jit(solution)/shard_map/ppermute | solution.py:190
  193.4 0.9 copy-start.13
  198.2 13.0 %collective-permute-start.21 = (bf16[96,2304]{1,0:T(8,128)(2,1)}, bf16[96,2304]{1,0:T(8,128)(2,1)}, u32[]{:S(2)}, u32[]{:S(2)}) collective-permute-start(bf16[96,2304]{1,0:T(8,128)(2,1)} %collective-permute-done.18), channel_id=1, source_target_pairs={{0,4},{4,12},{12,20},{20,28},{28,24},{24,16},{16,8},{8,0},{1,5},{5... | collective-permute-start | bytes 1327112 | tf_op jit(solution)/shard_map/ppermute | solution.py:180
  199.4 12.8 %collective-permute-start.22 = (bf16[96,2304]{1,0:T(8,128)(2,1)}, bf16[96,2304]{1,0:T(8,128)(2,1)}, u32[]{:S(2)}, u32[]{:S(2)}) collective-permute-start(bf16[96,2304]{1,0:T(8,128)(2,1)} %collective-permute-done.19), channel_id=1, source_target_pairs={{0,8},{4,0},{12,4},{20,12},{28,20},{24,28},{16,24},{8,16},{1,9},{5... | collective-permute-start | bytes 1327112 | tf_op jit(solution)/shard_map/ppermute | solution.py:180
  208.4 17.3 %collective-permute-start.20 = (bf16[96,2304]{1,0:T(8,128)(2,1)}, bf16[96,2304]{1,0:T(8,128)(2,1)}, u32[]{:S(2)}, u32[]{:S(2)}) collective-permute-start(bf16[96,2304]{1,0:T(8,128)(2,1)} %get-tuple-element.22), channel_id=1, source_target_pairs={{0,4},{4,12},{12,20},{20,28},{28,24},{24,16},{16,8},{8,0},{1,5},{5... | collective-permute-start | bytes 1327112 | tf_op jit(solution)/shard_map/ppermute | solution.py:190
  209.6 16.1 %collective-permute-start.32 = (bf16[96,2304]{1,0:T(8,128)(2,1)}, bf16[96,2304]{1,0:T(8,128)(2,1)}, u32[]{:S(2)}, u32[]{:S(2)}) collective-permute-start(bf16[96,2304]{1,0:T(8,128)(2,1)} %get-tuple-element.23), channel_id=1, source_target_pairs={{0,8},{4,0},{12,4},{20,12},{28,20},{24,28},{16,24},{8,16},{1,9},{5... | collective-permute-start | bytes 1327112 | tf_op jit(solution)/shard_map/ppermute | solution.py:190
  213.3 0.9 copy-start.14
  218.1 12.2 %collective-permute-start.24 = (bf16[96,2304]{1,0:T(8,128)(2,1)}, bf16[96,2304]{1,0:T(8,128)(2,1)}, u32[]{:S(2)}, u32[]{:S(2)}) collective-permute-start(bf16[96,2304]{1,0:T(8,128)(2,1)} %collective-permute-done.21), channel_id=1, source_target_pairs={{0,4},{4,12},{12,20},{20,28},{28,24},{24,16},{16,8},{8,0},{1,5},{5... | collective-permute-start | bytes 1327112 | tf_op jit(solution)/shard_map/ppermute | solution.py:180
  219.5 11.9 %collective-permute-start.25 = (bf16[96,2304]{1,0:T(8,128)(2,1)}, bf16[96,2304]{1,0:T(8,128)(2,1)}, u32[]{:S(2)}, u32[]{:S(2)}) collective-permute-start(bf16[96,2304]{1,0:T(8,128)(2,1)} %collective-permute-done.22), channel_id=1, source_target_pairs={{0,8},{4,0},{12,4},{20,12},{28,20},{24,28},{16,24},{8,16},{1,9},{5... | collective-permute-start | bytes 1327112 | tf_op jit(solution)/shard_map/ppermute | solution.py:180
  228.3 14.5 %collective-permute-start.23 = (bf16[96,2304]{1,0:T(8,128)(2,1)}, bf16[96,2304]{1,0:T(8,128)(2,1)}, u32[]{:S(2)}, u32[]{:S(2)}) collective-permute-start(bf16[96,2304]{1,0:T(8,128)(2,1)} %get-tuple-element.20), channel_id=1, source_target_pairs={{0,4},{4,12},{12,20},{20,28},{28,24},{24,16},{16,8},{8,0},{1,5},{5... | collective-permute-start | bytes 1327112 | tf_op jit(solution)/shard_map/ppermute | solution.py:190
  229.7 13.2 %collective-permute-start.33 = (bf16[96,2304]{1,0:T(8,128)(2,1)}, bf16[96,2304]{1,0:T(8,128)(2,1)}, u32[]{:S(2)}, u32[]{:S(2)}) collective-permute-start(bf16[96,2304]{1,0:T(8,128)(2,1)} %get-tuple-element.21), channel_id=1, source_target_pairs={{0,8},{4,0},{12,4},{20,12},{28,20},{24,28},{16,24},{8,16},{1,9},{5... | collective-permute-start | bytes 1327112 | tf_op jit(solution)/shard_map/ppermute | solution.py:190
  232.4 0.9 copy-start.8
  245.4 8.6 %collective-permute-start.26 = (bf16[96,2304]{1,0:T(8,128)(2,1)}, bf16[96,2304]{1,0:T(8,128)(2,1)}, u32[]{:S(2)}, u32[]{:S(2)}) collective-permute-start(bf16[96,2304]{1,0:T(8,128)(2,1)} %get-tuple-element.18), channel_id=1, source_target_pairs={{0,4},{4,12},{12,20},{20,28},{28,24},{24,16},{16,8},{8,0},{1,5},{5... | collective-permute-start | bytes 1327112 | tf_op jit(solution)/shard_map/ppermute | solution.py:192
  246.8 8.6 %collective-permute-start.34 = (bf16[96,2304]{1,0:T(8,128)(2,1)}, bf16[96,2304]{1,0:T(8,128)(2,1)}, u32[]{:S(2)}, u32[]{:S(2)}) collective-permute-start(bf16[96,2304]{1,0:T(8,128)(2,1)} %get-tuple-element.19), channel_id=1, source_target_pairs={{0,8},{4,0},{12,4},{20,12},{28,20},{24,28},{16,24},{8,16},{1,9},{5... | collective-permute-start | bytes 1327112 | tf_op jit(solution)/shard_map/ppermute | solution.py:192
  257.1 5.8 %collective-permute-start.36 = (bf16[48,2304]{1,0:T(8,128)(2,1)S(1)}, bf16[48,2304]{1,0:T(8,128)(2,1)S(1)}, u32[]{:S(2)}, u32[]{:S(2)}) collective-permute-start(bf16[48,2304]{1,0:T(8,128)(2,1)S(1)} %get-tuple-element.39), channel_id=1, source_target_pairs={{0,1},{1,2},{2,3},{3,0},{4,5},{5,6},{6,7},{7,4},{8,9},{9,10},{10,1... | collective-permute-start | bytes 663560 | tf_op jit(solution)/shard_map/ppermute | solution.py:297
  257.1 9.4 %collective-permute-start.35 = (bf16[48,2304]{1,0:T(8,128)(2,1)S(1)}, bf16[48,2304]{1,0:T(8,128)(2,1)S(1)}, u32[]{:S(2)}, u32[]{:S(2)}) collective-permute-start(bf16[48,2304]{1,0:T(8,128)(2,1)S(1)} %get-tuple-element.38), channel_id=1, source_target_pairs={{0,2},{1,3},{2,0},{3,1},{4,6},{5,7},{6,4},{7,5},{8,10},{9,11},{10,... | collective-permute-start | bytes 663560 | tf_op jit(solution)/shard_map/ppermute | solution.py:297
  260.5 9.9 %collective-permute-start.27 = (bf16[48,2304]{1,0:T(8,128)(2,1)S(1)}, bf16[48,2304]{1,0:T(8,128)(2,1)S(1)}, u32[]{:S(2)}, u32[]{:S(2)}) collective-permute-start(bf16[48,2304]{1,0:T(8,128)(2,1)S(1)} %get-tuple-element.37), channel_id=1, source_target_pairs={{0,3},{1,0},{2,1},{3,2},{4,7},{5,4},{6,5},{7,6},{8,11},{9,8},{10,9... | collective-permute-start | bytes 663560 | tf_op jit(solution)/shard_map/ppermute | solution.py:297
